TPU v7x, 1024 devices: a whole 4x8x16 slice. The times are simulated.
1024 devices in a mesh: ctx: 64 (over z, x), head: 16 (over y, core).
Axes of the slice: x: 4, y: 8, z: 16, core: 2. Of those that a mesh axis runs over, the one named last changes fastest.
Arguments:
- q_raw: bfloat16 [16384, 2048], P('ctx', 'head'), may hold values from -6 to 6
- k_raw: bfloat16 [16384, 2048], P('ctx', 'head'), may hold values from -6 to 6
- v_raw: bfloat16 [16384, 2048], P('ctx', 'head'), may hold values from -6 to 6
- conv_weight: float32 [3, 4, 2048], P(None, None, 'head'), may hold values from -3 to 3
- beta_logit: float32 [16, 16384], P('head', 'ctx'), may hold values from -10 to 3.5
- out_weight: bfloat16 [2048, 2048], P('head'), may hold values from -0.125 to 0.125
- out_grad: bfloat16 [16384, 2048], P('ctx', 'head'), may hold values from -6 to 6
Outputs:
- grad_q_raw: float32 [16384, 2048], P('ctx', 'head')
- grad_k_raw: float32 [16384, 2048], P('ctx', 'head')
- grad_v_raw: float32 [16384, 2048], P('ctx', 'head')
- grad_conv: float32 [3, 4, 2048], P(None, None, 'head')
- grad_beta: float32 [16, 16384], P('head', 'ctx')
All inputs are finite; a program needn't handle non-finite values.
Results may differ from a plain program's by a relative error of at most 0.00095.
Values may be sent and summed in bfloat16 or wider, within the bound.
No kernel may reach another device: no remote copies, remote signals or barrier semaphores. Data moves between devices by JAX's collectives and lax.ppermute only.
A program may use at most 64 MiB of HBM per device.

v0:
```python
import math

import jax
import jax.numpy as jnp
from jax import lax
from jax.sharding import PartitionSpec as P

FEATURE_DIM = 128
CONV = 4
BLOCK = 64


HIGHEST = lax.Precision.HIGHEST


def passed_along(block, axis, distance):
    devices = range(lax.axis_size(axis))
    route = [(i - distance, i) for i in devices if i - distance in devices]
    return lax.ppermute(block, axis, route)


def carried_in(part, axis, combine, identity, reverse):
    count = lax.axis_size(axis)
    place = lax.axis_index(axis)
    ahead = count - 1 - place if reverse else place
    gathered = jax.tree.map(lambda a: lax.all_gather(a, axis), part)
    state = jax.tree.map(lambda a, e: jnp.zeros_like(a) + jnp.asarray(e, a.dtype), part, identity)

    def one(turn, state):
        source = count - 1 - turn if reverse else turn
        return combine(
            state, jax.tree.map(lambda a: lax.dynamic_index_in_dim(a, source, 0, False), gathered)
        )

    return lax.fori_loop(0, ahead, one, state)


def conv_silu(extended, weights, row_count):
    summed = weights[0] * extended[0:row_count]
    for offset in range(1, CONV):
        summed = summed + weights[offset] * extended[offset : offset + row_count]
    return jax.nn.silu(summed)


def normed(entries):
    return entries * lax.rsqrt(jnp.sum(entries * entries, axis=-1, keepdims=True) + 1e-06)


def wy_factors(key_rows, value_rows, rates):
    weighted = key_rows * rates[:, None]
    strict = jnp.tril(jnp.dot(weighted, key_rows.T, precision=HIGHEST), -1)
    system = jnp.eye(strict.shape[0], dtype=strict.dtype) + strict
    w_keys = jax.scipy.linalg.solve_triangular(system, weighted, lower=True, unit_diagonal=True)
    w_values = jax.scipy.linalg.solve_triangular(
        system, value_rows * rates[:, None], lower=True, unit_diagonal=True
    )
    return (w_keys, w_values)


def block_step(state, block):
    query_rows, key_rows, value_rows, rates = block
    w_keys, w_values = wy_factors(key_rows, value_rows, rates)
    fresh = w_values - jnp.dot(w_keys, state, precision=HIGHEST)
    scores = jnp.tril(jnp.dot(query_rows, key_rows.T, precision=HIGHEST))
    output = jnp.dot(query_rows, state, precision=HIGHEST) + jnp.dot(
        scores, fresh, precision=HIGHEST
    )
    return (state + jnp.dot(key_rows.T, fresh, precision=HIGHEST), output)


def local_forward(ext_q, ext_k, ext_v, conv_three, logits, start_state):
    row_count = logits.shape[0]
    queries = normed(conv_silu(ext_q, conv_three[0], row_count))
    key_act = normed(conv_silu(ext_k, conv_three[1], row_count))
    value_act = conv_silu(ext_v, conv_three[2], row_count)
    rates = jax.nn.sigmoid(logits)
    blocks = row_count // BLOCK
    shaped = (
        queries.reshape(blocks, BLOCK, FEATURE_DIM),
        key_act.reshape(blocks, BLOCK, FEATURE_DIM),
        value_act.reshape(blocks, BLOCK, FEATURE_DIM),
        rates.reshape(blocks, BLOCK),
    )
    final, outputs = lax.scan(block_step, start_state, shaped)
    return (outputs.reshape(row_count, FEATURE_DIM), final)


def transition(ext_k, ext_v, conv_three, logits):
    row_count = logits.shape[0]
    key_act = normed(conv_silu(ext_k, conv_three[1], row_count))
    value_act = conv_silu(ext_v, conv_three[2], row_count)
    rates = jax.nn.sigmoid(logits)
    blocks = row_count // BLOCK
    shaped = (
        key_act.reshape(blocks, BLOCK, FEATURE_DIM),
        value_act.reshape(blocks, BLOCK, FEATURE_DIM),
        rates.reshape(blocks, BLOCK),
    )
    identity = jnp.eye(FEATURE_DIM, dtype=jnp.float32)

    def advance(carry, block):
        key_rows, value_rows, block_rates = block
        w_keys, w_values = wy_factors(key_rows, value_rows, block_rates)
        decay = identity - jnp.dot(key_rows.T, w_keys, precision=HIGHEST)
        written = jnp.dot(key_rows.T, w_values, precision=HIGHEST)
        return (
            (
                jnp.dot(decay, carry[0], precision=HIGHEST),
                jnp.dot(decay, carry[1], precision=HIGHEST) + written,
            ),
            None,
        )

    pairs, _ = lax.scan(
        advance, (identity, jnp.zeros((FEATURE_DIM, FEATURE_DIM), jnp.float32)), shaped
    )
    return pairs


def combine_pairs(earlier, later):
    product = jnp.matmul(later[0], earlier[0], precision=HIGHEST)
    offset_term = jnp.matmul(later[0], earlier[1], precision=HIGHEST) + later[1]
    return (product, offset_term)


def on_device(q_raw, k_raw, v_raw, conv_weight, beta_logit, out_weight, out_grad):
    row_count = q_raw.shape[0]
    col_count = q_raw.shape[1]
    head_count = col_count // FEATURE_DIM
    margin = CONV - 1
    tail = row_count - margin
    rim_rows = passed_along((q_raw[tail:], k_raw[tail:], v_raw[tail:]), "ctx", 1)

    def extend(rim_part, main_part):
        joined = jnp.concatenate([rim_part, main_part], 0).astype(jnp.float32)
        return joined.reshape(margin + row_count, head_count, FEATURE_DIM).transpose(1, 0, 2)

    ext_q = extend(rim_rows[0], q_raw)
    ext_k = extend(rim_rows[1], k_raw)
    ext_v = extend(rim_rows[2], v_raw)
    conv_heads = conv_weight.reshape(3, CONV, head_count, FEATURE_DIM).transpose(2, 0, 1, 3)
    out_cot = lax.dot_general(
        lax.all_gather(out_grad, "head", axis=1, tiled=True),
        out_weight,
        (((1,), (1,)), ((), ())),
        preferred_element_type=jnp.float32,
    )
    out_cot = out_cot.reshape(row_count, head_count, FEATURE_DIM).transpose(1, 0, 2)
    pairs = jax.vmap(transition)(ext_k, ext_v, conv_heads, beta_logit)
    identity = jnp.broadcast_to(
        jnp.eye(FEATURE_DIM, dtype=jnp.float32), (head_count, FEATURE_DIM, FEATURE_DIM)
    )
    zero_state = jnp.zeros((head_count, FEATURE_DIM, FEATURE_DIM), jnp.float32)
    carried = carried_in(pairs, "ctx", combine_pairs, (identity, zero_state), False)
    start_state = carried[1]
    batched = jax.vmap(local_forward)
    adjoint_map = jnp.swapaxes(pairs[0], 1, 2)
    _, backward = jax.vjp(batched, ext_q, ext_k, ext_v, conv_heads, beta_logit, start_state)
    local_seed = backward((out_cot, zero_state))[5]
    suffix = carried_in(
        (adjoint_map, local_seed), "ctx", combine_pairs, (identity, zero_state), True
    )
    grads = backward((out_cot, suffix[1]))
    rim_back = passed_along(
        (grads[0][:, :margin], grads[1][:, :margin], grads[2][:, :margin]), "ctx", -1
    )

    def finish(grad_ext, rim_part):
        main_part = grad_ext[:, margin:]
        main_part = jnp.concatenate([main_part[:, :tail], main_part[:, tail:] + rim_part], 1)
        return main_part.transpose(1, 0, 2).reshape(row_count, col_count)

    conv_local = grads[3].transpose(1, 2, 0, 3).reshape(3, CONV, col_count)
    scale = 1.0 / math.sqrt(row_count * lax.axis_size("ctx"))
    conv_total = lax.psum(conv_local, "ctx") * scale
    return (
        finish(grads[0], rim_back[0]),
        finish(grads[1], rim_back[1]),
        finish(grads[2], rim_back[2]),
        conv_total,
        grads[4],
    )


def solution(mesh):
    return jax.shard_map(
        on_device,
        mesh=mesh,
        in_specs=(
            P("ctx", "head"),
            P("ctx", "head"),
            P("ctx", "head"),
            P(None, None, "head"),
            P("head", "ctx"),
            P("head", None),
            P("ctx", "head"),
        ),
        out_specs=(
            P("ctx", "head"),
            P("ctx", "head"),
            P("ctx", "head"),
            P(None, None, "head"),
            P("head", "ctx"),
        ),
        check_vma=False,
    )
```

profile of v0, /device:TPU:6, one launch (start us, length us, event | category | flops | bytes accessed | tf_op | source)
XLA Modules:
  0.0 960.0 jit_solution(849954616179924073)
XLA Ops:
  8.0 4.2 collective-permute-start
  12.8 3.4 collective-permute-start.1
  17.7 1.9 fusion.210
  22.5 27.1 %while.117 = (s32[]{:T(128)}, f32[1,128,128]{2,1,0:T(8,128)S(1)}, f32[1,128,128]{2,1,0:T(8,128)S(1)}, f32[4,1,64,128]{3,2,1,0:T(8,128)S(1)}, f32[4,1,64]{2,1,0:T...) while((s32[]{:T(128)}, f32[1,128,128]{2,1,0:T(8,128)S(1)}, f32[1,128,128]{2,1,0:T(8,128)S(1)}, ...), condition=%wide.region_2.4_spmd.clone, body=%wide.region_1.3_spmd.clone.sunk | while | flops 94502976 | bytes 1134945 | solution.py:114
  22.8 4.9 custom-call.27
  29.6 4.9 custom-call.27
  36.4 4.9 custom-call.27
  43.2 4.9 custom-call.27
  51.1 3.4 collective-permute-start.2
  54.7 1.6 copy.35
  57.0 11.5 %all-gather.10.cloned.1.call-done = bf16[256,2048]{1,0:T(8,128)(2,1)} async-done(((bf16[256,128]{1,0:T(8,128)(2,1)}), bf16[256,2048]{1,0:T(8,128)(2,1)}) %all-gather.10.cloned.1.call-update) | async-done | bytes 1048592 | tf_op jit(solution)/shard_map/all_gather | solution.py:143
  68.5 1.7 fusion.211
  70.1 154.2 %all-gather.14.cloned.1.call-done = f32[64,128,128]{2,1,0:T(8,128)} async-done(((f32[1,128,128]{2,1,0:T(8,128)}), f32[64,128,128]{2,1,0:T(8,128)}) %all-gather.14.cloned.1.call-update) | async-done | bytes 4194320 | tf_op jit(solution)/shard_map/all_gather | solution.py:26
  224.3 151.2 %all-gather.16.cloned.1.call-done = f32[64,128,128]{2,1,0:T(8,128)} async-done(((f32[1,128,128]{2,1,0:T(8,128)}), f32[64,128,128]{2,1,0:T(8,128)}) %all-gather.16.cloned.1.call-update) | async-done | bytes 4194320 | tf_op jit(solution)/shard_map/all_gather | solution.py:26
  375.6 3.4 while.115
  379.0 32.0 %while.118 = (s32[]{:T(128)}, f32[1,128,128]{2,1,0:T(8,128)S(1)}, f32[4,1,64,1]{2,3,1,0:T(1,128)}, f32[4,1,128,64]{3,2,1,0:T(8,128)S(1)}, f32[4,1,64,128]{3,2,1,...) while((s32[]{:T(128)}, f32[1,128,128]{2,1,0:T(8,128)S(1)}, ...), condition=%wide.region_7.9_spmd.clone, body=%wide.region_6.8_spmd.clone.sunk | while | flops 50430016 | bytes 1693117 | solution.py:84
  380.1 4.9 custom-call.28
  388.2 4.9 custom-call.28
  396.2 4.9 custom-call.28
  404.2 4.9 custom-call.28
  411.1 4.6 while.120
  416.4 110.5 %all-gather.12.cloned.1.call-done = f32[64,128,128]{2,1,0:T(8,128)} async-done(((f32[1,128,128]{2,1,0:T(8,128)}), f32[64,128,128]{2,1,0:T(8,128)}) %all-gather.12.cloned.1.call-update) | async-done | bytes 4194320 | tf_op jit(solution)/shard_map/all_gather | solution.py:26
  527.0 151.6 %all-gather.18.cloned.1.call-done = f32[64,128,128]{2,1,0:T(8,128)} async-done(((f32[1,128,128]{2,1,0:T(8,128)}), f32[64,128,128]{2,1,0:T(8,128)}) %all-gather.18.cloned.1.call-update) | async-done | bytes 4194320 | tf_op jit(solution)/shard_map/all_gather | solution.py:26
  678.6 67.7 %while.116 = (s32[]{:T(128)}, f32[1,128,128]{2,1,0:T(8,128)S(1)}, s32[]{:T(128)}, f32[64,1,128,128]{3,2,1,0:T(8,128)}, f32[64,1,128,128]{3,2,1,0:T(8,128)}, /*index=5*/s32[]{:T(128)}, s32[]{:T(128)}, s32[]{:T(128)}, s32[]{:T(128)}) while((s32[]{:T(128)}, f32[1,128,128]{2,1,0:T(8,128)S(1)}, s32[]{:T(128)}, f32[64,1,128,128]{3,2,1,0:T(8,128)}, ...), condition=%wide.region_11.13_spmd, body=%wide.region_10.12_spmd.sunk | while | flops 25182212 | bytes 394379 | solution.py:35
  678.6 1.1 fusion.324
  679.7 1.1 fusion.324
  680.9 1.1 fusion.324
  682.0 1.1 fusion.324
  683.1 1.1 fusion.324
  684.3 1.1 fusion.324
  685.4 1.1 fusion.324
  686.5 1.1 fusion.324
  687.6 1.1 fusion.324
  688.8 1.1 fusion.324
  689.9 1.1 fusion.324
  691.0 1.1 fusion.324
  693.3 1.1 fusion.324
  694.4 1.1 fusion.324
  695.5 1.1 fusion.324
  696.7 1.1 fusion.324
  697.8 1.1 fusion.324
  698.9 1.1 fusion.324
  700.1 1.1 fusion.324
  701.2 1.1 fusion.324
  702.3 1.1 fusion.324
  703.4 1.1 fusion.324
  704.6 1.1 fusion.324
  705.7 1.1 fusion.324
  706.8 1.1 fusion.324
  708.0 1.1 fusion.324
  709.1 1.1 fusion.324
  710.2 1.1 fusion.324
  711.3 1.1 fusion.324
  712.5 1.1 fusion.324
  746.5 43.2 %while.119 = (s32[]{:T(128)}, f32[1,128,128]{1,2,0:T(8,128)S(1)}, f32[4,1,64,128]{3,2,1,0:T(8,128)S(1)}, f32[4,1,64,128]{3,2,1,0:T(8,128)S(1)}, f32[4,1,64,128]{...) while((s32[]{:T(128)}, f32[1,128,128]{1,2,0:T(8,128)S(1)}, ...), condition=%wide.region_15.18_spmd.clone.clone, body=%wide.region_12.17_spmd.clone.clone.sunk | while | flops 144912384 | bytes 2420481 | solution.py:84
  748.3 4.9 custom-call.29
  759.1 4.9 custom-call.29
  769.9 4.9 custom-call.29
  780.7 4.9 custom-call.29
  793.0 142.3 %psum.7 = f32[3,4,128]{2,1,0:T(4,128)S(1)} all-reduce(f32[3,4,128]{2,1,0:T(4,128)S(1)} %add_bitcast_fusion), channel_id=1, replica_groups=mesh['ctx'=64,'head'=16] {'ctx'}, use_global_device_ids=true, to_apply=%region_30.33 | all-reduce | flops 1536 | bytes 12288 | tf_op jit(solution)/shard_map/psum | solution.py:175
  935.9 2.0 collective-permute-start.5
  937.9 7.2 collective-permute-start.4
  945.2 2.0 collective-permute-start.3
  950.0 2.7 collective-permute-done.3
  (439 shorter events, 98.9 us)
Async XLA Ops:
  7.2 61.3 %copy-start = (bf16[128,2048]{1,0:T(8,128)(2,1)S(1)}, bf16[128,2048]{1,0:T(8,128)(2,1)}, u32[]{:S(2)}) copy-start(bf16[128,2048]{1,0:T(8,128)(2,1)} %param.30) | copy-start | bytes 1572868
  7.2 61.3 %all-gather.10.cloned.1.call-start = ((), (), s32[]{:S(2)}) async-start(), calls=%async_computation | async-start | bytes 1114112 | tf_op jit(solution)/shard_map/all_gather | solution.py:143
  8.0 11.8 %collective-permute-start = (bf16[3,128]{1,0:T(4,128)(2,1)S(1)}, bf16[3,128]{1,0:T(4,128)(2,1)S(1)}, u32[]{:S(2)}, u32[]{:S(2)}) collective-permute-start(bf16[3,128]{1,0:T(4,128)(2,1)S(1)} %slice.158), channel_id=1, source_target_pairs={{0,16},{16,32},{32,48},{48,64},{64,80},{80,96},{96,112},{112,128},... | collective-permute-start | bytes 2312 | tf_op jit(solution)/shard_map/ppermute | solution.py:19
  12.8 8.1 collective-permute-start.1
  16.3 208.1 %all-gather.14.cloned.1.call-start = ((), (), s32[]{:S(2)}) async-start(), calls=%async_computation.2 | async-start | bytes 4259840 | tf_op jit(solution)/shard_map/all_gather | solution.py:26
  17.0 5.5 copy-start.4
  17.0 5.5 copy-start.6
  17.1 5.5 copy-start.7
  17.1 5.5 copy-start.8
  17.1 5.5 copy-start.5
  20.6 30.5 %copy-start.3 = (bf16[256,128]{1,0:T(8,128)(2,1)S(1)}, bf16[256,128]{1,0:T(8,128)(2,1)}, u32[]{:S(2)}) copy-start(bf16[256,128]{1,0:T(8,128)(2,1)} %param.25) | copy-start | bytes 196612
  49.7 0.6 copy-start.1
  49.7 0.7 copy-start.2
  50.3 325.2 %all-gather.16.cloned.1.call-start = ((), (), s32[]{:S(2)}) async-start(), calls=%async_computation.3 | async-start | bytes 4259840 | tf_op jit(solution)/shard_map/all_gather | solution.py:26
  51.1 475.9 %all-gather.12.cloned.1.call-start = ((), (), s32[]{:S(2)}) async-start(), calls=%async_computation.1 | async-start | bytes 4259840 | tf_op jit(solution)/shard_map/all_gather | solution.py:26
  51.1 5.5 collective-permute-start.2
  54.6 2.2 copy-start.11
  54.6 2.2 copy-start.13
  54.6 2.2 copy-start.15
  54.6 324.4 %copy-start.9 = (f32[128]{0:T(128)}, f32[128]{0:T(128)S(1)}, u32[]{:S(2)}) copy-start(f32[128]{0:T(128)S(1)} %get-tuple-element.1598) | copy-start | bytes 1540
  57.0 621.6 %all-gather.18.cloned.1.call-start = ((), (), s32[]{:S(2)}) async-start(), calls=%async_computation.4 | async-start | bytes 4259840 | tf_op jit(solution)/shard_map/all_gather | solution.py:26
  789.7 155.4 %copy-start.10 = (f32[128]{0:T(128)S(1)}, f32[128]{0:T(128)}, u32[]{:S(2)}) copy-start(f32[128]{0:T(128)} %copy-done.9) | copy-start | bytes 1540
  789.7 155.4 %copy-start.12 = (f32[128]{0:T(128)S(1)}, f32[128]{0:T(128)}, u32[]{:S(2)}) copy-start(f32[128]{0:T(128)} %copy-done.11) | copy-start | bytes 1540
  789.7 155.4 %copy-start.14 = (f32[128]{0:T(128)S(1)}, f32[128]{0:T(128)}, u32[]{:S(2)}) copy-start(f32[128]{0:T(128)} %copy-done.13) | copy-start | bytes 1540
  789.7 155.4 %copy-start.16 = (f32[128]{0:T(128)S(1)}, f32[128]{0:T(128)}, u32[]{:S(2)}) copy-start(f32[128]{0:T(128)} %copy-done.15) | copy-start | bytes 1540
  789.7 158.3 %copy-start.17 = (f32[1,256]{1,0:T(1,128)S(1)}, f32[1,256]{1,0:T(1,128)}, u32[]{:S(2)}) copy-start(f32[1,256]{1,0:T(1,128)} %get-tuple-element.1558) | copy-start | bytes 3076
  935.9 12.7 %collective-permute-start.5 = (f32[1,3,128]{2,1,0:T(4,128)S(1)}, f32[1,3,128]{2,1,0:T(4,128)S(1)}, u32[]{:S(2)}, u32[]{:S(2)}) collective-permute-start(f32[1,3,128]{2,1,0:T(4,128)S(1)} %pad_add_fusion.3), channel_id=1, source_target_pairs={{16,0},{32,16},{48,32},{64,48},{80,64},{96,80},{112,96},{128,112},... | collective-permute-start | bytes 4616 | tf_op jit(solution)/shard_map/ppermute | solution.py:19
  937.9 11.5 %collective-permute-start.4 = (f32[1,3,128]{2,1,0:T(4,128)S(1)}, f32[1,3,128]{2,1,0:T(4,128)S(1)}, u32[]{:S(2)}, u32[]{:S(2)}) collective-permute-start(f32[1,3,128]{2,1,0:T(4,128)S(1)} %pad_add_fusion.4), channel_id=1, source_target_pairs={{16,0},{32,16},{48,32},{64,48},{80,64},{96,80},{112,96},{128,112},... | collective-permute-start | bytes 4616 | tf_op jit(solution)/shard_map/ppermute | solution.py:19
  945.2 7.6 collective-permute-start.3
Sparse Core Ops, SparseCore 0:
  16.4 52.0 all-gather.9
  73.1 151.1 all-gather.13
  228.4 147.0 all-gather.15
  379.5 147.3 all-gather.11
  531.5 147.0 all-gather.17
where the time goes:
time: 964 us; the launch traced here: 960 us
  waiting for transfers between devices  583 us (60%)
  blocking collectives  142 us (15%)
  matrix products  106 us (11%)
  other arithmetic  75.2 us (8%)
  starting transfers between devices  22.3 us (2%)
  between operations  14.4 us (1%)
  local copies, waits for them, and re-layouts  12.5 us (1%)
    all_gather x4, waiting for transfers between devices, carried_in(): gathered = jax.tree.map(lambda a: lax.all_gather(a, axis), part)  568 us
    psum x1, blocking collectives, on_device(): conv_total = lax.psum(conv_local, 'ctx') * scale  142 us
    dot_general x63, matrix products, combine_pairs(): offset_term = jnp.matmul(later[0], earlier[1], precision=HIGHEST) + later[1]  68.1 us
    another operation x24, other arithmetic, wy_factors(): jax.scipy.linalg.solve_triangular(system, value_rows * rates[:, None], lo...  42.9 us
    ppermute x6, starting transfers between devices, passed_along(): return lax.ppermute(block, axis, route)  22.1 us
    another operation x8, other arithmetic, wy_factors(): jax.scipy.linalg.solve_triangular(system, weighted, lower=True, unit_diag...  19.6 us
  transfers between devices with their start and end apart: 11, of which 7 were waited for; matrix products, arithmetic and copies ran while one was open for 8% of the time, Pallas kernels for 0%

commit v1 on v0

--- a/solution.py
+++ b/solution.py
@@ -19,20 +19,23 @@
     return lax.ppermute(block, axis, route)
 
 
-def carried_in(part, axis, combine, identity, reverse):
+def carried_in(parts, axis, combine, identity, reverse):
     count = lax.axis_size(axis)
     place = lax.axis_index(axis)
-    ahead = count - 1 - place if reverse else place
-    gathered = jax.tree.map(lambda a: lax.all_gather(a, axis), part)
-    state = jax.tree.map(lambda a, e: jnp.zeros_like(a) + jnp.asarray(e, a.dtype), part, identity)
-
-    def one(turn, state):
-        source = count - 1 - turn if reverse else turn
-        return combine(
-            state, jax.tree.map(lambda a: lax.dynamic_index_in_dim(a, source, 0, False), gathered)
-        )
-
-    return lax.fori_loop(0, ahead, one, state)
+    ranks = [count - 1 - place if back else place for back in reverse]
+    fill = lambda a, e: jnp.zeros_like(a) + jnp.asarray(e, a.dtype)
+    totals = list(parts)
+    states = [jax.tree.map(fill, part, identity) for part in parts]
+    distance = 1
+    while distance < count:
+        for n, back in enumerate(reverse):
+            got = passed_along(totals[n], axis, -distance if back else distance)
+            keep = lambda new, old: jnp.where(ranks[n] >= distance, new, old)
+            states[n] = jax.tree.map(keep, combine(got, states[n]), states[n])
+            if 2 * distance < count:
+                totals[n] = jax.tree.map(keep, combine(got, totals[n]), totals[n])
+        distance *= 2
+    return states
 
 
 def conv_silu(extended, weights, row_count):
@@ -151,15 +154,19 @@
         jnp.eye(FEATURE_DIM, dtype=jnp.float32), (head_count, FEATURE_DIM, FEATURE_DIM)
     )
     zero_state = jnp.zeros((head_count, FEATURE_DIM, FEATURE_DIM), jnp.float32)
-    carried = carried_in(pairs, "ctx", combine_pairs, (identity, zero_state), False)
-    start_state = carried[1]
     batched = jax.vmap(local_forward)
     adjoint_map = jnp.swapaxes(pairs[0], 1, 2)
+    _, seed_backward = jax.vjp(batched, ext_q, ext_k, ext_v, conv_heads, beta_logit, zero_state)
+    local_seed = seed_backward((out_cot, zero_state))[5]
+    carried, suffix = carried_in(
+        [pairs, (adjoint_map, local_seed)],
+        "ctx",
+        combine_pairs,
+        (identity, zero_state),
+        [False, True],
+    )
+    start_state = carried[1]
     _, backward = jax.vjp(batched, ext_q, ext_k, ext_v, conv_heads, beta_logit, start_state)
-    local_seed = backward((out_cot, zero_state))[5]
-    suffix = carried_in(
-        (adjoint_map, local_seed), "ctx", combine_pairs, (identity, zero_state), True
-    )
     grads = backward((out_cot, suffix[1]))
     rim_back = passed_along(
         (grads[0][:, :margin], grads[1][:, :margin], grads[2][:, :margin]), "ctx", -1

time: 964 us -> 481 us (0.50)
  waiting for transfers between devices: 583 us -> 37.5 us
  starting transfers between devices: 22.3 us -> 116 us
  matrix products: 106 us -> 54.1 us
  local copies, waits for them, and re-layouts: 12.5 us -> 27.4 us
  other arithmetic: 75.2 us -> 88 us
    all_gather x4 -> x0, waiting for transfers between devices: 568 us -> none  [carried_in(): gathered = jax.tree.map(lambda a: lax.all_gather(a, axis), part)]
    ppermute x6 -> x28, starting transfers between devices: 22.1 us -> 115 us  [passed_along(): return lax.ppermute(block, axis, route)]
    dot_general x63 -> x22, matrix products: 68.1 us -> 6.24 us  [combine_pairs(): offset_term = jnp.matmul(later[0], earlier[1], precision=HIGHEST) + later[1]]
    ppermute x6 -> x28, waiting for transfers between devices: 3.11 us -> 37.4 us  [passed_along(): return lax.ppermute(block, axis, route)]
    another operation x8 -> x16, other arithmetic: 19.6 us -> 39.2 us  [wy_factors(): jax.scipy.linalg.solve_triangular(system, weighted, lower=True, unit_diag...]
    all_gather x1, waiting for transfers between devices: 11.5 us -> 0.02 us  [on_device(): lax.all_gather(out_grad, 'head', axis=1, tiled=True)]
  transfers between devices with their start and end apart: 11 -> 29, of which waited for: 7 -> 6; matrix products, arithmetic and copies ran while one was open for 8% -> 20% of each run, Pallas kernels for 0% -> 0%
where the time goes in v1:
time: 481 us; the launch traced here: 479 us
  blocking collectives  139 us (29%)
  starting transfers between devices  116 us (24%)
  other arithmetic  88 us (18%)
  matrix products  54.1 us (11%)
  waiting for transfers between devices  37.5 us (8%)
  local copies, waits for them, and re-layouts  27.4 us (6%)
  between operations  15.7 us (3%)
    psum x1, blocking collectives, on_device(): conv_total = lax.psum(conv_local, 'ctx') * scale  139 us
    ppermute x28, starting transfers between devices, passed_along(): return lax.ppermute(block, axis, route)  115 us
    another operation x24, other arithmetic, wy_factors(): jax.scipy.linalg.solve_triangular(system, value_rows * rates[:, None], lo...  39.8 us
    another operation x16, other arithmetic, wy_factors(): jax.scipy.linalg.solve_triangular(system, weighted, lower=True, unit_diag...  39.2 us
    ppermute x28, waiting for transfers between devices, passed_along(): return lax.ppermute(block, axis, route)  37.4 us
    while x36, local copies, waits for them, and re-layouts  9.78 us
  transfers between devices with their start and end apart: 29, of which 6 were waited for; matrix products, arithmetic and copies ran while one was open for 20% of the time, Pallas kernels for 0%

profile of v1, /device:TPU:6, one launch (start us, length us, event | category | flops | bytes accessed | tf_op | source)
XLA Modules:
  0.0 478.8 jit_solution(13206001652263738280)
XLA Ops:
  8.0 4.2 collective-permute-start
  12.8 3.4 collective-permute-start.1
  16.9 3.4 collective-permute-start.7
  21.9 1.2 fusion.338
  25.7 27.1 %while.106 = (s32[]{:T(128)}, f32[1,128,128]{2,1,0:T(8,128)S(1)}, f32[1,128,128]{2,1,0:T(8,128)S(1)}, f32[4,1,64,128]{3,2,1,0:T(8,128)S(1)}, f32[4,1,64]{2,1,0:T...) while((s32[]{:T(128)}, f32[1,128,128]{2,1,0:T(8,128)S(1)}, f32[1,128,128]{2,1,0:T(8,128)S(1)}, ...), condition=%wide.region_2.4_spmd.clone, body=%wide.region_1.3_spmd.clone.sunk | while | flops 94502976 | bytes 1134945 | solution.py:117
  26.0 4.9 %custom-call.27 = f32[1,1,64,64]{2,3,1,0:T(8,128)S(1)} custom-call(f32[1,1,64,64]{3,2,1,0:T(8,128)S(1)} %fusion.484), custom_call_target="InvertDiagBlocksLowerTriangular" | custom-call | tf_op jit(solution)/shard_map/vmap()/while/body/eval_jaxpr/jit(_solve_triangular)/triangular_solve/custom-call.1 | solution.py:56
  32.7 4.9 %custom-call.27 = f32[1,1,64,64]{2,3,1,0:T(8,128)S(1)} custom-call(f32[1,1,64,64]{3,2,1,0:T(8,128)S(1)} %fusion.484), custom_call_target="InvertDiagBlocksLowerTriangular" | custom-call | tf_op jit(solution)/shard_map/vmap()/while/body/eval_jaxpr/jit(_solve_triangular)/triangular_solve/custom-call.1 | solution.py:56
  39.5 4.9 %custom-call.27 = f32[1,1,64,64]{2,3,1,0:T(8,128)S(1)} custom-call(f32[1,1,64,64]{3,2,1,0:T(8,128)S(1)} %fusion.484), custom_call_target="InvertDiagBlocksLowerTriangular" | custom-call | tf_op jit(solution)/shard_map/vmap()/while/body/eval_jaxpr/jit(_solve_triangular)/triangular_solve/custom-call.1 | solution.py:56
  46.3 4.9 %custom-call.27 = f32[1,1,64,64]{2,3,1,0:T(8,128)S(1)} custom-call(f32[1,1,64,64]{3,2,1,0:T(8,128)S(1)} %fusion.484), custom_call_target="InvertDiagBlocksLowerTriangular" | custom-call | tf_op jit(solution)/shard_map/vmap()/while/body/eval_jaxpr/jit(_solve_triangular)/triangular_solve/custom-call.1 | solution.py:56
  52.8 3.2 collective-permute-start.14
  56.2 4.2 collective-permute-start.19
  61.4 1.9 collective-permute-start.2
  63.5 22.9 %while.107 = (s32[]{:T(128)}, f32[4,1,64,128]{3,2,1,0:T(8,128)S(1)}, f32[4,1,64,64]{3,2,1,0:T(8,128)S(1)}, f32[4,1,128,64]{3,2,1,0:T(8,128)S(1)}, f32[4,1,64,128...) while((s32[]{:T(128)}, f32[4,1,64,128]{3,2,1,0:T(8,128)S(1)}, ...), condition=%wide.region_5.7_spmd.clone, body=%wide.region_4.6_spmd.clone.sunk | while | flops 18939968 | bytes 547173 | solution.py:87
  63.8 4.9 %custom-call.28 = f32[1,1,64,64]{2,3,1,0:T(8,128)S(1)} custom-call(f32[1,1,64,64]{3,2,1,0:T(8,128)S(1)} %fusion.496), custom_call_target="InvertDiagBlocksLowerTriangular" | custom-call | tf_op jit(solution)/shard_map/jvp(vmap())/while/body/eval_jaxpr/jit(_solve_triangular)/triangular_solve/custom-call.1 | solution.py:56
  69.5 4.9 %custom-call.28 = f32[1,1,64,64]{2,3,1,0:T(8,128)S(1)} custom-call(f32[1,1,64,64]{3,2,1,0:T(8,128)S(1)} %fusion.496), custom_call_target="InvertDiagBlocksLowerTriangular" | custom-call | tf_op jit(solution)/shard_map/jvp(vmap())/while/body/eval_jaxpr/jit(_solve_triangular)/triangular_solve/custom-call.1 | solution.py:56
  75.3 4.9 %custom-call.28 = f32[1,1,64,64]{2,3,1,0:T(8,128)S(1)} custom-call(f32[1,1,64,64]{3,2,1,0:T(8,128)S(1)} %fusion.496), custom_call_target="InvertDiagBlocksLowerTriangular" | custom-call | tf_op jit(solution)/shard_map/jvp(vmap())/while/body/eval_jaxpr/jit(_solve_triangular)/triangular_solve/custom-call.1 | solution.py:56
  81.0 4.9 %custom-call.28 = f32[1,1,64,64]{2,3,1,0:T(8,128)S(1)} custom-call(f32[1,1,64,64]{3,2,1,0:T(8,128)S(1)} %fusion.496), custom_call_target="InvertDiagBlocksLowerTriangular" | custom-call | tf_op jit(solution)/shard_map/jvp(vmap())/while/body/eval_jaxpr/jit(_solve_triangular)/triangular_solve/custom-call.1 | solution.py:56
  86.6 4.8 %collective-permute-start.15 = (f32[1,128,128]{2,1,0:T(8,128)S(1)}, f32[1,128,128]{2,1,0:T(8,128)S(1)}, u32[]{:S(2)}, u32[]{:S(2)}) collective-permute-start(f32[1,128,128]{2,1,0:T(8,128)S(1)} %fusion.262), channel_id=1, source_target_pairs={{0,32},{16,48},{32,64},{48,80},{64,96},{80,112},{96,128},{112,144}... | collective-permute-start | bytes 196616 | tf_op jit(solution)/shard_map/ppermute | solution.py:19
  91.7 4.3 collective-permute-start.20
  96.2 3.0 collective-permute-start.3
  100.1 4.4 collective-permute-start.16
  104.7 5.4 %collective-permute-start.21 = (f32[1,128,128]{2,1,0:T(8,128)S(1)}, f32[1,128,128]{2,1,0:T(8,128)S(1)}, u32[]{:S(2)}, u32[]{:S(2)}) collective-permute-start(f32[1,128,128]{2,1,0:T(8,128)S(1)} %fusion.251), channel_id=1, source_target_pairs={{0,64},{16,80},{32,96},{48,112},{64,128},{80,144},{96,160},{112,17... | collective-permute-start | bytes 196616 | tf_op jit(solution)/shard_map/ppermute | solution.py:19
  110.3 1.3 collective-permute-start.4
  112.5 6.7 %collective-permute-start.17 = (f32[1,128,128]{2,1,0:T(8,128)S(1)}, f32[1,128,128]{2,1,0:T(8,128)S(1)}, u32[]{:S(2)}, u32[]{:S(2)}) collective-permute-start(f32[1,128,128]{2,1,0:T(8,128)S(1)} %fusion.264), channel_id=1, source_target_pairs={{0,128},{16,144},{32,160},{48,176},{64,192},{80,208},{96,224},{112... | collective-permute-start | bytes 196616 | tf_op jit(solution)/shard_map/ppermute | solution.py:19
  119.5 7.3 %collective-permute-start.22 = (f32[1,128,128]{2,1,0:T(8,128)S(1)}, f32[1,128,128]{2,1,0:T(8,128)S(1)}, u32[]{:S(2)}, u32[]{:S(2)}) collective-permute-start(f32[1,128,128]{2,1,0:T(8,128)S(1)} %fusion.253), channel_id=1, source_target_pairs={{0,128},{16,144},{32,160},{48,176},{64,192},{80,208},{96,224},{112... | collective-permute-start | bytes 196616 | tf_op jit(solution)/shard_map/ppermute | solution.py:19
  127.0 1.3 collective-permute-start.5
  129.2 9.1 %collective-permute-start.23 = (f32[1,128,128]{2,1,0:T(8,128)S(1)}, f32[1,128,128]{2,1,0:T(8,128)S(1)}, u32[]{:S(2)}, u32[]{:S(2)}) collective-permute-start(f32[1,128,128]{2,1,0:T(8,128)S(1)} %fusion.255), channel_id=1, source_target_pairs={{0,256},{16,272},{32,288},{48,304},{64,320},{80,336},{96,352},{112... | collective-permute-start | bytes 196616 | tf_op jit(solution)/shard_map/ppermute | solution.py:19
  138.5 6.1 %collective-permute-start.18 = (f32[1,128,128]{2,1,0:T(8,128)S(1)}, f32[1,128,128]{2,1,0:T(8,128)S(1)}, u32[]{:S(2)}, u32[]{:S(2)}) collective-permute-start(f32[1,128,128]{2,1,0:T(8,128)S(1)} %fusion.265), channel_id=1, source_target_pairs={{0,256},{16,272},{32,288},{48,304},{64,320},{80,336},{96,352},{112... | collective-permute-start | bytes 196616 | tf_op jit(solution)/shard_map/ppermute | solution.py:19
  144.9 1.3 collective-permute-start.6
  147.1 10.8 %collective-permute-start.24 = (f32[1,128,128]{2,1,0:T(8,128)S(1)}, f32[1,128,128]{2,1,0:T(8,128)S(1)}, u32[]{:S(2)}, u32[]{:S(2)}) collective-permute-start(f32[1,128,128]{2,1,0:T(8,128)S(1)} %fusion.257), channel_id=1, source_target_pairs={{0,512},{16,528},{32,544},{48,560},{64,576},{80,592},{96,608},{112... | collective-permute-start | bytes 196616 | tf_op jit(solution)/shard_map/ppermute | solution.py:19
  160.1 1.7 fusion.339
  161.7 4.6 while.110
  166.4 3.9 collective-permute-start.8
  171.1 41.0 %while.108 = (s32[]{:T(128)}, f32[1,128,128]{2,1,0:T(8,128)S(1)}, f32[4,1,64,1]{2,3,1,0:T(1,128)}, f32[4,1,128,64]{3,2,1,0:T(8,128)S(1)}, f32[4,1,64,128]{3,2,1,...) while((s32[]{:T(128)}, f32[1,128,128]{2,1,0:T(8,128)S(1)}, ...), condition=%wide.region_9.11_spmd.clone, body=%wide.region_8.10_spmd.clone.sunk | while | flops 50430016 | bytes 1722161 | solution.py:87
  172.6 4.9 %custom-call.29 = f32[1,1,64,64]{2,3,1,0:T(8,128)S(1)} custom-call(f32[1,1,64,64]{3,2,1,0:T(8,128)S(1)} %fusion.505), custom_call_target="InvertDiagBlocksLowerTriangular" | custom-call | tf_op jit(solution)/shard_map/jvp(vmap())/while/body/eval_jaxpr/jit(_solve_triangular)/triangular_solve/custom-call.1 | solution.py:57
  182.9 4.9 %custom-call.29 = f32[1,1,64,64]{2,3,1,0:T(8,128)S(1)} custom-call(f32[1,1,64,64]{3,2,1,0:T(8,128)S(1)} %fusion.505), custom_call_target="InvertDiagBlocksLowerTriangular" | custom-call | tf_op jit(solution)/shard_map/jvp(vmap())/while/body/eval_jaxpr/jit(_solve_triangular)/triangular_solve/custom-call.1 | solution.py:57
  193.1 4.9 %custom-call.29 = f32[1,1,64,64]{2,3,1,0:T(8,128)S(1)} custom-call(f32[1,1,64,64]{3,2,1,0:T(8,128)S(1)} %fusion.505), custom_call_target="InvertDiagBlocksLowerTriangular" | custom-call | tf_op jit(solution)/shard_map/jvp(vmap())/while/body/eval_jaxpr/jit(_solve_triangular)/triangular_solve/custom-call.1 | solution.py:57
  203.3 4.9 %custom-call.29 = f32[1,1,64,64]{2,3,1,0:T(8,128)S(1)} custom-call(f32[1,1,64,64]{3,2,1,0:T(8,128)S(1)} %fusion.505), custom_call_target="InvertDiagBlocksLowerTriangular" | custom-call | tf_op jit(solution)/shard_map/jvp(vmap())/while/body/eval_jaxpr/jit(_solve_triangular)/triangular_solve/custom-call.1 | solution.py:57
  212.9 1.1 fusion.239
  214.0 3.5 collective-permute-start.9
  217.5 1.1 convolution_select_fusion.16
  218.6 4.0 collective-permute-done.9
  222.8 1.4 collective-permute-start.10
  224.5 4.6 collective-permute-done.10
  229.3 1.6 collective-permute-start.11
  231.2 6.1 %collective-permute-done.11 = f32[1,128,128]{2,1,0:T(8,128)S(1)} collective-permute-done((f32[1,128,128]{2,1,0:T(8,128)S(1)}, f32[1,128,128]{2,1,0:T(8,128)S(1)}, u32[]{:S(2)}, u32[]{:S(2)}) %collective-permute-start.11) | collective-permute-done | bytes 65568 | tf_op jit(solution)/shard_map/ppermute | solution.py:19
  237.5 1.4 collective-permute-start.12
  239.2 8.5 %collective-permute-done.12 = f32[1,128,128]{2,1,0:T(8,128)S(1)} collective-permute-done((f32[1,128,128]{2,1,0:T(8,128)S(1)}, f32[1,128,128]{2,1,0:T(8,128)S(1)}, u32[]{:S(2)}, u32[]{:S(2)}) %collective-permute-start.12) | collective-permute-done | bytes 65568 | tf_op jit(solution)/shard_map/ppermute | solution.py:19
  247.9 1.4 collective-permute-start.13
  249.6 13.5 %collective-permute-done.13 = f32[1,128,128]{2,1,0:T(8,128)S(1)} collective-permute-done((f32[1,128,128]{2,1,0:T(8,128)S(1)}, f32[1,128,128]{2,1,0:T(8,128)S(1)}, u32[]{:S(2)}, u32[]{:S(2)}) %collective-permute-start.13) | collective-permute-done | bytes 65568 | tf_op jit(solution)/shard_map/ppermute | solution.py:19
  263.5 43.2 %while.109 = (s32[]{:T(128)}, f32[1,128,128]{1,2,0:T(8,128)S(1)}, f32[4,1,64,128]{3,2,1,0:T(8,128)S(1)}, f32[4,1,64,128]{3,2,1,0:T(8,128)S(1)}, f32[4,1,64,128]{...) while((s32[]{:T(128)}, f32[1,128,128]{1,2,0:T(8,128)S(1)}, ...), condition=%wide.region_13.16_spmd.clone.clone, body=%wide.region_10.15_spmd.clone.clone.sunk | while | flops 144912384 | bytes 2420481 | solution.py:87
  263.8 1.0 convolution_add_fusion.15
  265.3 4.9 %custom-call.30 = f32[1,1,64,64]{2,3,1,0:T(8,128)S(1)} custom-call(f32[1,1,64,64]{3,2,1,0:T(8,128)S(1)} %fusion.546), custom_call_target="InvertDiagBlocksLowerTriangular" | custom-call | tf_op jit(solution)/shard_map/transpose(jvp(vmap()))/while/body/eval_jaxpr/jit(_solve_triangular)/triangular_solve | solution.py:57
  274.6 1.0 convolution_add_fusion.15
  276.1 4.9 %custom-call.30 = f32[1,1,64,64]{2,3,1,0:T(8,128)S(1)} custom-call(f32[1,1,64,64]{3,2,1,0:T(8,128)S(1)} %fusion.546), custom_call_target="InvertDiagBlocksLowerTriangular" | custom-call | tf_op jit(solution)/shard_map/transpose(jvp(vmap()))/while/body/eval_jaxpr/jit(_solve_triangular)/triangular_solve | solution.py:57
  285.4 1.0 convolution_add_fusion.15
  286.9 4.9 %custom-call.30 = f32[1,1,64,64]{2,3,1,0:T(8,128)S(1)} custom-call(f32[1,1,64,64]{3,2,1,0:T(8,128)S(1)} %fusion.546), custom_call_target="InvertDiagBlocksLowerTriangular" | custom-call | tf_op jit(solution)/shard_map/transpose(jvp(vmap()))/while/body/eval_jaxpr/jit(_solve_triangular)/triangular_solve | solution.py:57
  296.1 1.0 convolution_add_fusion.15
  297.7 4.9 %custom-call.30 = f32[1,1,64,64]{2,3,1,0:T(8,128)S(1)} custom-call(f32[1,1,64,64]{3,2,1,0:T(8,128)S(1)} %fusion.546), custom_call_target="InvertDiagBlocksLowerTriangular" | custom-call | tf_op jit(solution)/shard_map/transpose(jvp(vmap()))/while/body/eval_jaxpr/jit(_solve_triangular)/triangular_solve | solution.py:57
  306.7 1.0 multiply_reduce_fusion.11
  312.3 138.9 %psum.7 = f32[3,4,128]{2,1,0:T(4,128)S(1)} all-reduce(f32[3,4,128]{2,1,0:T(4,128)S(1)} %add_bitcast_fusion), channel_id=1, replica_groups=mesh['ctx'=64,'head'=16] {'ctx'}, use_global_device_ids=true, to_apply=%region_28.31 | all-reduce | flops 1536 | bytes 12288 | tf_op jit(solution)/shard_map/psum | solution.py:182
  451.8 6.8 %collective-permute-start.27 = (f32[1,3,128]{2,1,0:T(4,128)S(1)}, f32[1,3,128]{2,1,0:T(4,128)S(1)}, u32[]{:S(2)}, u32[]{:S(2)}) collective-permute-start(f32[1,3,128]{2,1,0:T(4,128)S(1)} %pad_add_fusion.3), channel_id=1, source_target_pairs={{16,0},{32,16},{48,32},{64,48},{80,64},{96,80},{112,96},{128,112},... | collective-permute-start | bytes 4616 | tf_op jit(solution)/shard_map/ppermute | solution.py:19
  458.6 2.5 collective-permute-start.26
  461.2 6.7 %collective-permute-start.25 = (f32[1,3,128]{2,1,0:T(4,128)S(1)}, f32[1,3,128]{2,1,0:T(4,128)S(1)}, u32[]{:S(2)}, u32[]{:S(2)}) collective-permute-start(f32[1,3,128]{2,1,0:T(4,128)S(1)} %pad_add_fusion.5), channel_id=1, source_target_pairs={{16,0},{32,16},{48,32},{64,48},{80,64},{96,80},{112,96},{128,112},... | collective-permute-start | bytes 4616 | tf_op jit(solution)/shard_map/ppermute | solution.py:19
  (518 shorter events, 81.7 us)
Async XLA Ops:
  7.2 152.9 %copy-start = (bf16[128,2048]{1,0:T(8,128)(2,1)S(1)}, bf16[128,2048]{1,0:T(8,128)(2,1)}, u32[]{:S(2)}) copy-start(bf16[128,2048]{1,0:T(8,128)(2,1)} %param.28) | copy-start | bytes 1572868
  7.2 152.9 %all-gather.2.cloned.1.call-start = ((), (), s32[]{:S(2)}) async-start(), calls=%async_computation | async-start | bytes 1114112 | tf_op jit(solution)/shard_map/all_gather | solution.py:146
  8.0 15.3 %collective-permute-start = (bf16[3,128]{1,0:T(4,128)(2,1)S(1)}, bf16[3,128]{1,0:T(4,128)(2,1)S(1)}, u32[]{:S(2)}, u32[]{:S(2)}) collective-permute-start(bf16[3,128]{1,0:T(4,128)(2,1)S(1)} %slice.176), channel_id=1, source_target_pairs={{0,16},{16,32},{32,48},{48,64},{64,80},{80,96},{96,112},{112,128},... | collective-permute-start | bytes 2312 | tf_op jit(solution)/shard_map/ppermute | solution.py:19
  12.8 11.8 %collective-permute-start.1 = (bf16[3,128]{1,0:T(4,128)(2,1)S(1)}, bf16[3,128]{1,0:T(4,128)(2,1)S(1)}, u32[]{:S(2)}, u32[]{:S(2)}) collective-permute-start(bf16[3,128]{1,0:T(4,128)(2,1)S(1)} %slice.186), channel_id=1, source_target_pairs={{0,16},{16,32},{32,48},{48,64},{64,80},{80,96},{96,112},{112,128},... | collective-permute-start | bytes 2312 | tf_op jit(solution)/shard_map/ppermute | solution.py:19
  16.9 43.4 %collective-permute-start.7 = (bf16[3,128]{1,0:T(4,128)(2,1)S(1)}, bf16[3,128]{1,0:T(4,128)(2,1)S(1)}, u32[]{:S(2)}, u32[]{:S(2)}) collective-permute-start(bf16[3,128]{1,0:T(4,128)(2,1)S(1)} %slice.195), channel_id=1, source_target_pairs={{0,16},{16,32},{32,48},{48,64},{64,80},{80,96},{96,112},{112,128},... | collective-permute-start | bytes 2312 | tf_op jit(solution)/shard_map/ppermute | solution.py:19
  20.3 2.9 copy-start.20
  21.1 2.2 copy-start.40
  21.1 2.2 copy-start.42
  21.1 2.2 copy-start.44
  21.1 2.2 copy-start.46
  21.2 3.8 copy-start.48
  21.2 3.8 copy-start.50
  21.2 3.8 copy-start.52
  21.2 3.8 copy-start.54
  21.2 39.2 %copy-start.32 = (f32[128]{0:T(128)}, f32[128]{0:T(128)S(1)}, u32[]{:S(2)}) copy-start(f32[128]{0:T(128)S(1)} %get-tuple-element.1542) | copy-start | bytes 1540
  21.2 39.2 %copy-start.34 = (f32[128]{0:T(128)}, f32[128]{0:T(128)S(1)}, u32[]{:S(2)}) copy-start(f32[128]{0:T(128)S(1)} %get-tuple-element.1543) | copy-start | bytes 1540
  21.2 39.2 %copy-start.36 = (f32[128]{0:T(128)}, f32[128]{0:T(128)S(1)}, u32[]{:S(2)}) copy-start(f32[128]{0:T(128)S(1)} %get-tuple-element.1544) | copy-start | bytes 1540
  21.3 39.2 %copy-start.38 = (f32[128]{0:T(128)}, f32[128]{0:T(128)S(1)}, u32[]{:S(2)}) copy-start(f32[128]{0:T(128)S(1)} %get-tuple-element.1545) | copy-start | bytes 1540
  52.8 7.6 %copy-start.22 = (bf16[256,128]{1,0:T(8,128)(2,1)S(1)}, bf16[256,128]{1,0:T(8,128)(2,1)}, u32[]{:S(2)}) copy-start(bf16[256,128]{1,0:T(8,128)(2,1)} %param.23) | copy-start | bytes 196612
  52.8 33.6 %collective-permute-start.14 = (f32[1,128,128]{2,1,0:T(8,128)S(1)}, f32[1,128,128]{2,1,0:T(8,128)S(1)}, u32[]{:S(2)}, u32[]{:S(2)}) collective-permute-start(f32[1,128,128]{2,1,0:T(8,128)S(1)} %get-tuple-element.1099), channel_id=1, source_target_pairs={{0,16},{16,32},{32,48},{48,64},{64,80},{80,96},{96,112},{112,128},... | collective-permute-start | bytes 196616 | tf_op jit(solution)/shard_map/ppermute | solution.py:19
  56.1 39.9 %copy-start.11 = (f32[1,128,128]{1,2,0:T(8,128)}, f32[1,128,128]{1,2,0:T(8,128)S(1)}, u32[]{:S(2)}) copy-start(f32[1,128,128]{1,2,0:T(8,128)S(1)} %copy.15) | copy-start | bytes 196612
  56.2 35.3 %collective-permute-start.19 = (f32[1,128,128]{2,1,0:T(8,128)S(1)}, f32[1,128,128]{2,1,0:T(8,128)S(1)}, u32[]{:S(2)}, u32[]{:S(2)}) collective-permute-start(f32[1,128,128]{2,1,0:T(8,128)S(1)} %get-tuple-element.1104), channel_id=1, source_target_pairs={{0,16},{16,32},{32,48},{48,64},{64,80},{80,96},{96,112},{112,128},... | collective-permute-start | bytes 196616 | tf_op jit(solution)/shard_map/ppermute | solution.py:19
  61.2 2.1 copy-start.25
  61.4 34.7 %collective-permute-start.2 = (f32[1,128,128]{2,1,0:T(8,128)S(1)}, f32[1,128,128]{2,1,0:T(8,128)S(1)}, u32[]{:S(2)}, u32[]{:S(2)}) collective-permute-start(f32[1,128,128]{2,1,0:T(8,128)S(1)} %bitcast.1100), channel_id=1, source_target_pairs={{16,0},{32,16},{48,32},{64,48},{80,64},{96,80},{112,96},{128,112},... | collective-permute-start | bytes 196616 | tf_op jit(solution)/shard_map/ppermute | solution.py:19
  86.6 13.3 %collective-permute-start.15 = (f32[1,128,128]{2,1,0:T(8,128)S(1)}, f32[1,128,128]{2,1,0:T(8,128)S(1)}, u32[]{:S(2)}, u32[]{:S(2)}) collective-permute-start(f32[1,128,128]{2,1,0:T(8,128)S(1)} %fusion.262), channel_id=1, source_target_pairs={{0,32},{16,48},{32,64},{48,80},{64,96},{80,112},{96,128},{112,144}... | collective-permute-start | bytes 196616 | tf_op jit(solution)/shard_map/ppermute | solution.py:19
  91.7 12.8 %collective-permute-start.20 = (f32[1,128,128]{2,1,0:T(8,128)S(1)}, f32[1,128,128]{2,1,0:T(8,128)S(1)}, u32[]{:S(2)}, u32[]{:S(2)}) collective-permute-start(f32[1,128,128]{2,1,0:T(8,128)S(1)} %fusion.249), channel_id=1, source_target_pairs={{0,32},{16,48},{32,64},{48,80},{64,96},{80,112},{96,128},{112,144}... | collective-permute-start | bytes 196616 | tf_op jit(solution)/shard_map/ppermute | solution.py:19
  96.2 13.9 %collective-permute-start.3 = (f32[1,128,128]{2,1,0:T(8,128)S(1)}, f32[1,128,128]{2,1,0:T(8,128)S(1)}, u32[]{:S(2)}, u32[]{:S(2)}) collective-permute-start(f32[1,128,128]{2,1,0:T(8,128)S(1)} %fusion.258), channel_id=1, source_target_pairs={{32,0},{48,16},{64,32},{80,48},{96,64},{112,80},{128,96},{144,112}... | collective-permute-start | bytes 196616 | tf_op jit(solution)/shard_map/ppermute | solution.py:19
  99.9 12.2 %copy-start.13 = (f32[128,128]{1,0:T(8,128)}, f32[128,128]{1,0:T(8,128)S(1)}, u32[]{:S(2)}) copy-start(f32[128,128]{1,0:T(8,128)S(1)} %convolution_select_fusion.17) | copy-start | bytes 196612
  100.1 12.2 %collective-permute-start.16 = (f32[1,128,128]{2,1,0:T(8,128)S(1)}, f32[1,128,128]{2,1,0:T(8,128)S(1)}, u32[]{:S(2)}, u32[]{:S(2)}) collective-permute-start(f32[1,128,128]{2,1,0:T(8,128)S(1)} %fusion.263), channel_id=1, source_target_pairs={{0,64},{16,80},{32,96},{48,112},{64,128},{80,144},{96,160},{112,17... | collective-permute-start | bytes 196616 | tf_op jit(solution)/shard_map/ppermute | solution.py:19
  104.7 14.6 %collective-permute-start.21 = (f32[1,128,128]{2,1,0:T(8,128)S(1)}, f32[1,128,128]{2,1,0:T(8,128)S(1)}, u32[]{:S(2)}, u32[]{:S(2)}) collective-permute-start(f32[1,128,128]{2,1,0:T(8,128)S(1)} %fusion.251), channel_id=1, source_target_pairs={{0,64},{16,80},{32,96},{48,112},{64,128},{80,144},{96,160},{112,17... | collective-permute-start | bytes 196616 | tf_op jit(solution)/shard_map/ppermute | solution.py:19
  110.3 16.5 %copy-start.1 = (f32[1,128,128]{2,1,0:T(8,128)}, f32[1,128,128]{2,1,0:T(8,128)S(1)}, u32[]{:S(2)}) copy-start(f32[1,128,128]{2,1,0:T(8,128)S(1)} %fusion.259) | copy-start | bytes 196612
  110.3 16.4 %collective-permute-start.4 = (f32[1,128,128]{2,1,0:T(8,128)S(1)}, f32[1,128,128]{2,1,0:T(8,128)S(1)}, u32[]{:S(2)}, u32[]{:S(2)}) collective-permute-start(f32[1,128,128]{2,1,0:T(8,128)S(1)} %fusion.259), channel_id=1, source_target_pairs={{64,0},{80,16},{96,32},{112,48},{128,64},{144,80},{160,96},{176,11... | collective-permute-start | bytes 196616 | tf_op jit(solution)/shard_map/ppermute | solution.py:19
  112.3 16.5 %copy-start.3 = (f32[128,128]{1,0:T(8,128)}, f32[128,128]{1,0:T(8,128)S(1)}, u32[]{:S(2)}) copy-start(f32[128,128]{1,0:T(8,128)S(1)} %convolution_select_fusion.13) | copy-start | bytes 196612
  112.5 25.8 %collective-permute-start.17 = (f32[1,128,128]{2,1,0:T(8,128)S(1)}, f32[1,128,128]{2,1,0:T(8,128)S(1)}, u32[]{:S(2)}, u32[]{:S(2)}) collective-permute-start(f32[1,128,128]{2,1,0:T(8,128)S(1)} %fusion.264), channel_id=1, source_target_pairs={{0,128},{16,144},{32,160},{48,176},{64,192},{80,208},{96,224},{112... | collective-permute-start | bytes 196616 | tf_op jit(solution)/shard_map/ppermute | solution.py:19
  119.5 9.5 %collective-permute-start.22 = (f32[1,128,128]{2,1,0:T(8,128)S(1)}, f32[1,128,128]{2,1,0:T(8,128)S(1)}, u32[]{:S(2)}, u32[]{:S(2)}) collective-permute-start(f32[1,128,128]{2,1,0:T(8,128)S(1)} %fusion.253), channel_id=1, source_target_pairs={{0,128},{16,144},{32,160},{48,176},{64,192},{80,208},{96,224},{112... | collective-permute-start | bytes 196616 | tf_op jit(solution)/shard_map/ppermute | solution.py:19
  127.0 17.7 %copy-start.5 = (f32[1,128,128]{2,1,0:T(8,128)}, f32[1,128,128]{2,1,0:T(8,128)S(1)}, u32[]{:S(2)}) copy-start(f32[1,128,128]{2,1,0:T(8,128)S(1)} %fusion.260) | copy-start | bytes 196612
  127.0 17.7 %collective-permute-start.5 = (f32[1,128,128]{2,1,0:T(8,128)S(1)}, f32[1,128,128]{2,1,0:T(8,128)S(1)}, u32[]{:S(2)}, u32[]{:S(2)}) collective-permute-start(f32[1,128,128]{2,1,0:T(8,128)S(1)} %fusion.260), channel_id=1, source_target_pairs={{128,0},{144,16},{160,32},{176,48},{192,64},{208,80},{224,96},{240... | collective-permute-start | bytes 196616 | tf_op jit(solution)/shard_map/ppermute | solution.py:19
  129.0 17.7 %copy-start.7 = (f32[128,128]{1,0:T(8,128)}, f32[128,128]{1,0:T(8,128)S(1)}, u32[]{:S(2)}) copy-start(f32[128,128]{1,0:T(8,128)S(1)} %convolution_select_fusion.12) | copy-start | bytes 196612
  129.2 17.7 %collective-permute-start.23 = (f32[1,128,128]{2,1,0:T(8,128)S(1)}, f32[1,128,128]{2,1,0:T(8,128)S(1)}, u32[]{:S(2)}, u32[]{:S(2)}) collective-permute-start(f32[1,128,128]{2,1,0:T(8,128)S(1)} %fusion.255), channel_id=1, source_target_pairs={{0,256},{16,272},{32,288},{48,304},{64,320},{80,336},{96,352},{112... | collective-permute-start | bytes 196616 | tf_op jit(solution)/shard_map/ppermute | solution.py:19
  138.5 19.6 %collective-permute-start.18 = (f32[1,128,128]{2,1,0:T(8,128)S(1)}, f32[1,128,128]{2,1,0:T(8,128)S(1)}, u32[]{:S(2)}, u32[]{:S(2)}) collective-permute-start(f32[1,128,128]{2,1,0:T(8,128)S(1)} %fusion.265), channel_id=1, source_target_pairs={{0,256},{16,272},{32,288},{48,304},{64,320},{80,336},{96,352},{112... | collective-permute-start | bytes 196616 | tf_op jit(solution)/shard_map/ppermute | solution.py:19
  144.9 13.5 %collective-permute-start.6 = (f32[1,128,128]{2,1,0:T(8,128)S(1)}, f32[1,128,128]{2,1,0:T(8,128)S(1)}, u32[]{:S(2)}, u32[]{:S(2)}) collective-permute-start(f32[1,128,128]{2,1,0:T(8,128)S(1)} %fusion.261), channel_id=1, source_target_pairs={{256,0},{272,16},{288,32},{304,48},{320,64},{336,80},{352,96},{368... | collective-permute-start | bytes 196616 | tf_op jit(solution)/shard_map/ppermute | solution.py:19
  146.9 11.5 %copy-start.9 = (f32[128,128]{1,0:T(8,128)}, f32[128,128]{1,0:T(8,128)S(1)}, u32[]{:S(2)}) copy-start(f32[128,128]{1,0:T(8,128)S(1)} %convolution_select_fusion.11) | copy-start | bytes 196612
  147.1 12.7 %collective-permute-start.24 = (f32[1,128,128]{2,1,0:T(8,128)S(1)}, f32[1,128,128]{2,1,0:T(8,128)S(1)}, u32[]{:S(2)}, u32[]{:S(2)}) collective-permute-start(f32[1,128,128]{2,1,0:T(8,128)S(1)} %fusion.257), channel_id=1, source_target_pairs={{0,512},{16,528},{32,544},{48,560},{64,576},{80,592},{96,608},{112... | collective-permute-start | bytes 196616 | tf_op jit(solution)/shard_map/ppermute | solution.py:19
  166.4 45.8 %collective-permute-start.8 = (f32[1,128,128]{1,2,0:T(8,128)S(1)}, f32[1,128,128]{1,2,0:T(8,128)}, u32[]{:S(2)}, u32[]{:S(2)}) collective-permute-start(f32[1,128,128]{1,2,0:T(8,128)S(1)} %get-tuple-element.1103), channel_id=1, source_target_pairs={{16,0},{32,16},{48,32},{64,48},{80,64},{96,80},{112,96},{128,112},... | collective-permute-start | bytes 196616 | tf_op jit(solution)/shard_map/ppermute | solution.py:19
  214.0 8.6 %collective-permute-start.9 = (f32[1,128,128]{2,1,0:T(8,128)S(1)}, f32[1,128,128]{2,1,0:T(8,128)S(1)}, u32[]{:S(2)}, u32[]{:S(2)}) collective-permute-start(f32[1,128,128]{2,1,0:T(8,128)S(1)} %fusion.239), channel_id=1, source_target_pairs={{32,0},{48,16},{64,32},{80,48},{96,64},{112,80},{128,96},{144,112}... | collective-permute-start | bytes 196616 | tf_op jit(solution)/shard_map/ppermute | solution.py:19
  218.6 5.7 %copy-start.14 = (f32[128,128]{1,0:T(8,128)S(1)}, f32[128,128]{1,0:T(8,128)}, u32[]{:S(2)}) copy-start(f32[128,128]{1,0:T(8,128)} %copy-done.13) | copy-start | bytes 196612
  222.8 6.3 %copy-start.2 = (f32[1,128,128]{2,1,0:T(8,128)S(1)}, f32[1,128,128]{2,1,0:T(8,128)}, u32[]{:S(2)}) copy-start(f32[1,128,128]{2,1,0:T(8,128)} %copy-done.1) | copy-start | bytes 196612
  222.8 6.3 %collective-permute-start.10 = (f32[1,128,128]{2,1,0:T(8,128)S(1)}, f32[1,128,128]{2,1,0:T(8,128)S(1)}, u32[]{:S(2)}, u32[]{:S(2)}) collective-permute-start(f32[1,128,128]{2,1,0:T(8,128)S(1)} %fusion.241), channel_id=1, source_target_pairs={{64,0},{80,16},{96,32},{112,48},{128,64},{144,80},{160,96},{176,11... | collective-permute-start | bytes 196616 | tf_op jit(solution)/shard_map/ppermute | solution.py:19
  224.5 6.5 %copy-start.4 = (f32[128,128]{1,0:T(8,128)S(1)}, f32[128,128]{1,0:T(8,128)}, u32[]{:S(2)}) copy-start(f32[128,128]{1,0:T(8,128)} %copy-done.3) | copy-start | bytes 196612
  229.3 8.0 %copy-start.6 = (f32[1,128,128]{2,1,0:T(8,128)S(1)}, f32[1,128,128]{2,1,0:T(8,128)}, u32[]{:S(2)}) copy-start(f32[1,128,128]{2,1,0:T(8,128)} %copy-done.5) | copy-start | bytes 196612
  229.3 8.0 %collective-permute-start.11 = (f32[1,128,128]{2,1,0:T(8,128)S(1)}, f32[1,128,128]{2,1,0:T(8,128)S(1)}, u32[]{:S(2)}, u32[]{:S(2)}) collective-permute-start(f32[1,128,128]{2,1,0:T(8,128)S(1)} %fusion.243), channel_id=1, source_target_pairs={{128,0},{144,16},{160,32},{176,48},{192,64},{208,80},{224,96},{240... | collective-permute-start | bytes 196616 | tf_op jit(solution)/shard_map/ppermute | solution.py:19
  231.2 7.8 %copy-start.8 = (f32[128,128]{1,0:T(8,128)S(1)}, f32[128,128]{1,0:T(8,128)}, u32[]{:S(2)}) copy-start(f32[128,128]{1,0:T(8,128)} %copy-done.7) | copy-start | bytes 196612
  237.5 10.2 %copy-start.16 = (f32[1,128,128]{2,1,0:T(8,128)S(1)}, f32[1,128,128]{2,1,0:T(8,128)}, u32[]{:S(2)}) copy-start(f32[1,128,128]{2,1,0:T(8,128)} %copy-done.15) | copy-start | bytes 196612
  237.5 10.2 %collective-permute-start.12 = (f32[1,128,128]{2,1,0:T(8,128)S(1)}, f32[1,128,128]{2,1,0:T(8,128)S(1)}, u32[]{:S(2)}, u32[]{:S(2)}) collective-permute-start(f32[1,128,128]{2,1,0:T(8,128)S(1)} %fusion.245), channel_id=1, source_target_pairs={{256,0},{272,16},{288,32},{304,48},{320,64},{336,80},{352,96},{368... | collective-permute-start | bytes 196616 | tf_op jit(solution)/shard_map/ppermute | solution.py:19
  239.2 10.2 %copy-start.10 = (f32[128,128]{1,0:T(8,128)S(1)}, f32[128,128]{1,0:T(8,128)}, u32[]{:S(2)}) copy-start(f32[128,128]{1,0:T(8,128)} %copy-done.9) | copy-start | bytes 196612
  247.9 15.2 %copy-start.17 = (f32[128,128]{1,0:T(8,128)S(1)}, f32[128,128]{1,0:T(8,128)}, u32[]{:S(2)}) copy-start(f32[128,128]{1,0:T(8,128)} %convolution_select_fusion.10) | copy-start | bytes 196612
  247.9 15.2 %collective-permute-start.13 = (f32[1,128,128]{2,1,0:T(8,128)S(1)}, f32[1,128,128]{2,1,0:T(8,128)S(1)}, u32[]{:S(2)}, u32[]{:S(2)}) collective-permute-start(f32[1,128,128]{2,1,0:T(8,128)S(1)} %fusion.247), channel_id=1, source_target_pairs={{512,0},{528,16},{544,32},{560,48},{576,64},{592,80},{608,96},{624... | collective-permute-start | bytes 196616 | tf_op jit(solution)/shard_map/ppermute | solution.py:19
  451.1 9.9 %copy-start.39 = (f32[128]{0:T(128)S(1)}, f32[128]{0:T(128)}, u32[]{:S(2)}) copy-start(f32[128]{0:T(128)} %copy-done.38) | copy-start | bytes 1540
  451.8 9.3 %copy-start.33 = (f32[128]{0:T(128)S(1)}, f32[128]{0:T(128)}, u32[]{:S(2)}) copy-start(f32[128]{0:T(128)} %copy-done.32) | copy-start | bytes 1540
  451.8 9.3 %copy-start.35 = (f32[128]{0:T(128)S(1)}, f32[128]{0:T(128)}, u32[]{:S(2)}) copy-start(f32[128]{0:T(128)} %copy-done.34) | copy-start | bytes 1540
  451.8 9.3 %copy-start.37 = (f32[128]{0:T(128)S(1)}, f32[128]{0:T(128)}, u32[]{:S(2)}) copy-start(f32[128]{0:T(128)} %copy-done.36) | copy-start | bytes 1540
  451.8 18.2 %collective-permute-start.27 = (f32[1,3,128]{2,1,0:T(4,128)S(1)}, f32[1,3,128]{2,1,0:T(4,128)S(1)}, u32[]{:S(2)}, u32[]{:S(2)}) collective-permute-start(f32[1,3,128]{2,1,0:T(4,128)S(1)} %pad_add_fusion.3), channel_id=1, source_target_pairs={{16,0},{32,16},{48,32},{64,48},{80,64},{96,80},{112,96},{128,112},... | collective-permute-start | bytes 4616 | tf_op jit(solution)/shard_map/ppermute | solution.py:19
  458.6 12.1 %collective-permute-start.26 = (f32[1,3,128]{2,1,0:T(4,128)S(1)}, f32[1,3,128]{2,1,0:T(4,128)S(1)}, u32[]{:S(2)}, u32[]{:S(2)}) collective-permute-start(f32[1,3,128]{2,1,0:T(4,128)S(1)} %pad_add_fusion.4), channel_id=1, source_target_pairs={{16,0},{32,16},{48,32},{64,48},{80,64},{96,80},{112,96},{128,112},... | collective-permute-start | bytes 4616 | tf_op jit(solution)/shard_map/ppermute | solution.py:19
  461.2 10.2 %collective-permute-start.25 = (f32[1,3,128]{2,1,0:T(4,128)S(1)}, f32[1,3,128]{2,1,0:T(4,128)S(1)}, u32[]{:S(2)}, u32[]{:S(2)}) collective-permute-start(f32[1,3,128]{2,1,0:T(4,128)S(1)} %pad_add_fusion.5), channel_id=1, source_target_pairs={{16,0},{32,16},{48,32},{64,48},{80,64},{96,80},{112,96},{128,112},... | collective-permute-start | bytes 4616 | tf_op jit(solution)/shard_map/ppermute | solution.py:19
  (37 other events, 25.1 us)
Sparse Core Ops, SparseCore 0:
  20.5 52.5 all-gather.1

commit v2 on v1

--- a/solution.py
+++ b/solution.py
@@ -19,23 +19,41 @@
     return lax.ppermute(block, axis, route)
 
 
-def carried_in(parts, axis, combine, identity, reverse):
+def carried_in(parts, axis, combine, identity, reverse, radix=4):
     count = lax.axis_size(axis)
     place = lax.axis_index(axis)
     ranks = [count - 1 - place if back else place for back in reverse]
     fill = lambda a, e: jnp.zeros_like(a) + jnp.asarray(e, a.dtype)
-    totals = list(parts)
-    states = [jax.tree.map(fill, part, identity) for part in parts]
+    totals = [jnp.stack(part) for part in parts]
+    states = [jnp.stack(jax.tree.map(fill, part, identity)) for part in parts]
+    join = lambda a, b: jnp.stack(combine((a[0], a[1]), (b[0], b[1])))
     distance = 1
     while distance < count:
         for n, back in enumerate(reverse):
-            got = passed_along(totals[n], axis, -distance if back else distance)
-            keep = lambda new, old: jnp.where(ranks[n] >= distance, new, old)
-            states[n] = jax.tree.map(keep, combine(got, states[n]), states[n])
-            if 2 * distance < count:
-                totals[n] = jax.tree.map(keep, combine(got, totals[n]), totals[n])
+            state, total = states[n], totals[n]
+            for step in range(1, radix):
+                reach = step * distance
+                if reach >= count:
+                    break
+                got = passed_along(totals[n], axis, -reach if back else reach)
+                valid = ranks[n] >= reach
+                state = jnp.where(valid, join(got, state), state)
+                if radix * distance < count:
+                    total = jnp.where(valid, join(got, total), total)
+            states[n], totals[n] = state, total
+        distance *= radix
+    return [(s[0], s[1]) for s in states]
+
+
+def summed(part, axis):
+    count = lax.axis_size(axis)
+    if count & (count - 1):
+        return lax.psum(part, axis)
+    distance = 1
+    while distance < count:
+        part = part + lax.ppermute(part, axis, [(i, i ^ distance) for i in range(count)])
         distance *= 2
-    return states
+    return part
 
 
 def conv_silu(extended, weights, row_count):
@@ -179,7 +197,7 @@
 
     conv_local = grads[3].transpose(1, 2, 0, 3).reshape(3, CONV, col_count)
     scale = 1.0 / math.sqrt(row_count * lax.axis_size("ctx"))
-    conv_total = lax.psum(conv_local, "ctx") * scale
+    conv_total = summed(conv_local, "ctx") * scale
     return (
         finish(grads[0], rim_back[0]),
         finish(grads[1], rim_back[1]),

time: 481 us -> 354 us (0.74)
  blocking collectives: 139 us -> 0 us
  matrix products: 54.1 us -> 72.2 us
  waiting for transfers between devices: 37.5 us -> 22 us
  starting transfers between devices: 116 us -> 126 us
  local copies, waits for them, and re-layouts: 27.4 us -> 19.1 us
  other arithmetic: 88 us -> 93 us
    psum x1 -> x0, blocking collectives: 139 us -> none  [on_device(): conv_total = lax.psum(conv_local, 'ctx') * scale]
    ppermute x0 -> x6, starting transfers between devices: none -> 34.7 us  [summed(): lax.ppermute(part, axis, [(i, i ^ distance) for i in range(count)])]
    ppermute x28 -> x24, waiting for transfers between devices: 37.4 us -> 8.84 us  [passed_along(): return lax.ppermute(block, axis, route)]
    ppermute x28 -> x24, starting transfers between devices: 115 us -> 91.1 us  [passed_along(): return lax.ppermute(block, axis, route)]
    ppermute x0 -> x6, waiting for transfers between devices: none -> 13.2 us  [summed(): lax.ppermute(part, axis, [(i, i ^ distance) for i in range(count)])]
    while x36 -> x4, local copies, waits for them, and re-layouts: 9.78 us -> 0.03 us
    dot_general x18 -> x30, matrix products: 4.26 us -> 12.6 us  [combine_pairs(): product = jnp.matmul(later[0], earlier[0], precision=HIGHEST)]
    dot_general x22 -> x30, matrix products: 6.24 us -> 13.5 us  [combine_pairs(): offset_term = jnp.matmul(later[0], earlier[1], precision=HIGHEST) + later[1]]
  transfers between devices with their start and end apart: 29 -> 31, of which waited for: 6 -> 10; matrix products, arithmetic and copies ran while one was open for 20% -> 35% of each run, Pallas kernels for 0% -> 0%
where the time goes in v2:
time: 354 us; the launch traced here: 350 us
  starting transfers between devices  126 us (36%)
  other arithmetic  93 us (26%)
  matrix products  72.2 us (20%)
  waiting for transfers between devices  22 us (6%)
  local copies, waits for them, and re-layouts  19.1 us (5%)
  between operations  15.8 us (4%)
    ppermute x24, starting transfers between devices, passed_along(): return lax.ppermute(block, axis, route)  91.1 us
    another operation x24, other arithmetic, wy_factors(): jax.scipy.linalg.solve_triangular(system, value_rows * rates[:, None], lo...  42.9 us
    another operation x16, other arithmetic, wy_factors(): jax.scipy.linalg.solve_triangular(system, weighted, lower=True, unit_diag...  39.2 us
    ppermute x6, starting transfers between devices, summed(): lax.ppermute(part, axis, [(i, i ^ distance) for i in range(count)])  34.7 us
    dot_general x30, matrix products, combine_pairs(): offset_term = jnp.matmul(later[0], earlier[1], precision=HIGHEST) + later[1]  13.5 us
    unnamed x114, local copies, waits for them, and re-layouts  13.5 us
    ppermute x6, waiting for transfers between devices, summed(): lax.ppermute(part, axis, [(i, i ^ distance) for i in range(count)])  13.2 us
    dot_general x30, matrix products, combine_pairs(): product = jnp.matmul(later[0], earlier[0], precision=HIGHEST)  12.6 us
  transfers between devices with their start and end apart: 31, of which 10 were waited for; matrix products, arithmetic and copies ran while one was open for 35% of the time, Pallas kernels for 0%

profile of v2, /device:TPU:6, one launch (start us, length us, event | category | flops | bytes accessed | tf_op | source)
XLA Modules:
  0.0 349.9 jit_solution(3449098769594827181)
XLA Ops:
  8.0 4.2 %collective-permute-start.2 = (bf16[3,128]{1,0:T(4,128)(2,1)S(1)}, bf16[3,128]{1,0:T(4,128)(2,1)S(1)}, u32[]{:S(2)}, u32[]{:S(2)}) collective-permute-start(bf16[3,128]{1,0:T(4,128)(2,1)S(1)} %slice.489), channel_id=1, source_target_pairs={{0,16},{16,32},{32,48},{48,64},{64,80},{80,96},{96,112},{112,128},... | collective-permute-start | bytes 2312 | tf_op jit(solution)/shard_map/ppermute | solution.py:19
  12.8 3.4 collective-permute-start
  16.9 3.4 collective-permute-start.1
  22.5 1.3 fusion.279
  26.3 27.1 %while.106 = (s32[]{:T(128)}, f32[1,128,128]{2,1,0:T(8,128)S(1)}, f32[1,128,128]{2,1,0:T(8,128)S(1)}, f32[4,1,64,128]{3,2,1,0:T(8,128)S(1)}, f32[4,1,64]{2,1,0:T...) while((s32[]{:T(128)}, f32[1,128,128]{2,1,0:T(8,128)S(1)}, f32[1,128,128]{2,1,0:T(8,128)S(1)}, ...), condition=%wide.region_2.4_spmd.clone, body=%wide.region_1.3_spmd.clone.sunk | while | flops 94502976 | bytes 1134953 | solution.py:135
  26.6 4.9 %custom-call.27 = f32[1,1,64,64]{2,3,1,0:T(8,128)S(1)} custom-call(f32[1,1,64,64]{3,2,1,0:T(8,128)S(1)} %fusion.408), custom_call_target="InvertDiagBlocksLowerTriangular" | custom-call | tf_op jit(solution)/shard_map/vmap()/while/body/eval_jaxpr/jit(_solve_triangular)/triangular_solve/custom-call.1 | solution.py:74
  33.4 4.9 %custom-call.27 = f32[1,1,64,64]{2,3,1,0:T(8,128)S(1)} custom-call(f32[1,1,64,64]{3,2,1,0:T(8,128)S(1)} %fusion.408), custom_call_target="InvertDiagBlocksLowerTriangular" | custom-call | tf_op jit(solution)/shard_map/vmap()/while/body/eval_jaxpr/jit(_solve_triangular)/triangular_solve/custom-call.1 | solution.py:74
  40.1 4.9 %custom-call.27 = f32[1,1,64,64]{2,3,1,0:T(8,128)S(1)} custom-call(f32[1,1,64,64]{3,2,1,0:T(8,128)S(1)} %fusion.408), custom_call_target="InvertDiagBlocksLowerTriangular" | custom-call | tf_op jit(solution)/shard_map/vmap()/while/body/eval_jaxpr/jit(_solve_triangular)/triangular_solve/custom-call.1 | solution.py:74
  46.9 4.9 %custom-call.27 = f32[1,1,64,64]{2,3,1,0:T(8,128)S(1)} custom-call(f32[1,1,64,64]{3,2,1,0:T(8,128)S(1)} %fusion.408), custom_call_target="InvertDiagBlocksLowerTriangular" | custom-call | tf_op jit(solution)/shard_map/vmap()/while/body/eval_jaxpr/jit(_solve_triangular)/triangular_solve/custom-call.1 | solution.py:74
  53.5 3.1 collective-permute-start.12
  58.2 22.9 %while.107 = (s32[]{:T(128)}, f32[4,1,64,128]{3,2,1,0:T(8,128)S(1)}, f32[4,1,64,64]{3,2,1,0:T(8,128)S(1)}, f32[4,1,128,64]{3,2,1,0:T(8,128)S(1)}, f32[4,1,64,128...) while((s32[]{:T(128)}, f32[4,1,64,128]{3,2,1,0:T(8,128)S(1)}, ...), condition=%wide.region_5.7_spmd.clone, body=%wide.region_4.6_spmd.clone.sunk | while | flops 18939968 | bytes 547181 | solution.py:105
  58.5 4.9 %custom-call.28 = f32[1,1,64,64]{2,3,1,0:T(8,128)S(1)} custom-call(f32[1,1,64,64]{3,2,1,0:T(8,128)S(1)} %fusion.420), custom_call_target="InvertDiagBlocksLowerTriangular" | custom-call | tf_op jit(solution)/shard_map/jvp(vmap())/while/body/eval_jaxpr/jit(_solve_triangular)/triangular_solve/custom-call.1 | solution.py:74
  64.2 4.9 %custom-call.28 = f32[1,1,64,64]{2,3,1,0:T(8,128)S(1)} custom-call(f32[1,1,64,64]{3,2,1,0:T(8,128)S(1)} %fusion.420), custom_call_target="InvertDiagBlocksLowerTriangular" | custom-call | tf_op jit(solution)/shard_map/jvp(vmap())/while/body/eval_jaxpr/jit(_solve_triangular)/triangular_solve/custom-call.1 | solution.py:74
  69.9 4.9 %custom-call.28 = f32[1,1,64,64]{2,3,1,0:T(8,128)S(1)} custom-call(f32[1,1,64,64]{3,2,1,0:T(8,128)S(1)} %fusion.420), custom_call_target="InvertDiagBlocksLowerTriangular" | custom-call | tf_op jit(solution)/shard_map/jvp(vmap())/while/body/eval_jaxpr/jit(_solve_triangular)/triangular_solve/custom-call.1 | solution.py:74
  75.7 4.9 %custom-call.28 = f32[1,1,64,64]{2,3,1,0:T(8,128)S(1)} custom-call(f32[1,1,64,64]{3,2,1,0:T(8,128)S(1)} %fusion.420), custom_call_target="InvertDiagBlocksLowerTriangular" | custom-call | tf_op jit(solution)/shard_map/jvp(vmap())/while/body/eval_jaxpr/jit(_solve_triangular)/triangular_solve/custom-call.1 | solution.py:74
  81.7 5.1 %collective-permute-start.13 = (f32[2,1,128,128]{3,2,1,0:T(8,128)S(1)}, f32[2,1,128,128]{3,2,1,0:T(8,128)S(1)}, u32[]{:S(2)}, u32[]{:S(2)}) collective-permute-start(f32[2,1,128,128]{3,2,1,0:T(8,128)S(1)} %pad_maximum_fusion.1), channel_id=1, source_target_pairs={{0,32},{16,48},{32,64},{48,80},{64,96},{80,112},{96,128},{112,144}... | collective-permute-start | bytes 393224 | tf_op jit(solution)/shard_map/ppermute | solution.py:19
  86.8 3.6 %collective-permute-start.14 = (f32[2,1,128,128]{3,2,1,0:T(8,128)S(1)}, f32[2,1,128,128]{3,2,1,0:T(8,128)S(1)}, u32[]{:S(2)}, u32[]{:S(2)}) collective-permute-start(f32[2,1,128,128]{3,2,1,0:T(8,128)S(1)} %pad_maximum_fusion.1), channel_id=1, source_target_pairs={{0,48},{16,64},{32,80},{48,96},{64,112},{80,128},{96,144},{112,160... | collective-permute-start | bytes 393224 | tf_op jit(solution)/shard_map/ppermute | solution.py:19
  92.1 2.8 collective-permute-done.14
  96.2 5.1 %collective-permute-start.15 = (f32[2,1,128,128]{3,2,1,0:T(8,128)}, f32[2,1,128,128]{3,2,1,0:T(8,128)}, u32[]{:S(2)}, u32[]{:S(2)}) collective-permute-start(f32[2,1,128,128]{3,2,1,0:T(8,128)} %maximum_select_fusion.17), channel_id=1, source_target_pairs={{0,64},{16,80},{32,96},{48,112},{64,128},{80,144},{96,160},{112,17... | collective-permute-start | bytes 393224 | tf_op jit(solution)/shard_map/ppermute | solution.py:19
  101.3 6.5 %collective-permute-start.16 = (f32[2,1,128,128]{3,2,1,0:T(8,128)}, f32[2,1,128,128]{3,2,1,0:T(8,128)S(1)}, u32[]{:S(2)}, u32[]{:S(2)}) collective-permute-start(f32[2,1,128,128]{3,2,1,0:T(8,128)} %maximum_select_fusion.17), channel_id=1, source_target_pairs={{0,128},{16,144},{32,160},{48,176},{64,192},{80,208},{96,224},{112... | collective-permute-start | bytes 393224 | tf_op jit(solution)/shard_map/ppermute | solution.py:19
  107.8 9.8 %collective-permute-start.17 = (f32[2,1,128,128]{3,2,1,0:T(8,128)}, f32[2,1,128,128]{3,2,1,0:T(8,128)}, u32[]{:S(2)}, u32[]{:S(2)}) collective-permute-start(f32[2,1,128,128]{3,2,1,0:T(8,128)} %maximum_select_fusion.17), channel_id=1, source_target_pairs={{0,192},{16,208},{32,224},{48,240},{64,256},{80,272},{96,288},{112... | collective-permute-start | bytes 393224 | tf_op jit(solution)/shard_map/ppermute | solution.py:19
  119.2 1.7 fusion.280
  120.8 4.6 %while.110 = (s32[]{:T(128)}, f32[1,128,128]{1,2,0:T(8,128)S(1)}, f32[4,1,64,128]{3,2,1,0:T(8,128)S(1)}, f32[4,1,64,128]{3,2,1,0:T(8,128)S(1)}, f32[4,1,128,64]{...) while((s32[]{:T(128)}, f32[1,128,128]{1,2,0:T(8,128)S(1)}, ...), condition=%wide.region_7.9_spmd.clone, body=%wide.region_6.8_spmd.clone.sunk | while | flops 44122116 | bytes 690827 | solution.py:105
  125.6 1.9 collective-permute-start.3
  127.5 1.1 fusion.231
  128.6 1.1 convolution_bitcast_fusion.21
  129.7 2.9 collective-permute-start.4
  132.7 1.9 collective-permute-start.5
  134.6 1.3 collective-permute-done.3
  136.3 2.7 collective-permute-done.4
  139.4 2.0 collective-permute-done.5
  141.9 1.3 collective-permute-start.6
  143.2 1.3 collective-permute-start.7
  144.5 1.3 collective-permute-start.8
  154.4 15.3 %collective-permute-start.20 = (f32[2,1,128,128]{3,2,1,0:T(8,128)S(1)}, f32[2,1,128,128]{3,2,1,0:T(8,128)S(1)}, u32[]{:S(2)}, u32[]{:S(2)}) collective-permute-start(f32[2,1,128,128]{3,2,1,0:T(8,128)S(1)} %maximum_select_fusion.23), channel_id=1, source_target_pairs={{0,768},{16,784},{32,800},{48,816},{64,832},{80,848},{96,864},{112... | collective-permute-start | bytes 393224 | tf_op jit(solution)/shard_map/ppermute | solution.py:19
  169.7 1.3 collective-permute-start.18
  174.5 7.3 %collective-permute-start.19 = (f32[2,1,128,128]{3,2,1,0:T(8,128)S(1)}, f32[2,1,128,128]{3,2,1,0:T(8,128)S(1)}, u32[]{:S(2)}, u32[]{:S(2)}) collective-permute-start(f32[2,1,128,128]{3,2,1,0:T(8,128)S(1)} %maximum_select_fusion.23), channel_id=1, source_target_pairs={{0,512},{16,528},{32,544},{48,560},{64,576},{80,592},{96,608},{112... | collective-permute-start | bytes 393224 | tf_op jit(solution)/shard_map/ppermute | solution.py:19
  184.8 1.3 collective-permute-start.11
  186.0 1.5 collective-permute-start.9
  187.5 1.3 collective-permute-start.10
  191.7 31.7 %while.108 = (s32[]{:T(128)}, f32[1,128,128]{2,1,0:T(8,128)S(1)}, f32[4,1,64,1]{2,3,1,0:T(1,128)S(1)}, f32[4,1,128,64]{3,2,1,0:T(8,128)S(1)}, f32[4,1,64,128]{3,...) while((s32[]{:T(128)}, f32[1,128,128]{2,1,0:T(8,128)S(1)}, ...), condition=%wide.region_9.11_spmd.clone, body=%wide.region_8.10_spmd.clone.sunk | while | flops 50430016 | bytes 1695181 | solution.py:105
  192.7 4.9 %custom-call.29 = f32[1,1,64,64]{2,3,1,0:T(8,128)S(1)} custom-call(f32[1,1,64,64]{3,2,1,0:T(8,128)S(1)} %fusion.429), custom_call_target="InvertDiagBlocksLowerTriangular" | custom-call | tf_op jit(solution)/shard_map/jvp(vmap())/while/body/eval_jaxpr/jit(_solve_triangular)/triangular_solve/custom-call.1 | solution.py:75
  200.6 4.9 %custom-call.29 = f32[1,1,64,64]{2,3,1,0:T(8,128)S(1)} custom-call(f32[1,1,64,64]{3,2,1,0:T(8,128)S(1)} %fusion.429), custom_call_target="InvertDiagBlocksLowerTriangular" | custom-call | tf_op jit(solution)/shard_map/jvp(vmap())/while/body/eval_jaxpr/jit(_solve_triangular)/triangular_solve/custom-call.1 | solution.py:75
  208.6 4.9 %custom-call.29 = f32[1,1,64,64]{2,3,1,0:T(8,128)S(1)} custom-call(f32[1,1,64,64]{3,2,1,0:T(8,128)S(1)} %fusion.429), custom_call_target="InvertDiagBlocksLowerTriangular" | custom-call | tf_op jit(solution)/shard_map/jvp(vmap())/while/body/eval_jaxpr/jit(_solve_triangular)/triangular_solve/custom-call.1 | solution.py:75
  216.5 4.9 %custom-call.29 = f32[1,1,64,64]{2,3,1,0:T(8,128)S(1)} custom-call(f32[1,1,64,64]{3,2,1,0:T(8,128)S(1)} %fusion.429), custom_call_target="InvertDiagBlocksLowerTriangular" | custom-call | tf_op jit(solution)/shard_map/jvp(vmap())/while/body/eval_jaxpr/jit(_solve_triangular)/triangular_solve/custom-call.1 | solution.py:75
  223.4 1.1 fusion.246
  232.7 43.6 %while.109 = (s32[]{:T(128)}, f32[1,128,128]{1,2,0:T(8,128)S(1)}, f32[4,1,64,128]{3,2,1,0:T(8,128)S(1)}, f32[4,1,64,128]{3,2,1,0:T(8,128)S(1)}, f32[4,1,64,128]{...) while((s32[]{:T(128)}, f32[1,128,128]{1,2,0:T(8,128)S(1)}, ...), condition=%wide.region_13.16_spmd.clone.clone, body=%wide.region_10.15_spmd.clone.clone.sunk | while | flops 144912384 | bytes 2420489 | solution.py:105
  235.3 4.9 %custom-call.30 = f32[1,1,64,64]{2,3,1,0:T(8,128)S(1)} custom-call(f32[1,1,64,64]{3,2,1,0:T(8,128)S(1)} %fusion.470), custom_call_target="InvertDiagBlocksLowerTriangular" | custom-call | tf_op jit(solution)/shard_map/transpose(jvp(vmap()))/while/body/eval_jaxpr/jit(_solve_triangular)/triangular_solve | solution.py:75
  246.2 4.9 %custom-call.30 = f32[1,1,64,64]{2,3,1,0:T(8,128)S(1)} custom-call(f32[1,1,64,64]{3,2,1,0:T(8,128)S(1)} %fusion.470), custom_call_target="InvertDiagBlocksLowerTriangular" | custom-call | tf_op jit(solution)/shard_map/transpose(jvp(vmap()))/while/body/eval_jaxpr/jit(_solve_triangular)/triangular_solve | solution.py:75
  257.1 4.9 %custom-call.30 = f32[1,1,64,64]{2,3,1,0:T(8,128)S(1)} custom-call(f32[1,1,64,64]{3,2,1,0:T(8,128)S(1)} %fusion.470), custom_call_target="InvertDiagBlocksLowerTriangular" | custom-call | tf_op jit(solution)/shard_map/transpose(jvp(vmap()))/while/body/eval_jaxpr/jit(_solve_triangular)/triangular_solve | solution.py:75
  268.0 4.9 %custom-call.30 = f32[1,1,64,64]{2,3,1,0:T(8,128)S(1)} custom-call(f32[1,1,64,64]{3,2,1,0:T(8,128)S(1)} %fusion.470), custom_call_target="InvertDiagBlocksLowerTriangular" | custom-call | tf_op jit(solution)/shard_map/transpose(jvp(vmap()))/while/body/eval_jaxpr/jit(_solve_triangular)/triangular_solve | solution.py:75
  280.9 3.1 collective-permute-start.21
  287.1 2.2 collective-permute-start.22
  289.3 3.1 collective-permute-start.23
  292.4 1.9 collective-permute-start.24
  294.4 3.6 %collective-permute-done.24 = f32[3,4,128]{2,1,0:T(4,128)S(1)} collective-permute-done((f32[3,4,128]{2,1,0:T(4,128)S(1)}, f32[3,4,128]{2,1,0:T(4,128)S(1)}, u32[]{:S(2)}, u32[]{:S(2)}) %collective-permute-start.24) | collective-permute-done | bytes 6176 | tf_op jit(solution)/shard_map/ppermute | solution.py:54
  298.0 2.0 collective-permute-start.25
  300.0 5.0 %collective-permute-done.25 = f32[3,4,128]{2,1,0:T(4,128)S(1)} collective-permute-done((f32[3,4,128]{2,1,0:T(4,128)S(1)}, f32[3,4,128]{2,1,0:T(4,128)S(1)}, u32[]{:S(2)}, u32[]{:S(2)}) %collective-permute-start.25) | collective-permute-done | bytes 6176 | tf_op jit(solution)/shard_map/ppermute | solution.py:54
  305.0 3.9 %collective-permute-start.26 = (f32[3,4,128]{2,1,0:T(4,128)S(1)}, f32[3,4,128]{2,1,0:T(4,128)S(1)}, u32[]{:S(2)}, u32[]{:S(2)}) collective-permute-start(f32[3,4,128]{2,1,0:T(4,128)S(1)} %fusion.297), channel_id=1, source_target_pairs={{0,64},{16,80},{32,96},{48,112},{64,0},{80,16},{96,32},{112,48},{1... | collective-permute-start | bytes 18440 | tf_op jit(solution)/shard_map/ppermute | solution.py:54
  308.9 1.6 collective-permute-done.26
  310.5 4.6 %collective-permute-start.27 = (f32[3,4,128]{2,1,0:T(4,128)S(1)}, f32[3,4,128]{2,1,0:T(4,128)S(1)}, u32[]{:S(2)}, u32[]{:S(2)}) collective-permute-start(f32[3,4,128]{2,1,0:T(4,128)S(1)} %add.463), channel_id=1, source_target_pairs={{0,128},{16,144},{32,160},{48,176},{64,192},{80,208},{96,224},{112... | collective-permute-start | bytes 18440 | tf_op jit(solution)/shard_map/ppermute | solution.py:54
  315.7 1.2 collective-permute-done.27
  316.9 8.5 %collective-permute-start.28 = (f32[3,4,128]{2,1,0:T(4,128)S(1)}, f32[3,4,128]{2,1,0:T(4,128)S(1)}, u32[]{:S(2)}, u32[]{:S(2)}) collective-permute-start(f32[3,4,128]{2,1,0:T(4,128)S(1)} %add.464), channel_id=1, source_target_pairs={{0,256},{16,272},{32,288},{48,304},{64,320},{80,336},{96,352},{112... | collective-permute-start | bytes 18440 | tf_op jit(solution)/shard_map/ppermute | solution.py:54
  327.0 13.9 %collective-permute-start.29 = (f32[3,4,128]{2,1,0:T(4,128)S(1)}, f32[3,4,128]{2,1,0:T(4,128)S(1)}, u32[]{:S(2)}, u32[]{:S(2)}) collective-permute-start(f32[3,4,128]{2,1,0:T(4,128)S(1)} %add.465), channel_id=1, source_target_pairs={{0,512},{16,528},{32,544},{48,560},{64,576},{80,592},{96,608},{112... | collective-permute-start | bytes 18440 | tf_op jit(solution)/shard_map/ppermute | solution.py:54
  (545 shorter events, 101.8 us)
Async XLA Ops:
  7.2 112.0 %copy-start = (bf16[128,2048]{1,0:T(8,128)(2,1)S(1)}, bf16[128,2048]{1,0:T(8,128)(2,1)}, u32[]{:S(2)}) copy-start(bf16[128,2048]{1,0:T(8,128)(2,1)} %param.28) | copy-start | bytes 1572868
  7.2 112.0 %all-gather.2.cloned.1.call-start = ((), (), s32[]{:S(2)}) async-start(), calls=%async_computation | async-start | bytes 1114112 | tf_op jit(solution)/shard_map/all_gather | solution.py:164
  8.0 48.6 %collective-permute-start.2 = (bf16[3,128]{1,0:T(4,128)(2,1)S(1)}, bf16[3,128]{1,0:T(4,128)(2,1)S(1)}, u32[]{:S(2)}, u32[]{:S(2)}) collective-permute-start(bf16[3,128]{1,0:T(4,128)(2,1)S(1)} %slice.489), channel_id=1, source_target_pairs={{0,16},{16,32},{32,48},{48,64},{64,80},{80,96},{96,112},{112,128},... | collective-permute-start | bytes 2312 | tf_op jit(solution)/shard_map/ppermute | solution.py:19
  12.8 11.0 %collective-permute-start = (bf16[3,128]{1,0:T(4,128)(2,1)S(1)}, bf16[3,128]{1,0:T(4,128)(2,1)S(1)}, u32[]{:S(2)}, u32[]{:S(2)}) collective-permute-start(bf16[3,128]{1,0:T(4,128)(2,1)S(1)} %slice.470), channel_id=1, source_target_pairs={{0,16},{16,32},{32,48},{48,64},{64,80},{80,96},{96,112},{112,128},... | collective-permute-start | bytes 2312 | tf_op jit(solution)/shard_map/ppermute | solution.py:19
  16.9 8.3 %collective-permute-start.1 = (bf16[3,128]{1,0:T(4,128)(2,1)S(1)}, bf16[3,128]{1,0:T(4,128)(2,1)S(1)}, u32[]{:S(2)}, u32[]{:S(2)}) collective-permute-start(bf16[3,128]{1,0:T(4,128)(2,1)S(1)} %slice.480), channel_id=1, source_target_pairs={{0,16},{16,32},{32,48},{48,64},{64,80},{80,96},{96,112},{112,128},... | collective-permute-start | bytes 2312 | tf_op jit(solution)/shard_map/ppermute | solution.py:19
  21.0 0.7 copy-start.26
  21.0 2.9 copy-start.14
  21.7 34.9 %copy-start.43 = (f32[128]{0:T(128)}, f32[128]{0:T(128)S(1)}, u32[]{:S(2)}) copy-start(f32[128]{0:T(128)S(1)} %get-tuple-element.1544) | copy-start | bytes 1540
  21.7 34.9 %copy-start.45 = (f32[128]{0:T(128)}, f32[128]{0:T(128)S(1)}, u32[]{:S(2)}) copy-start(f32[128]{0:T(128)S(1)} %get-tuple-element.1545) | copy-start | bytes 1540
  21.7 34.9 %copy-start.47 = (f32[128]{0:T(128)}, f32[128]{0:T(128)S(1)}, u32[]{:S(2)}) copy-start(f32[128]{0:T(128)S(1)} %get-tuple-element.1546) | copy-start | bytes 1540
  21.7 34.9 %copy-start.49 = (f32[128]{0:T(128)}, f32[128]{0:T(128)S(1)}, u32[]{:S(2)}) copy-start(f32[128]{0:T(128)S(1)} %get-tuple-element.1547) | copy-start | bytes 1540
  21.7 2.2 copy-start.35
  21.7 2.2 copy-start.37
  21.7 2.2 copy-start.39
  21.7 2.2 copy-start.41
  21.8 3.8 %copy-start.27 = (f32[128]{0:T(128)}, f32[128]{0:T(128)S(1)}, u32[]{:S(2)}) copy-start(f32[128]{0:T(128)S(1)} %get-tuple-element.1536) | copy-start | bytes 1540
  21.8 3.8 %copy-start.29 = (f32[128]{0:T(128)}, f32[128]{0:T(128)S(1)}, u32[]{:S(2)}) copy-start(f32[128]{0:T(128)S(1)} %get-tuple-element.1537) | copy-start | bytes 1540
  21.8 3.8 %copy-start.31 = (f32[128]{0:T(128)}, f32[128]{0:T(128)S(1)}, u32[]{:S(2)}) copy-start(f32[128]{0:T(128)S(1)} %get-tuple-element.1538) | copy-start | bytes 1540
  21.8 3.8 %copy-start.33 = (f32[128]{0:T(128)}, f32[128]{0:T(128)S(1)}, u32[]{:S(2)}) copy-start(f32[128]{0:T(128)S(1)} %get-tuple-element.1539) | copy-start | bytes 1540
  21.8 0.7 copy-start.54
  24.7 0.8 copy-start.15
  53.4 3.2 copy-start.16
  53.5 37.0 %collective-permute-start.12 = (f32[2,1,128,128]{3,2,1,0:T(8,128)S(1)}, f32[2,1,128,128]{3,2,1,0:T(8,128)S(1)}, u32[]{:S(2)}, u32[]{:S(2)}) collective-permute-start(f32[2,1,128,128]{3,2,1,0:T(8,128)S(1)} %pad_maximum_fusion.1), channel_id=1, source_target_pairs={{0,16},{16,32},{32,48},{48,64},{64,80},{80,96},{96,112},{112,128},... | collective-permute-start | bytes 393224 | tf_op jit(solution)/shard_map/ppermute | solution.py:19
  81.7 9.7 %collective-permute-start.13 = (f32[2,1,128,128]{3,2,1,0:T(8,128)S(1)}, f32[2,1,128,128]{3,2,1,0:T(8,128)S(1)}, u32[]{:S(2)}, u32[]{:S(2)}) collective-permute-start(f32[2,1,128,128]{3,2,1,0:T(8,128)S(1)} %pad_maximum_fusion.1), channel_id=1, source_target_pairs={{0,32},{16,48},{32,64},{48,80},{64,96},{80,112},{96,128},{112,144}... | collective-permute-start | bytes 393224 | tf_op jit(solution)/shard_map/ppermute | solution.py:19
  86.8 8.1 %collective-permute-start.14 = (f32[2,1,128,128]{3,2,1,0:T(8,128)S(1)}, f32[2,1,128,128]{3,2,1,0:T(8,128)S(1)}, u32[]{:S(2)}, u32[]{:S(2)}) collective-permute-start(f32[2,1,128,128]{3,2,1,0:T(8,128)S(1)} %pad_maximum_fusion.1), channel_id=1, source_target_pairs={{0,48},{16,64},{32,80},{48,96},{64,112},{80,128},{96,144},{112,160... | collective-permute-start | bytes 393224 | tf_op jit(solution)/shard_map/ppermute | solution.py:19
  95.5 22.0 %copy-start.11 = (f32[2,1,128,128]{3,2,1,0:T(8,128)S(1)}, f32[2,1,128,128]{3,2,1,0:T(8,128)}, u32[]{:S(2)}) copy-start(f32[2,1,128,128]{3,2,1,0:T(8,128)} %copy-done.10) | copy-start | bytes 393220
  96.2 31.3 %collective-permute-start.15 = (f32[2,1,128,128]{3,2,1,0:T(8,128)}, f32[2,1,128,128]{3,2,1,0:T(8,128)}, u32[]{:S(2)}, u32[]{:S(2)}) collective-permute-start(f32[2,1,128,128]{3,2,1,0:T(8,128)} %maximum_select_fusion.17), channel_id=1, source_target_pairs={{0,64},{16,80},{32,96},{48,112},{64,128},{80,144},{96,160},{112,17... | collective-permute-start | bytes 393224 | tf_op jit(solution)/shard_map/ppermute | solution.py:19
  101.3 50.5 %collective-permute-start.16 = (f32[2,1,128,128]{3,2,1,0:T(8,128)}, f32[2,1,128,128]{3,2,1,0:T(8,128)S(1)}, u32[]{:S(2)}, u32[]{:S(2)}) collective-permute-start(f32[2,1,128,128]{3,2,1,0:T(8,128)} %maximum_select_fusion.17), channel_id=1, source_target_pairs={{0,128},{16,144},{32,160},{48,176},{64,192},{80,208},{96,224},{112... | collective-permute-start | bytes 393224 | tf_op jit(solution)/shard_map/ppermute | solution.py:19
  107.8 44.4 %collective-permute-start.17 = (f32[2,1,128,128]{3,2,1,0:T(8,128)}, f32[2,1,128,128]{3,2,1,0:T(8,128)}, u32[]{:S(2)}, u32[]{:S(2)}) collective-permute-start(f32[2,1,128,128]{3,2,1,0:T(8,128)} %maximum_select_fusion.17), channel_id=1, source_target_pairs={{0,192},{16,208},{32,224},{48,240},{64,256},{80,272},{96,288},{112... | collective-permute-start | bytes 393224 | tf_op jit(solution)/shard_map/ppermute | solution.py:19
  125.6 10.3 %collective-permute-start.3 = (f32[2,1,128,128]{3,2,1,0:T(8,128)S(1)}, f32[2,1,128,128]{3,2,1,0:T(8,128)S(1)}, u32[]{:S(2)}, u32[]{:S(2)}) collective-permute-start(f32[2,1,128,128]{3,2,1,0:T(8,128)S(1)} %pad_maximum_fusion), channel_id=1, source_target_pairs={{16,0},{32,16},{48,32},{64,48},{80,64},{96,80},{112,96},{128,112},... | collective-permute-start | bytes 393224 | tf_op jit(solution)/shard_map/ppermute | solution.py:19
  129.7 9.3 %collective-permute-start.4 = (f32[2,1,128,128]{3,2,1,0:T(8,128)S(1)}, f32[2,1,128,128]{3,2,1,0:T(8,128)S(1)}, u32[]{:S(2)}, u32[]{:S(2)}) collective-permute-start(f32[2,1,128,128]{3,2,1,0:T(8,128)S(1)} %pad_maximum_fusion), channel_id=1, source_target_pairs={{32,0},{48,16},{64,32},{80,48},{96,64},{112,80},{128,96},{144,112}... | collective-permute-start | bytes 393224 | tf_op jit(solution)/shard_map/ppermute | solution.py:19
  132.7 8.8 %collective-permute-start.5 = (f32[2,1,128,128]{3,2,1,0:T(8,128)S(1)}, f32[2,1,128,128]{3,2,1,0:T(8,128)S(1)}, u32[]{:S(2)}, u32[]{:S(2)}) collective-permute-start(f32[2,1,128,128]{3,2,1,0:T(8,128)S(1)} %pad_maximum_fusion), channel_id=1, source_target_pairs={{48,0},{64,16},{80,32},{96,48},{112,64},{128,80},{144,96},{160,112... | collective-permute-start | bytes 393224 | tf_op jit(solution)/shard_map/ppermute | solution.py:19
  141.9 32.6 %collective-permute-start.6 = (f32[2,1,128,128]{3,2,1,0:T(8,128)S(1)}, f32[2,1,128,128]{3,2,1,0:T(8,128)S(1)}, u32[]{:S(2)}, u32[]{:S(2)}) collective-permute-start(f32[2,1,128,128]{3,2,1,0:T(8,128)S(1)} %maximum_select_fusion.4), channel_id=1, source_target_pairs={{64,0},{80,16},{96,32},{112,48},{128,64},{144,80},{160,96},{176,11... | collective-permute-start | bytes 393224 | tf_op jit(solution)/shard_map/ppermute | solution.py:19
  143.2 39.5 %collective-permute-start.7 = (f32[2,1,128,128]{3,2,1,0:T(8,128)S(1)}, f32[2,1,128,128]{3,2,1,0:T(8,128)S(1)}, u32[]{:S(2)}, u32[]{:S(2)}) collective-permute-start(f32[2,1,128,128]{3,2,1,0:T(8,128)S(1)} %maximum_select_fusion.4), channel_id=1, source_target_pairs={{128,0},{144,16},{160,32},{176,48},{192,64},{208,80},{224,96},{240... | collective-permute-start | bytes 393224 | tf_op jit(solution)/shard_map/ppermute | solution.py:19
  144.5 38.9 %collective-permute-start.8 = (f32[2,1,128,128]{3,2,1,0:T(8,128)S(1)}, f32[2,1,128,128]{3,2,1,0:T(8,128)S(1)}, u32[]{:S(2)}, u32[]{:S(2)}) collective-permute-start(f32[2,1,128,128]{3,2,1,0:T(8,128)S(1)} %maximum_select_fusion.4), channel_id=1, source_target_pairs={{192,0},{208,16},{224,32},{240,48},{256,64},{272,80},{288,96},{304... | collective-permute-start | bytes 393224 | tf_op jit(solution)/shard_map/ppermute | solution.py:19
  145.8 0.7 copy-start.17
  146.0 0.8 copy-start.12
  146.0 0.9 copy-start.13
  146.9 0.9 copy-start.6
  148.2 0.9 copy-start.8
  154.4 35.4 %collective-permute-start.20 = (f32[2,1,128,128]{3,2,1,0:T(8,128)S(1)}, f32[2,1,128,128]{3,2,1,0:T(8,128)S(1)}, u32[]{:S(2)}, u32[]{:S(2)}) collective-permute-start(f32[2,1,128,128]{3,2,1,0:T(8,128)S(1)} %maximum_select_fusion.23), channel_id=1, source_target_pairs={{0,768},{16,784},{32,800},{48,816},{64,832},{80,848},{96,864},{112... | collective-permute-start | bytes 393224 | tf_op jit(solution)/shard_map/ppermute | solution.py:19
  169.7 17.8 %collective-permute-start.18 = (f32[2,1,128,128]{3,2,1,0:T(8,128)S(1)}, f32[2,1,128,128]{3,2,1,0:T(8,128)S(1)}, u32[]{:S(2)}, u32[]{:S(2)}) collective-permute-start(f32[2,1,128,128]{3,2,1,0:T(8,128)S(1)} %maximum_select_fusion.23), channel_id=1, source_target_pairs={{0,256},{16,272},{32,288},{48,304},{64,320},{80,336},{96,352},{112... | collective-permute-start | bytes 393224 | tf_op jit(solution)/shard_map/ppermute | solution.py:19
  174.5 14.8 %collective-permute-start.19 = (f32[2,1,128,128]{3,2,1,0:T(8,128)S(1)}, f32[2,1,128,128]{3,2,1,0:T(8,128)S(1)}, u32[]{:S(2)}, u32[]{:S(2)}) collective-permute-start(f32[2,1,128,128]{3,2,1,0:T(8,128)S(1)} %maximum_select_fusion.23), channel_id=1, source_target_pairs={{0,512},{16,528},{32,544},{48,560},{64,576},{80,592},{96,608},{112... | collective-permute-start | bytes 393224 | tf_op jit(solution)/shard_map/ppermute | solution.py:19
  184.8 45.7 %collective-permute-start.11 = (f32[2,1,128,128]{3,2,1,0:T(8,128)}, f32[2,1,128,128]{3,2,1,0:T(8,128)}, u32[]{:S(2)}, u32[]{:S(2)}) collective-permute-start(f32[2,1,128,128]{3,2,1,0:T(8,128)} %maximum_select_fusion.10), channel_id=1, source_target_pairs={{768,0},{784,16},{800,32},{816,48},{832,64},{848,80},{864,96},{880... | collective-permute-start | bytes 393224 | tf_op jit(solution)/shard_map/ppermute | solution.py:19
  186.0 40.1 %collective-permute-start.9 = (f32[2,1,128,128]{3,2,1,0:T(8,128)}, f32[2,1,128,128]{3,2,1,0:T(8,128)}, u32[]{:S(2)}, u32[]{:S(2)}) collective-permute-start(f32[2,1,128,128]{3,2,1,0:T(8,128)} %maximum_select_fusion.10), channel_id=1, source_target_pairs={{256,0},{272,16},{288,32},{304,48},{320,64},{336,80},{352,96},{368... | collective-permute-start | bytes 393224 | tf_op jit(solution)/shard_map/ppermute | solution.py:19
  187.5 40.7 %collective-permute-start.10 = (f32[2,1,128,128]{3,2,1,0:T(8,128)}, f32[2,1,128,128]{3,2,1,0:T(8,128)}, u32[]{:S(2)}, u32[]{:S(2)}) collective-permute-start(f32[2,1,128,128]{3,2,1,0:T(8,128)} %maximum_select_fusion.10), channel_id=1, source_target_pairs={{512,0},{528,16},{544,32},{560,48},{576,64},{592,80},{608,96},{624... | collective-permute-start | bytes 393224 | tf_op jit(solution)/shard_map/ppermute | solution.py:19
  191.0 0.7 copy-start.53
  191.0 0.7 copy-start.55
  223.4 1.1 copy-start.2
  224.7 0.9 copy-start.4
  276.3 0.7 copy-start.25
  280.1 0.7 copy-start.36
  280.1 0.7 copy-start.38
  280.9 3.2 copy-start.9
  280.9 13.4 %collective-permute-start.21 = (f32[1,3,128]{2,1,0:T(4,128)S(1)}, f32[1,3,128]{2,1,0:T(4,128)S(1)}, u32[]{:S(2)}, u32[]{:S(2)}) collective-permute-start(f32[1,3,128]{2,1,0:T(4,128)S(1)} %pad_add_fusion.5), channel_id=1, source_target_pairs={{16,0},{32,16},{48,32},{64,48},{80,64},{96,80},{112,96},{128,112},... | collective-permute-start | bytes 4616 | tf_op jit(solution)/shard_map/ppermute | solution.py:19
  285.7 0.7 copy-start.51
  287.1 12.8 %collective-permute-start.22 = (f32[1,3,128]{2,1,0:T(4,128)S(1)}, f32[1,3,128]{2,1,0:T(4,128)S(1)}, u32[]{:S(2)}, u32[]{:S(2)}) collective-permute-start(f32[1,3,128]{2,1,0:T(4,128)S(1)} %pad_add_fusion.4), channel_id=1, source_target_pairs={{16,0},{32,16},{48,32},{64,48},{80,64},{96,80},{112,96},{128,112},... | collective-permute-start | bytes 4616 | tf_op jit(solution)/shard_map/ppermute | solution.py:19
  289.3 19.6 %collective-permute-start.23 = (f32[1,3,128]{2,1,0:T(4,128)S(1)}, f32[1,3,128]{2,1,0:T(4,128)S(1)}, u32[]{:S(2)}, u32[]{:S(2)}) collective-permute-start(f32[1,3,128]{2,1,0:T(4,128)S(1)} %pad_add_fusion.3), channel_id=1, source_target_pairs={{16,0},{32,16},{48,32},{64,48},{80,64},{96,80},{112,96},{128,112},... | collective-permute-start | bytes 4616 | tf_op jit(solution)/shard_map/ppermute | solution.py:19
  292.4 5.5 %collective-permute-start.24 = (f32[3,4,128]{2,1,0:T(4,128)S(1)}, f32[3,4,128]{2,1,0:T(4,128)S(1)}, u32[]{:S(2)}, u32[]{:S(2)}) collective-permute-start(f32[3,4,128]{2,1,0:T(4,128)S(1)} %add_bitcast_fusion), channel_id=1, source_target_pairs={{0,16},{16,0},{32,48},{48,32},{64,80},{80,64},{96,112},{112,96},{1... | collective-permute-start | bytes 18440 | tf_op jit(solution)/shard_map/ppermute | solution.py:54
  298.0 7.0 %collective-permute-start.25 = (f32[3,4,128]{2,1,0:T(4,128)S(1)}, f32[3,4,128]{2,1,0:T(4,128)S(1)}, u32[]{:S(2)}, u32[]{:S(2)}) collective-permute-start(f32[3,4,128]{2,1,0:T(4,128)S(1)} %fusion.275), channel_id=1, source_target_pairs={{0,32},{16,48},{32,0},{48,16},{64,96},{80,112},{96,64},{112,80},{1... | collective-permute-start | bytes 18440 | tf_op jit(solution)/shard_map/ppermute | solution.py:54
  305.0 5.5 %collective-permute-start.26 = (f32[3,4,128]{2,1,0:T(4,128)S(1)}, f32[3,4,128]{2,1,0:T(4,128)S(1)}, u32[]{:S(2)}, u32[]{:S(2)}) collective-permute-start(f32[3,4,128]{2,1,0:T(4,128)S(1)} %fusion.297), channel_id=1, source_target_pairs={{0,64},{16,80},{32,96},{48,112},{64,0},{80,16},{96,32},{112,48},{1... | collective-permute-start | bytes 18440 | tf_op jit(solution)/shard_map/ppermute | solution.py:54
  310.5 6.4 %collective-permute-start.27 = (f32[3,4,128]{2,1,0:T(4,128)S(1)}, f32[3,4,128]{2,1,0:T(4,128)S(1)}, u32[]{:S(2)}, u32[]{:S(2)}) collective-permute-start(f32[3,4,128]{2,1,0:T(4,128)S(1)} %add.463), channel_id=1, source_target_pairs={{0,128},{16,144},{32,160},{48,176},{64,192},{80,208},{96,224},{112... | collective-permute-start | bytes 18440 | tf_op jit(solution)/shard_map/ppermute | solution.py:54
  316.9 10.1 %collective-permute-start.28 = (f32[3,4,128]{2,1,0:T(4,128)S(1)}, f32[3,4,128]{2,1,0:T(4,128)S(1)}, u32[]{:S(2)}, u32[]{:S(2)}) collective-permute-start(f32[3,4,128]{2,1,0:T(4,128)S(1)} %add.464), channel_id=1, source_target_pairs={{0,256},{16,272},{32,288},{48,304},{64,320},{80,336},{96,352},{112... | collective-permute-start | bytes 18440 | tf_op jit(solution)/shard_map/ppermute | solution.py:54
  327.0 15.5 %collective-permute-start.29 = (f32[3,4,128]{2,1,0:T(4,128)S(1)}, f32[3,4,128]{2,1,0:T(4,128)S(1)}, u32[]{:S(2)}, u32[]{:S(2)}) collective-permute-start(f32[3,4,128]{2,1,0:T(4,128)S(1)} %add.465), channel_id=1, source_target_pairs={{0,512},{16,528},{32,544},{48,560},{64,576},{80,592},{96,608},{112... | collective-permute-start | bytes 18440 | tf_op jit(solution)/shard_map/ppermute | solution.py:54
  (23 other events, 14.6 us)
Sparse Core Ops, SparseCore 0:
  20.5 52.4 all-gather.1

commit v3 on v2

--- a/solution.py
+++ b/solution.py
@@ -47,12 +47,26 @@
 
 def summed(part, axis):
     count = lax.axis_size(axis)
-    if count & (count - 1):
-        return lax.psum(part, axis)
+    place = lax.axis_index(axis)
     distance = 1
     while distance < count:
-        part = part + lax.ppermute(part, axis, [(i, i ^ distance) for i in range(count)])
-        distance *= 2
+        radix = 4 if (count // distance) % 4 == 0 else 2
+        if (count // distance) % radix:
+            return lax.psum(part, axis)
+        digit = (place // distance) % radix
+        got = [part]
+        for shift in range(1, radix):
+            route = []
+            for i in range(count):
+                own = (i // distance) % radix
+                route.append((i + ((own + shift) % radix - own) * distance, i))
+            got.append(lax.ppermute(part, axis, route))
+        ordered = jnp.stack(got)[(jnp.arange(radix) - digit) % radix]
+        if radix == 4:
+            part = (ordered[0] + ordered[1]) + (ordered[2] + ordered[3])
+        else:
+            part = ordered[0] + ordered[1]
+        distance *= radix
     return part
 
 
@@ -79,63 +93,44 @@
 
 
 def block_step(state, block):
-    query_rows, key_rows, value_rows, rates = block
-    w_keys, w_values = wy_factors(key_rows, value_rows, rates)
+    query_rows, key_rows, w_keys, w_values, scores = block
     fresh = w_values - jnp.dot(w_keys, state, precision=HIGHEST)
-    scores = jnp.tril(jnp.dot(query_rows, key_rows.T, precision=HIGHEST))
     output = jnp.dot(query_rows, state, precision=HIGHEST) + jnp.dot(
         scores, fresh, precision=HIGHEST
     )
     return (state + jnp.dot(key_rows.T, fresh, precision=HIGHEST), output)
 
 
-def local_forward(ext_q, ext_k, ext_v, conv_three, logits, start_state):
+def prepare(ext_q, ext_k, ext_v, conv_three, logits):
     row_count = logits.shape[0]
-    queries = normed(conv_silu(ext_q, conv_three[0], row_count))
-    key_act = normed(conv_silu(ext_k, conv_three[1], row_count))
-    value_act = conv_silu(ext_v, conv_three[2], row_count)
-    rates = jax.nn.sigmoid(logits)
     blocks = row_count // BLOCK
-    shaped = (
-        queries.reshape(blocks, BLOCK, FEATURE_DIM),
-        key_act.reshape(blocks, BLOCK, FEATURE_DIM),
-        value_act.reshape(blocks, BLOCK, FEATURE_DIM),
-        rates.reshape(blocks, BLOCK),
-    )
-    final, outputs = lax.scan(block_step, start_state, shaped)
-    return (outputs.reshape(row_count, FEATURE_DIM), final)
-
-
-def transition(ext_k, ext_v, conv_three, logits):
-    row_count = logits.shape[0]
-    key_act = normed(conv_silu(ext_k, conv_three[1], row_count))
-    value_act = conv_silu(ext_v, conv_three[2], row_count)
-    rates = jax.nn.sigmoid(logits)
-    blocks = row_count // BLOCK
-    shaped = (
-        key_act.reshape(blocks, BLOCK, FEATURE_DIM),
-        value_act.reshape(blocks, BLOCK, FEATURE_DIM),
-        rates.reshape(blocks, BLOCK),
-    )
+    shape = (blocks, BLOCK, FEATURE_DIM)
+    queries = normed(conv_silu(ext_q, conv_three[0], row_count)).reshape(shape)
+    key_act = normed(conv_silu(ext_k, conv_three[1], row_count)).reshape(shape)
+    value_act = conv_silu(ext_v, conv_three[2], row_count).reshape(shape)
+    rates = jax.nn.sigmoid(logits).reshape(blocks, BLOCK)
+    w_keys, w_values = jax.vmap(wy_factors)(key_act, value_act, rates)
+    scores = jnp.tril(jnp.einsum("bif,bjf->bij", queries, key_act, precision=HIGHEST))
+    return (queries, key_act, w_keys, w_values, scores)
+
+
+def recur(prepared, start_state):
+    final, outputs = lax.scan(block_step, start_state, prepared, unroll=True)
+    return (outputs.reshape(-1, FEATURE_DIM), final)
+
+
+def transition(prepared):
+    _, key_act, w_keys, w_values, _ = prepared
     identity = jnp.eye(FEATURE_DIM, dtype=jnp.float32)
-
-    def advance(carry, block):
-        key_rows, value_rows, block_rates = block
-        w_keys, w_values = wy_factors(key_rows, value_rows, block_rates)
-        decay = identity - jnp.dot(key_rows.T, w_keys, precision=HIGHEST)
-        written = jnp.dot(key_rows.T, w_values, precision=HIGHEST)
-        return (
-            (
-                jnp.dot(decay, carry[0], precision=HIGHEST),
-                jnp.dot(decay, carry[1], precision=HIGHEST) + written,
-            ),
-            None,
+    decay = identity - jnp.einsum("bif,big->bfg", key_act, w_keys, precision=HIGHEST)
+    written = jnp.einsum("bif,big->bfg", key_act, w_values, precision=HIGHEST)
+    pair = (decay[0], written[0])
+    for block in range(1, decay.shape[0]):
+        pair = (
+            jnp.dot(decay[block], pair[0], precision=HIGHEST),
+            jnp.dot(decay[block], pair[1], precision=HIGHEST) + written[block],
         )
-
-    pairs, _ = lax.scan(
-        advance, (identity, jnp.zeros((FEATURE_DIM, FEATURE_DIM), jnp.float32)), shaped
-    )
-    return pairs
+    return pair
 
 
 def combine_pairs(earlier, later):
@@ -167,15 +162,18 @@
         preferred_element_type=jnp.float32,
     )
     out_cot = out_cot.reshape(row_count, head_count, FEATURE_DIM).transpose(1, 0, 2)
-    pairs = jax.vmap(transition)(ext_k, ext_v, conv_heads, beta_logit)
+    prepared, prepare_back = jax.vjp(
+        jax.vmap(prepare), ext_q, ext_k, ext_v, conv_heads, beta_logit
+    )
+    pairs = jax.vmap(transition)(prepared)
     identity = jnp.broadcast_to(
         jnp.eye(FEATURE_DIM, dtype=jnp.float32), (head_count, FEATURE_DIM, FEATURE_DIM)
     )
     zero_state = jnp.zeros((head_count, FEATURE_DIM, FEATURE_DIM), jnp.float32)
-    batched = jax.vmap(local_forward)
+    batched = jax.vmap(recur)
     adjoint_map = jnp.swapaxes(pairs[0], 1, 2)
-    _, seed_backward = jax.vjp(batched, ext_q, ext_k, ext_v, conv_heads, beta_logit, zero_state)
-    local_seed = seed_backward((out_cot, zero_state))[5]
+    _, seed_backward = jax.vjp(lambda state: batched(prepared, state), zero_state)
+    local_seed = seed_backward((out_cot, zero_state))[0]
     carried, suffix = carried_in(
         [pairs, (adjoint_map, local_seed)],
         "ctx",
@@ -183,9 +181,8 @@
         (identity, zero_state),
         [False, True],
     )
-    start_state = carried[1]
-    _, backward = jax.vjp(batched, ext_q, ext_k, ext_v, conv_heads, beta_logit, start_state)
-    grads = backward((out_cot, suffix[1]))
+    _, backward = jax.vjp(batched, prepared, carried[1])
+    grads = prepare_back(backward((out_cot, suffix[1]))[0])
     rim_back = passed_along(
         (grads[0][:, :margin], grads[1][:, :margin], grads[2][:, :margin]), "ctx", -1
     )

time: 354 us -> 274 us (0.77)
  other arithmetic: 93 us -> 26.7 us
  waiting for transfers between devices: 22 us -> 65.5 us
  matrix products: 72.2 us -> 32.2 us
  local copies, waits for them, and re-layouts: 19.1 us -> 5.51 us
    ppermute x24, waiting for transfers between devices: 8.84 us -> 57.2 us  [passed_along(): return lax.ppermute(block, axis, route)]
    another operation x26 -> x5, other arithmetic: 42.9 us -> 0.14 us  [the longest x24 42.9 us: wy_factors(): jax.scipy.linalg.solve_triangular(system, value_rows * rates[:, None], lo...]
    another operation x16 -> x3, other arithmetic: 39.2 us -> 19.7 us  [wy_factors(): jax.scipy.linalg.solve_triangular(system, weighted, lower=True, unit_diag...]
    unnamed x114 -> x12, local copies, waits for them, and re-layouts: 13.5 us -> 0.85 us
    dot_general x30, matrix products: 13.5 us -> 6.22 us  [combine_pairs(): offset_term = jnp.matmul(later[0], earlier[1], precision=HIGHEST) + later[1]]
    dot_general x20 -> x3, matrix products: 7.92 us -> 1.08 us  [wy_factors(): strict = jnp.tril(jnp.dot(weighted, key_rows.T, precision=HIGHEST), -1)]
    dot_general x30, matrix products: 12.6 us -> 6.2 us  [combine_pairs(): product = jnp.matmul(later[0], earlier[0], precision=HIGHEST)]
    dot_general x32 -> x11, matrix products: 9.89 us -> 3.61 us  [the longest x3 1 us: prepare(): jnp.einsum('bif,bjf->bij', queries, key_act, precision=HIGHEST)]
  transfers between devices with their start and end apart: 31 -> 34, of which waited for: 10 -> 16; matrix products, arithmetic and copies ran while one was open for 35% -> 16% of each run, Pallas kernels for 0% -> 0%
where the time goes in v3:
time: 274 us; the launch traced here: 270 us
  starting transfers between devices  124 us (45%)
  waiting for transfers between devices  65.5 us (24%)
  matrix products  32.2 us (12%)
  other arithmetic  26.7 us (10%)
  between operations  16 us (6%)
  local copies, waits for them, and re-layouts  5.51 us (2%)
    ppermute x24, starting transfers between devices, passed_along(): return lax.ppermute(block, axis, route)  93.3 us
    ppermute x24, waiting for transfers between devices, passed_along(): return lax.ppermute(block, axis, route)  57.2 us
    ppermute x9, starting transfers between devices, summed(): got.append(lax.ppermute(part, axis, route))  31 us
    another operation x3, other arithmetic, wy_factors(): jax.scipy.linalg.solve_triangular(system, weighted, lower=True, unit_diag...  19.7 us
    ppermute x9, waiting for transfers between devices, summed(): got.append(lax.ppermute(part, axis, route))  8.27 us
    dot_general x30, matrix products, combine_pairs(): offset_term = jnp.matmul(later[0], earlier[1], precision=HIGHEST) + later[1]  6.22 us
    dot_general x30, matrix products, combine_pairs(): product = jnp.matmul(later[0], earlier[0], precision=HIGHEST)  6.2 us
  transfers between devices with their start and end apart: 34, of which 16 were waited for; matrix products, arithmetic and copies ran while one was open for 16% of the time, Pallas kernels for 0%

profile of v3, /device:TPU:6, one launch (start us, length us, event | category | flops | bytes accessed | tf_op | source)
XLA Modules:
  0.0 270.3 jit_solution(3625094477856745837)
XLA Ops:
  7.2 0.7 slice.704
  8.0 4.2 %collective-permute-start.11 = (bf16[3,128]{1,0:T(4,128)(2,1)S(1)}, bf16[3,128]{1,0:T(4,128)(2,1)S(1)}, u32[]{:S(2)}, u32[]{:S(2)}) collective-permute-start(bf16[3,128]{1,0:T(4,128)(2,1)S(1)} %slice.704), channel_id=1, source_target_pairs={{0,16},{16,32},{32,48},{48,64},{64,80},{80,96},{96,112},{112,128},... | collective-permute-start | bytes 2312 | tf_op jit(solution)/shard_map/ppermute | solution.py:19
  12.2 0.7 slice.618
  12.8 3.4 %collective-permute-start = (bf16[3,128]{1,0:T(4,128)(2,1)S(1)}, bf16[3,128]{1,0:T(4,128)(2,1)S(1)}, u32[]{:S(2)}, u32[]{:S(2)}) collective-permute-start(bf16[3,128]{1,0:T(4,128)(2,1)S(1)} %slice.618), channel_id=1, source_target_pairs={{0,16},{16,32},{32,48},{48,64},{64,80},{80,96},{96,112},{112,128},... | collective-permute-start | bytes 2312 | tf_op jit(solution)/shard_map/ppermute | solution.py:19
  16.2 0.7 slice.632
  16.9 3.4 %collective-permute-start.1 = (bf16[3,128]{1,0:T(4,128)(2,1)S(1)}, bf16[3,128]{1,0:T(4,128)(2,1)S(1)}, u32[]{:S(2)}, u32[]{:S(2)}) collective-permute-start(bf16[3,128]{1,0:T(4,128)(2,1)S(1)} %slice.632), channel_id=1, source_target_pairs={{0,16},{16,32},{32,48},{48,64},{64,80},{80,96},{96,112},{112,128},... | collective-permute-start | bytes 2312 | tf_op jit(solution)/shard_map/ppermute | solution.py:19
  20.5 0.7 copy-done.4
  21.4 0.5 broadcast.684
  22.1 0.7 fusion.176
  23.6 19.7 %custom-call.10 = f32[1,4,1,64,64]{3,4,2,1,0:T(8,128)S(1)} custom-call(f32[1,4,1,64,64]{4,3,2,1,0:T(8,128)S(1)} %fusion.16), custom_call_target="InvertDiagBlocksLowerTriangular" | custom-call | tf_op jit(solution)/shard_map/jvp(vmap(vmap(jit(_solve_triangular))))/triangular_solve | solution.py:88
  43.9 0.6 convolution_bitcast_fusion
  44.9 0.6 fusion
  47.1 3.1 %collective-permute-start.2 = (f32[2,1,128,128]{2,3,1,0:T(8,128)S(1)}, f32[2,1,128,128]{2,3,1,0:T(8,128)S(1)}, u32[]{:S(2)}, u32[]{:S(2)}) collective-permute-start(f32[2,1,128,128]{2,3,1,0:T(8,128)S(1)} %pad_maximum_fusion), channel_id=1, source_target_pairs={{0,16},{16,32},{32,48},{48,64},{64,80},{80,96},{96,112},{112,128},... | collective-permute-start | bytes 393224 | tf_op jit(solution)/shard_map/ppermute | solution.py:19
  50.2 5.1 %collective-permute-start.3 = (f32[2,1,128,128]{2,3,1,0:T(8,128)S(1)}, f32[2,1,128,128]{2,3,1,0:T(8,128)S(1)}, u32[]{:S(2)}, u32[]{:S(2)}) collective-permute-start(f32[2,1,128,128]{2,3,1,0:T(8,128)S(1)} %pad_maximum_fusion), channel_id=1, source_target_pairs={{0,32},{16,48},{32,64},{48,80},{64,96},{80,112},{96,128},{112,144}... | collective-permute-start | bytes 393224 | tf_op jit(solution)/shard_map/ppermute | solution.py:19
  55.4 3.7 %collective-permute-start.4 = (f32[2,1,128,128]{2,3,1,0:T(8,128)S(1)}, f32[2,1,128,128]{2,3,1,0:T(8,128)S(1)}, u32[]{:S(2)}, u32[]{:S(2)}) collective-permute-start(f32[2,1,128,128]{2,3,1,0:T(8,128)S(1)} %pad_maximum_fusion), channel_id=1, source_target_pairs={{0,48},{16,64},{32,80},{48,96},{64,112},{80,128},{96,144},{112,160... | collective-permute-start | bytes 393224 | tf_op jit(solution)/shard_map/ppermute | solution.py:19
  60.2 3.2 %collective-permute-done.4 = f32[2,1,128,128]{2,3,1,0:T(8,128)S(1)} collective-permute-done((f32[2,1,128,128]{2,3,1,0:T(8,128)S(1)}, f32[2,1,128,128]{2,3,1,0:T(8,128)S(1)}, u32[]{:S(2)}, u32[]{:S(2)}) %collective-permute-start.4) | collective-permute-done | bytes 131104 | tf_op jit(solution)/shard_map/ppermute | solution.py:19
  63.9 4.3 %collective-permute-start.5 = (f32[2,1,128,128]{2,3,1,0:T(8,128)S(1)}, f32[2,1,128,128]{2,3,1,0:T(8,128)S(1)}, u32[]{:S(2)}, u32[]{:S(2)}) collective-permute-start(f32[2,1,128,128]{2,3,1,0:T(8,128)S(1)} %maximum_select_fusion.4), channel_id=1, source_target_pairs={{0,64},{16,80},{32,96},{48,112},{64,128},{80,144},{96,160},{112,17... | collective-permute-start | bytes 393224 | tf_op jit(solution)/shard_map/ppermute | solution.py:19
  68.2 7.3 %collective-permute-start.6 = (f32[2,1,128,128]{2,3,1,0:T(8,128)S(1)}, f32[2,1,128,128]{2,3,1,0:T(8,128)S(1)}, u32[]{:S(2)}, u32[]{:S(2)}) collective-permute-start(f32[2,1,128,128]{2,3,1,0:T(8,128)S(1)} %maximum_select_fusion.4), channel_id=1, source_target_pairs={{0,128},{16,144},{32,160},{48,176},{64,192},{80,208},{96,224},{112... | collective-permute-start | bytes 393224 | tf_op jit(solution)/shard_map/ppermute | solution.py:19
  75.5 9.1 %collective-permute-start.7 = (f32[2,1,128,128]{2,3,1,0:T(8,128)S(1)}, f32[2,1,128,128]{2,3,1,0:T(8,128)S(1)}, u32[]{:S(2)}, u32[]{:S(2)}) collective-permute-start(f32[2,1,128,128]{2,3,1,0:T(8,128)S(1)} %maximum_select_fusion.4), channel_id=1, source_target_pairs={{0,192},{16,208},{32,224},{48,240},{64,256},{80,272},{96,288},{112... | collective-permute-start | bytes 393224 | tf_op jit(solution)/shard_map/ppermute | solution.py:19
  87.6 15.4 %collective-permute-start.10 = (f32[2,1,128,128]{2,3,1,0:T(8,128)S(1)}, f32[2,1,128,128]{2,3,1,0:T(8,128)S(1)}, u32[]{:S(2)}, u32[]{:S(2)}) collective-permute-start(f32[2,1,128,128]{2,3,1,0:T(8,128)S(1)} %maximum_select_fusion.10), channel_id=1, source_target_pairs={{0,768},{16,784},{32,800},{48,816},{64,832},{80,848},{96,864},{112... | collective-permute-start | bytes 393224 | tf_op jit(solution)/shard_map/ppermute | solution.py:19
  103.0 1.3 collective-permute-start.8
  104.3 7.5 %collective-permute-start.9 = (f32[2,1,128,128]{2,3,1,0:T(8,128)S(1)}, f32[2,1,128,128]{2,3,1,0:T(8,128)S(1)}, u32[]{:S(2)}, u32[]{:S(2)}) collective-permute-start(f32[2,1,128,128]{2,3,1,0:T(8,128)S(1)} %maximum_select_fusion.10), channel_id=1, source_target_pairs={{0,512},{16,528},{32,544},{48,560},{64,576},{80,592},{96,608},{112... | collective-permute-start | bytes 393224 | tf_op jit(solution)/shard_map/ppermute | solution.py:19
  114.5 5.7 %collective-permute-done.10 = f32[2,1,128,128]{2,3,1,0:T(8,128)S(1)} collective-permute-done((f32[2,1,128,128]{2,3,1,0:T(8,128)S(1)}, f32[2,1,128,128]{2,3,1,0:T(8,128)S(1)}, u32[]{:S(2)}, u32[]{:S(2)}) %collective-permute-start.10) | collective-permute-done | bytes 131104 | tf_op jit(solution)/shard_map/ppermute | solution.py:19
  122.6 1.7 fusion.177
  131.1 1.9 collective-permute-start.13
  133.1 4.0 %collective-permute-start.14 = (f32[2,1,128,128]{2,3,1,0:T(8,128)S(1)}, f32[2,1,128,128]{2,3,1,0:T(8,128)S(1)}, u32[]{:S(2)}, u32[]{:S(2)}) collective-permute-start(f32[2,1,128,128]{2,3,1,0:T(8,128)S(1)} %pad_maximum_fusion.1), channel_id=1, source_target_pairs={{32,0},{48,16},{64,32},{80,48},{96,64},{112,80},{128,96},{144,112}... | collective-permute-start | bytes 393224 | tf_op jit(solution)/shard_map/ppermute | solution.py:19
  137.0 1.9 collective-permute-start.15
  139.0 1.9 collective-permute-start.12
  140.9 5.6 %collective-permute-done.12 = f32[1,3,128]{2,1,0:T(4,128)S(1)} collective-permute-done((f32[1,3,128]{2,1,0:T(4,128)S(1)}, f32[1,3,128]{2,1,0:T(4,128)S(1)}, u32[]{:S(2)}, u32[]{:S(2)}) %collective-permute-start.12) | collective-permute-done | bytes 1568 | tf_op jit(solution)/shard_map/ppermute | solution.py:19
  146.6 0.7 maximum_bitcast_fusion.2
  148.6 1.3 collective-permute-start.16
  149.9 1.3 collective-permute-start.17
  151.2 1.3 collective-permute-start.18
  153.9 3.5 %collective-permute-done.16 = f32[2,1,128,128]{2,3,1,0:T(8,128)S(1)} collective-permute-done((f32[2,1,128,128]{2,3,1,0:T(8,128)S(1)}, f32[2,1,128,128]{2,3,1,0:T(8,128)S(1)}, u32[]{:S(2)}, u32[]{:S(2)}) %collective-permute-start.16) | collective-permute-done | bytes 131104 | tf_op jit(solution)/shard_map/ppermute | solution.py:19
  157.8 3.9 %collective-permute-done.17 = f32[2,1,128,128]{2,3,1,0:T(8,128)S(1)} collective-permute-done((f32[2,1,128,128]{2,3,1,0:T(8,128)S(1)}, f32[2,1,128,128]{2,3,1,0:T(8,128)S(1)}, u32[]{:S(2)}, u32[]{:S(2)}) %collective-permute-start.17) | collective-permute-done | bytes 131104 | tf_op jit(solution)/shard_map/ppermute | solution.py:19
  162.2 7.7 %collective-permute-done.18 = f32[2,1,128,128]{2,3,1,0:T(8,128)S(1)} collective-permute-done((f32[2,1,128,128]{2,3,1,0:T(8,128)S(1)}, f32[2,1,128,128]{2,3,1,0:T(8,128)S(1)}, u32[]{:S(2)}, u32[]{:S(2)}) %collective-permute-start.18) | collective-permute-done | bytes 131104 | tf_op jit(solution)/shard_map/ppermute | solution.py:19
  170.3 1.3 collective-permute-start.21
  171.6 1.3 collective-permute-start.19
  172.9 1.5 collective-permute-start.20
  175.9 8.8 %collective-permute-done.19 = f32[2,1,128,128]{2,3,1,0:T(8,128)S(1)} collective-permute-done((f32[2,1,128,128]{2,3,1,0:T(8,128)S(1)}, f32[2,1,128,128]{2,3,1,0:T(8,128)S(1)}, u32[]{:S(2)}, u32[]{:S(2)}) %collective-permute-start.19) | collective-permute-done | bytes 131104 | tf_op jit(solution)/shard_map/ppermute | solution.py:19
  185.2 3.6 %collective-permute-done.20 = f32[2,1,128,128]{2,3,1,0:T(8,128)S(1)} collective-permute-done((f32[2,1,128,128]{2,3,1,0:T(8,128)S(1)}, f32[2,1,128,128]{2,3,1,0:T(8,128)S(1)}, u32[]{:S(2)}, u32[]{:S(2)}) %collective-permute-start.20) | collective-permute-done | bytes 131104 | tf_op jit(solution)/shard_map/ppermute | solution.py:19
  196.8 1.9 collective-permute-start.26
  198.7 2.2 collective-permute-start.25
  200.9 3.7 %collective-permute-start.24 = (f32[3,4,128]{2,1,0:T(4,128)S(1)}, f32[3,4,128]{2,1,0:T(4,128)S(1)}, u32[]{:S(2)}, u32[]{:S(2)}) collective-permute-start(f32[3,4,128]{2,1,0:T(4,128)S(1)} %get-tuple-element.61), channel_id=1, source_target_pairs={{16,0},{32,16},{48,32},{0,48},{80,64},{96,80},{112,96},{64,112},{1... | collective-permute-start | bytes 18440 | tf_op jit(solution)/shard_map/ppermute | solution.py:63
  204.6 3.4 %collective-permute-start.22 = (f32[1,3,128]{2,1,0:T(4,128)S(1)}, f32[1,3,128]{2,1,0:T(4,128)S(1)}, u32[]{:S(2)}, u32[]{:S(2)}) collective-permute-start(f32[1,3,128]{2,1,0:T(4,128)S(1)} %pad_add_fusion.5), channel_id=1, source_target_pairs={{16,0},{32,16},{48,32},{64,48},{80,64},{96,80},{112,96},{128,112},... | collective-permute-start | bytes 4616 | tf_op jit(solution)/shard_map/ppermute | solution.py:19
  208.0 4.5 %collective-permute-start.23 = (f32[1,3,128]{2,1,0:T(4,128)S(1)}, f32[1,3,128]{2,1,0:T(4,128)S(1)}, u32[]{:S(2)}, u32[]{:S(2)}) collective-permute-start(f32[1,3,128]{2,1,0:T(4,128)S(1)} %pad_add_fusion.4), channel_id=1, source_target_pairs={{16,0},{32,16},{48,32},{64,48},{80,64},{96,80},{112,96},{128,112},... | collective-permute-start | bytes 4616 | tf_op jit(solution)/shard_map/ppermute | solution.py:19
  212.7 0.6 fusion.157
  213.3 13.4 %collective-permute-done.22 = f32[1,3,128]{2,1,0:T(4,128)S(1)} collective-permute-done((f32[1,3,128]{2,1,0:T(4,128)S(1)}, f32[1,3,128]{2,1,0:T(4,128)S(1)}, u32[]{:S(2)}, u32[]{:S(2)}) %collective-permute-start.22) | collective-permute-done | bytes 1568 | tf_op jit(solution)/shard_map/ppermute | solution.py:19
  226.8 0.7 maximum_bitcast_fusion.6
  227.4 1.3 collective-permute-done.23
  228.8 0.7 maximum_bitcast_fusion.7
  229.5 0.6 gather_fusion
  230.1 5.4 %collective-permute-start.29 = (f32[3,4,128]{2,1,0:T(4,128)S(1)}, f32[3,4,128]{2,1,0:T(4,128)S(1)}, u32[]{:S(2)}, u32[]{:S(2)}) collective-permute-start(f32[3,4,128]{2,1,0:T(4,128)S(1)} %fusion.231), channel_id=1, source_target_pairs={{192,0},{208,16},{224,32},{240,48},{0,64},{16,80},{32,96},{48,112}... | collective-permute-start | bytes 18440 | tf_op jit(solution)/shard_map/ppermute | solution.py:63
  235.4 2.0 collective-permute-start.28
  237.5 4.2 %collective-permute-start.27 = (f32[3,4,128]{2,1,0:T(4,128)S(1)}, f32[3,4,128]{2,1,0:T(4,128)S(1)}, u32[]{:S(2)}, u32[]{:S(2)}) collective-permute-start(f32[3,4,128]{2,1,0:T(4,128)S(1)} %fusion.231), channel_id=1, source_target_pairs={{64,0},{80,16},{96,32},{112,48},{128,64},{144,80},{160,96},{176,11... | collective-permute-start | bytes 18440 | tf_op jit(solution)/shard_map/ppermute | solution.py:63
  241.9 1.1 collective-permute-done.27
  243.0 0.6 gather_fusion.1
  243.6 1.9 collective-permute-start.32
  245.5 1.9 collective-permute-start.31
  247.4 7.8 %collective-permute-start.30 = (f32[3,4,128]{2,1,0:T(4,128)S(1)}, f32[3,4,128]{2,1,0:T(4,128)S(1)}, u32[]{:S(2)}, u32[]{:S(2)}) collective-permute-start(f32[3,4,128]{2,1,0:T(4,128)S(1)} %fusion.230), channel_id=1, source_target_pairs={{256,0},{272,16},{288,32},{304,48},{320,64},{336,80},{352,96},{368... | collective-permute-start | bytes 18440 | tf_op jit(solution)/shard_map/ppermute | solution.py:63
  255.3 4.4 %collective-permute-done.31 = f32[3,4,128]{2,1,0:T(4,128)S(1)} collective-permute-done((f32[3,4,128]{2,1,0:T(4,128)S(1)}, f32[3,4,128]{2,1,0:T(4,128)S(1)}, u32[]{:S(2)}, u32[]{:S(2)}) %collective-permute-start.31) | collective-permute-done | bytes 6176 | tf_op jit(solution)/shard_map/ppermute | solution.py:63
  259.8 2.5 collective-permute-done.30
  262.2 0.6 gather_fusion.2
  262.8 0.6 fusion.154
  (252 shorter events, 33.9 us)
Async XLA Ops:
  7.2 115.4 %copy-start = (bf16[128,2048]{1,0:T(8,128)(2,1)S(1)}, bf16[128,2048]{1,0:T(8,128)(2,1)}, u32[]{:S(2)}) copy-start(bf16[128,2048]{1,0:T(8,128)(2,1)} %param.18) | copy-start | bytes 1572868
  7.2 115.4 %all-gather.2.cloned.1.call-start = ((), (), s32[]{:S(2)}) async-start(), calls=%async_computation | async-start | bytes 1114112 | tf_op jit(solution)/shard_map/all_gather | solution.py:159
  8.0 51.2 %collective-permute-start.11 = (bf16[3,128]{1,0:T(4,128)(2,1)S(1)}, bf16[3,128]{1,0:T(4,128)(2,1)S(1)}, u32[]{:S(2)}, u32[]{:S(2)}) collective-permute-start(bf16[3,128]{1,0:T(4,128)(2,1)S(1)} %slice.704), channel_id=1, source_target_pairs={{0,16},{16,32},{32,48},{48,64},{64,80},{80,96},{96,112},{112,128},... | collective-permute-start | bytes 2312 | tf_op jit(solution)/shard_map/ppermute | solution.py:19
  12.8 10.0 %collective-permute-start = (bf16[3,128]{1,0:T(4,128)(2,1)S(1)}, bf16[3,128]{1,0:T(4,128)(2,1)S(1)}, u32[]{:S(2)}, u32[]{:S(2)}) collective-permute-start(bf16[3,128]{1,0:T(4,128)(2,1)S(1)} %slice.618), channel_id=1, source_target_pairs={{0,16},{16,32},{32,48},{48,64},{64,80},{80,96},{96,112},{112,128},... | collective-permute-start | bytes 2312 | tf_op jit(solution)/shard_map/ppermute | solution.py:19
  16.9 26.4 %collective-permute-start.1 = (bf16[3,128]{1,0:T(4,128)(2,1)S(1)}, bf16[3,128]{1,0:T(4,128)(2,1)S(1)}, u32[]{:S(2)}, u32[]{:S(2)}) collective-permute-start(bf16[3,128]{1,0:T(4,128)(2,1)S(1)} %slice.632), channel_id=1, source_target_pairs={{0,16},{16,32},{32,48},{48,64},{64,80},{80,96},{96,112},{112,128},... | collective-permute-start | bytes 2312 | tf_op jit(solution)/shard_map/ppermute | solution.py:19
  20.5 0.7 copy-start.4
  20.5 2.4 copy-start.1
  21.4 0.7 copy-start.5
  23.2 20.1 %copy-start.2 = (bf16[256,128]{1,0:T(8,128)(2,1)S(1)}, bf16[256,128]{1,0:T(8,128)(2,1)}, u32[]{:S(2)}) copy-start(bf16[256,128]{1,0:T(8,128)(2,1)} %param.15) | copy-start | bytes 196612
  47.1 12.1 %copy-start.3 = (bf16[256,128]{1,0:T(8,128)(2,1)S(1)}, bf16[256,128]{1,0:T(8,128)(2,1)}, u32[]{:S(2)}) copy-start(bf16[256,128]{1,0:T(8,128)(2,1)} %param.13) | copy-start | bytes 196612
  47.1 12.1 %collective-permute-start.2 = (f32[2,1,128,128]{2,3,1,0:T(8,128)S(1)}, f32[2,1,128,128]{2,3,1,0:T(8,128)S(1)}, u32[]{:S(2)}, u32[]{:S(2)}) collective-permute-start(f32[2,1,128,128]{2,3,1,0:T(8,128)S(1)} %pad_maximum_fusion), channel_id=1, source_target_pairs={{0,16},{16,32},{32,48},{48,64},{64,80},{80,96},{96,112},{112,128},... | collective-permute-start | bytes 393224 | tf_op jit(solution)/shard_map/ppermute | solution.py:19
  50.2 9.5 %collective-permute-start.3 = (f32[2,1,128,128]{2,3,1,0:T(8,128)S(1)}, f32[2,1,128,128]{2,3,1,0:T(8,128)S(1)}, u32[]{:S(2)}, u32[]{:S(2)}) collective-permute-start(f32[2,1,128,128]{2,3,1,0:T(8,128)S(1)} %pad_maximum_fusion), channel_id=1, source_target_pairs={{0,32},{16,48},{32,64},{48,80},{64,96},{80,112},{96,128},{112,144}... | collective-permute-start | bytes 393224 | tf_op jit(solution)/shard_map/ppermute | solution.py:19
  55.4 8.1 %collective-permute-start.4 = (f32[2,1,128,128]{2,3,1,0:T(8,128)S(1)}, f32[2,1,128,128]{2,3,1,0:T(8,128)S(1)}, u32[]{:S(2)}, u32[]{:S(2)}) collective-permute-start(f32[2,1,128,128]{2,3,1,0:T(8,128)S(1)} %pad_maximum_fusion), channel_id=1, source_target_pairs={{0,48},{16,64},{32,80},{48,96},{64,112},{80,128},{96,144},{112,160... | collective-permute-start | bytes 393224 | tf_op jit(solution)/shard_map/ppermute | solution.py:19
  63.9 22.1 %collective-permute-start.5 = (f32[2,1,128,128]{2,3,1,0:T(8,128)S(1)}, f32[2,1,128,128]{2,3,1,0:T(8,128)S(1)}, u32[]{:S(2)}, u32[]{:S(2)}) collective-permute-start(f32[2,1,128,128]{2,3,1,0:T(8,128)S(1)} %maximum_select_fusion.4), channel_id=1, source_target_pairs={{0,64},{16,80},{32,96},{48,112},{64,128},{80,144},{96,160},{112,17... | collective-permute-start | bytes 393224 | tf_op jit(solution)/shard_map/ppermute | solution.py:19
  68.2 18.3 %collective-permute-start.6 = (f32[2,1,128,128]{2,3,1,0:T(8,128)S(1)}, f32[2,1,128,128]{2,3,1,0:T(8,128)S(1)}, u32[]{:S(2)}, u32[]{:S(2)}) collective-permute-start(f32[2,1,128,128]{2,3,1,0:T(8,128)S(1)} %maximum_select_fusion.4), channel_id=1, source_target_pairs={{0,128},{16,144},{32,160},{48,176},{64,192},{80,208},{96,224},{112... | collective-permute-start | bytes 393224 | tf_op jit(solution)/shard_map/ppermute | solution.py:19
  75.5 11.6 %collective-permute-start.7 = (f32[2,1,128,128]{2,3,1,0:T(8,128)S(1)}, f32[2,1,128,128]{2,3,1,0:T(8,128)S(1)}, u32[]{:S(2)}, u32[]{:S(2)}) collective-permute-start(f32[2,1,128,128]{2,3,1,0:T(8,128)S(1)} %maximum_select_fusion.4), channel_id=1, source_target_pairs={{0,192},{16,208},{32,224},{48,240},{64,256},{80,272},{96,288},{112... | collective-permute-start | bytes 393224 | tf_op jit(solution)/shard_map/ppermute | solution.py:19
  87.6 32.6 %collective-permute-start.10 = (f32[2,1,128,128]{2,3,1,0:T(8,128)S(1)}, f32[2,1,128,128]{2,3,1,0:T(8,128)S(1)}, u32[]{:S(2)}, u32[]{:S(2)}) collective-permute-start(f32[2,1,128,128]{2,3,1,0:T(8,128)S(1)} %maximum_select_fusion.10), channel_id=1, source_target_pairs={{0,768},{16,784},{32,800},{48,816},{64,832},{80,848},{96,864},{112... | collective-permute-start | bytes 393224 | tf_op jit(solution)/shard_map/ppermute | solution.py:19
  103.0 10.2 %collective-permute-start.8 = (f32[2,1,128,128]{2,3,1,0:T(8,128)S(1)}, f32[2,1,128,128]{2,3,1,0:T(8,128)S(1)}, u32[]{:S(2)}, u32[]{:S(2)}) collective-permute-start(f32[2,1,128,128]{2,3,1,0:T(8,128)S(1)} %maximum_select_fusion.10), channel_id=1, source_target_pairs={{0,256},{16,272},{32,288},{48,304},{64,320},{80,336},{96,352},{112... | collective-permute-start | bytes 393224 | tf_op jit(solution)/shard_map/ppermute | solution.py:19
  104.3 9.8 %collective-permute-start.9 = (f32[2,1,128,128]{2,3,1,0:T(8,128)S(1)}, f32[2,1,128,128]{2,3,1,0:T(8,128)S(1)}, u32[]{:S(2)}, u32[]{:S(2)}) collective-permute-start(f32[2,1,128,128]{2,3,1,0:T(8,128)S(1)} %maximum_select_fusion.10), channel_id=1, source_target_pairs={{0,512},{16,528},{32,544},{48,560},{64,576},{80,592},{96,608},{112... | collective-permute-start | bytes 393224 | tf_op jit(solution)/shard_map/ppermute | solution.py:19
  131.1 16.1 %collective-permute-start.13 = (f32[2,1,128,128]{2,3,1,0:T(8,128)S(1)}, f32[2,1,128,128]{2,3,1,0:T(8,128)S(1)}, u32[]{:S(2)}, u32[]{:S(2)}) collective-permute-start(f32[2,1,128,128]{2,3,1,0:T(8,128)S(1)} %pad_maximum_fusion.1), channel_id=1, source_target_pairs={{16,0},{32,16},{48,32},{64,48},{80,64},{96,80},{112,96},{128,112},... | collective-permute-start | bytes 393224 | tf_op jit(solution)/shard_map/ppermute | solution.py:19
  133.1 14.6 %collective-permute-start.14 = (f32[2,1,128,128]{2,3,1,0:T(8,128)S(1)}, f32[2,1,128,128]{2,3,1,0:T(8,128)S(1)}, u32[]{:S(2)}, u32[]{:S(2)}) collective-permute-start(f32[2,1,128,128]{2,3,1,0:T(8,128)S(1)} %pad_maximum_fusion.1), channel_id=1, source_target_pairs={{32,0},{48,16},{64,32},{80,48},{96,64},{112,80},{128,96},{144,112}... | collective-permute-start | bytes 393224 | tf_op jit(solution)/shard_map/ppermute | solution.py:19
  137.0 11.1 %collective-permute-start.15 = (f32[2,1,128,128]{2,3,1,0:T(8,128)S(1)}, f32[2,1,128,128]{2,3,1,0:T(8,128)S(1)}, u32[]{:S(2)}, u32[]{:S(2)}) collective-permute-start(f32[2,1,128,128]{2,3,1,0:T(8,128)S(1)} %pad_maximum_fusion.1), channel_id=1, source_target_pairs={{48,0},{64,16},{80,32},{96,48},{112,64},{128,80},{144,96},{160,112... | collective-permute-start | bytes 393224 | tf_op jit(solution)/shard_map/ppermute | solution.py:19
  139.0 7.6 %collective-permute-start.12 = (f32[1,3,128]{2,1,0:T(4,128)S(1)}, f32[1,3,128]{2,1,0:T(4,128)S(1)}, u32[]{:S(2)}, u32[]{:S(2)}) collective-permute-start(f32[1,3,128]{2,1,0:T(4,128)S(1)} %pad_add_fusion.6), channel_id=1, source_target_pairs={{16,0},{32,16},{48,32},{64,48},{80,64},{96,80},{112,96},{128,112},... | collective-permute-start | bytes 4616 | tf_op jit(solution)/shard_map/ppermute | solution.py:19
  148.6 8.7 %collective-permute-start.16 = (f32[2,1,128,128]{2,3,1,0:T(8,128)S(1)}, f32[2,1,128,128]{2,3,1,0:T(8,128)S(1)}, u32[]{:S(2)}, u32[]{:S(2)}) collective-permute-start(f32[2,1,128,128]{2,3,1,0:T(8,128)S(1)} %maximum_select_fusion.17), channel_id=1, source_target_pairs={{64,0},{80,16},{96,32},{112,48},{128,64},{144,80},{160,96},{176,11... | collective-permute-start | bytes 393224 | tf_op jit(solution)/shard_map/ppermute | solution.py:19
  149.9 11.8 %collective-permute-start.17 = (f32[2,1,128,128]{2,3,1,0:T(8,128)S(1)}, f32[2,1,128,128]{2,3,1,0:T(8,128)S(1)}, u32[]{:S(2)}, u32[]{:S(2)}) collective-permute-start(f32[2,1,128,128]{2,3,1,0:T(8,128)S(1)} %maximum_select_fusion.17), channel_id=1, source_target_pairs={{128,0},{144,16},{160,32},{176,48},{192,64},{208,80},{224,96},{240... | collective-permute-start | bytes 393224 | tf_op jit(solution)/shard_map/ppermute | solution.py:19
  151.2 18.6 %collective-permute-start.18 = (f32[2,1,128,128]{2,3,1,0:T(8,128)S(1)}, f32[2,1,128,128]{2,3,1,0:T(8,128)S(1)}, u32[]{:S(2)}, u32[]{:S(2)}) collective-permute-start(f32[2,1,128,128]{2,3,1,0:T(8,128)S(1)} %maximum_select_fusion.17), channel_id=1, source_target_pairs={{192,0},{208,16},{224,32},{240,48},{256,64},{272,80},{288,96},{304... | collective-permute-start | bytes 393224 | tf_op jit(solution)/shard_map/ppermute | solution.py:19
  170.3 18.9 %collective-permute-start.21 = (f32[2,1,128,128]{2,3,1,0:T(8,128)S(1)}, f32[2,1,128,128]{2,3,1,0:T(8,128)S(1)}, u32[]{:S(2)}, u32[]{:S(2)}) collective-permute-start(f32[2,1,128,128]{2,3,1,0:T(8,128)S(1)} %maximum_select_fusion.23), channel_id=1, source_target_pairs={{768,0},{784,16},{800,32},{816,48},{832,64},{848,80},{864,96},{880... | collective-permute-start | bytes 393224 | tf_op jit(solution)/shard_map/ppermute | solution.py:19
  171.6 13.1 %collective-permute-start.19 = (f32[2,1,128,128]{2,3,1,0:T(8,128)S(1)}, f32[2,1,128,128]{2,3,1,0:T(8,128)S(1)}, u32[]{:S(2)}, u32[]{:S(2)}) collective-permute-start(f32[2,1,128,128]{2,3,1,0:T(8,128)S(1)} %maximum_select_fusion.23), channel_id=1, source_target_pairs={{256,0},{272,16},{288,32},{304,48},{320,64},{336,80},{352,96},{368... | collective-permute-start | bytes 393224 | tf_op jit(solution)/shard_map/ppermute | solution.py:19
  172.9 15.9 %collective-permute-start.20 = (f32[2,1,128,128]{2,3,1,0:T(8,128)S(1)}, f32[2,1,128,128]{2,3,1,0:T(8,128)S(1)}, u32[]{:S(2)}, u32[]{:S(2)}) collective-permute-start(f32[2,1,128,128]{2,3,1,0:T(8,128)S(1)} %maximum_select_fusion.23), channel_id=1, source_target_pairs={{512,0},{528,16},{544,32},{560,48},{576,64},{592,80},{608,96},{624... | collective-permute-start | bytes 393224 | tf_op jit(solution)/shard_map/ppermute | solution.py:19
  196.8 32.6 %collective-permute-start.26 = (f32[3,4,128]{2,1,0:T(4,128)S(1)}, f32[3,4,128]{2,1,0:T(4,128)S(1)}, u32[]{:S(2)}, u32[]{:S(2)}) collective-permute-start(f32[3,4,128]{2,1,0:T(4,128)S(1)} %get-tuple-element.61), channel_id=1, source_target_pairs={{48,0},{0,16},{16,32},{32,48},{112,64},{64,80},{80,96},{96,112},{1... | collective-permute-start | bytes 18440 | tf_op jit(solution)/shard_map/ppermute | solution.py:63
  198.7 30.7 %collective-permute-start.25 = (f32[3,4,128]{2,1,0:T(4,128)S(1)}, f32[3,4,128]{2,1,0:T(4,128)S(1)}, u32[]{:S(2)}, u32[]{:S(2)}) collective-permute-start(f32[3,4,128]{2,1,0:T(4,128)S(1)} %get-tuple-element.61), channel_id=1, source_target_pairs={{32,0},{48,16},{0,32},{16,48},{96,64},{112,80},{64,96},{80,112},{1... | collective-permute-start | bytes 18440 | tf_op jit(solution)/shard_map/ppermute | solution.py:63
  200.9 28.5 %collective-permute-start.24 = (f32[3,4,128]{2,1,0:T(4,128)S(1)}, f32[3,4,128]{2,1,0:T(4,128)S(1)}, u32[]{:S(2)}, u32[]{:S(2)}) collective-permute-start(f32[3,4,128]{2,1,0:T(4,128)S(1)} %get-tuple-element.61), channel_id=1, source_target_pairs={{16,0},{32,16},{48,32},{0,48},{80,64},{96,80},{112,96},{64,112},{1... | collective-permute-start | bytes 18440 | tf_op jit(solution)/shard_map/ppermute | solution.py:63
  204.6 22.2 %collective-permute-start.22 = (f32[1,3,128]{2,1,0:T(4,128)S(1)}, f32[1,3,128]{2,1,0:T(4,128)S(1)}, u32[]{:S(2)}, u32[]{:S(2)}) collective-permute-start(f32[1,3,128]{2,1,0:T(4,128)S(1)} %pad_add_fusion.5), channel_id=1, source_target_pairs={{16,0},{32,16},{48,32},{64,48},{80,64},{96,80},{112,96},{128,112},... | collective-permute-start | bytes 4616 | tf_op jit(solution)/shard_map/ppermute | solution.py:19
  208.0 20.7 %collective-permute-start.23 = (f32[1,3,128]{2,1,0:T(4,128)S(1)}, f32[1,3,128]{2,1,0:T(4,128)S(1)}, u32[]{:S(2)}, u32[]{:S(2)}) collective-permute-start(f32[1,3,128]{2,1,0:T(4,128)S(1)} %pad_add_fusion.4), channel_id=1, source_target_pairs={{16,0},{32,16},{48,32},{64,48},{80,64},{96,80},{112,96},{128,112},... | collective-permute-start | bytes 4616 | tf_op jit(solution)/shard_map/ppermute | solution.py:19
  230.1 11.6 %collective-permute-start.29 = (f32[3,4,128]{2,1,0:T(4,128)S(1)}, f32[3,4,128]{2,1,0:T(4,128)S(1)}, u32[]{:S(2)}, u32[]{:S(2)}) collective-permute-start(f32[3,4,128]{2,1,0:T(4,128)S(1)} %fusion.231), channel_id=1, source_target_pairs={{192,0},{208,16},{224,32},{240,48},{0,64},{16,80},{32,96},{48,112}... | collective-permute-start | bytes 18440 | tf_op jit(solution)/shard_map/ppermute | solution.py:63
  235.4 6.4 %collective-permute-start.28 = (f32[3,4,128]{2,1,0:T(4,128)S(1)}, f32[3,4,128]{2,1,0:T(4,128)S(1)}, u32[]{:S(2)}, u32[]{:S(2)}) collective-permute-start(f32[3,4,128]{2,1,0:T(4,128)S(1)} %fusion.231), channel_id=1, source_target_pairs={{128,0},{144,16},{160,32},{176,48},{192,64},{208,80},{224,96},{240... | collective-permute-start | bytes 18440 | tf_op jit(solution)/shard_map/ppermute | solution.py:63
  237.5 5.5 %collective-permute-start.27 = (f32[3,4,128]{2,1,0:T(4,128)S(1)}, f32[3,4,128]{2,1,0:T(4,128)S(1)}, u32[]{:S(2)}, u32[]{:S(2)}) collective-permute-start(f32[3,4,128]{2,1,0:T(4,128)S(1)} %fusion.231), channel_id=1, source_target_pairs={{64,0},{80,16},{96,32},{112,48},{128,64},{144,80},{160,96},{176,11... | collective-permute-start | bytes 18440 | tf_op jit(solution)/shard_map/ppermute | solution.py:63
  243.6 11.7 %collective-permute-start.32 = (f32[3,4,128]{2,1,0:T(4,128)S(1)}, f32[3,4,128]{2,1,0:T(4,128)S(1)}, u32[]{:S(2)}, u32[]{:S(2)}) collective-permute-start(f32[3,4,128]{2,1,0:T(4,128)S(1)} %fusion.230), channel_id=1, source_target_pairs={{768,0},{784,16},{800,32},{816,48},{832,64},{848,80},{864,96},{880... | collective-permute-start | bytes 18440 | tf_op jit(solution)/shard_map/ppermute | solution.py:63
  245.5 14.2 %collective-permute-start.31 = (f32[3,4,128]{2,1,0:T(4,128)S(1)}, f32[3,4,128]{2,1,0:T(4,128)S(1)}, u32[]{:S(2)}, u32[]{:S(2)}) collective-permute-start(f32[3,4,128]{2,1,0:T(4,128)S(1)} %fusion.230), channel_id=1, source_target_pairs={{512,0},{528,16},{544,32},{560,48},{576,64},{592,80},{608,96},{624... | collective-permute-start | bytes 18440 | tf_op jit(solution)/shard_map/ppermute | solution.py:63
  247.4 14.8 %collective-permute-start.30 = (f32[3,4,128]{2,1,0:T(4,128)S(1)}, f32[3,4,128]{2,1,0:T(4,128)S(1)}, u32[]{:S(2)}, u32[]{:S(2)}) collective-permute-start(f32[3,4,128]{2,1,0:T(4,128)S(1)} %fusion.230), channel_id=1, source_target_pairs={{256,0},{272,16},{288,32},{304,48},{320,64},{336,80},{352,96},{368... | collective-permute-start | bytes 18440 | tf_op jit(solution)/shard_map/ppermute | solution.py:63
Sparse Core Ops, SparseCore 0:
  20.5 52.1 all-gather.1

commit v4 on v3

--- a/solution.py
+++ b/solution.py
@@ -19,7 +19,7 @@
     return lax.ppermute(block, axis, route)
 
 
-def carried_in(parts, axis, combine, identity, reverse, radix=4):
+def carried_in(parts, axis, combine, identity, reverse, radix=2):
     count = lax.axis_size(axis)
     place = lax.axis_index(axis)
     ranks = [count - 1 - place if back else place for back in reverse]
@@ -46,28 +46,7 @@
 
 
 def summed(part, axis):
-    count = lax.axis_size(axis)
-    place = lax.axis_index(axis)
-    distance = 1
-    while distance < count:
-        radix = 4 if (count // distance) % 4 == 0 else 2
-        if (count // distance) % radix:
-            return lax.psum(part, axis)
-        digit = (place // distance) % radix
-        got = [part]
-        for shift in range(1, radix):
-            route = []
-            for i in range(count):
-                own = (i // distance) % radix
-                route.append((i + ((own + shift) % radix - own) * distance, i))
-            got.append(lax.ppermute(part, axis, route))
-        ordered = jnp.stack(got)[(jnp.arange(radix) - digit) % radix]
-        if radix == 4:
-            part = (ordered[0] + ordered[1]) + (ordered[2] + ordered[3])
-        else:
-            part = ordered[0] + ordered[1]
-        distance *= radix
-    return part
+    return jnp.sum(lax.all_gather(part, axis), axis=0)
 
 
 def conv_silu(extended, weights, row_count):
@@ -145,7 +124,7 @@
     head_count = col_count // FEATURE_DIM
     margin = CONV - 1
     tail = row_count - margin
-    rim_rows = passed_along((q_raw[tail:], k_raw[tail:], v_raw[tail:]), "ctx", 1)
+    rim_rows = passed_along(jnp.stack([q_raw[tail:], k_raw[tail:], v_raw[tail:]]), "ctx", 1)
 
     def extend(rim_part, main_part):
         joined = jnp.concatenate([rim_part, main_part], 0).astype(jnp.float32)
@@ -184,7 +163,7 @@
     _, backward = jax.vjp(batched, prepared, carried[1])
     grads = prepare_back(backward((out_cot, suffix[1]))[0])
     rim_back = passed_along(
-        (grads[0][:, :margin], grads[1][:, :margin], grads[2][:, :margin]), "ctx", -1
+        jnp.stack([grads[0][:, :margin], grads[1][:, :margin], grads[2][:, :margin]]), "ctx", -1
     )
 
     def finish(grad_ext, rim_part):

time: 274 us -> 322 us (1.18); the launches traced: 270 us -> 322 us
  blocking collectives: 0 us -> 109 us
  starting transfers between devices: 124 us -> 65.5 us
  waiting for transfers between devices: 65.5 us -> 73.1 us
  matrix products: 32.2 us -> 28.9 us
    all_gather x0 -> x1, blocking collectives: none -> 109 us  [summed(): return jnp.sum(lax.all_gather(part, axis), axis=0)]
    ppermute x9 -> x0, starting transfers between devices: 31 us -> none  [summed(): got.append(lax.ppermute(part, axis, route))]
    ppermute x24 -> x14, starting transfers between devices: 93.3 us -> 65.5 us  [passed_along(): return lax.ppermute(block, axis, route)]
    ppermute x24 -> x14, waiting for transfers between devices: 57.2 us -> 73 us  [passed_along(): return lax.ppermute(block, axis, route)]
    ppermute x9 -> x0, waiting for transfers between devices: 8.27 us -> none  [summed(): got.append(lax.ppermute(part, axis, route))]
  transfers between devices with their start and end apart: 34 -> 15, of which waited for: 16 -> 12; matrix products, arithmetic and copies ran while one was open for 16% -> 11% of each run, Pallas kernels for 0% -> 0%
where the time goes in v4:
time: 322 us
  blocking collectives  109 us (34%)
  waiting for transfers between devices  73.1 us (23%)
  starting transfers between devices  65.5 us (20%)
  matrix products  28.9 us (9%)
  other arithmetic  26.1 us (8%)
  between operations  15.5 us (5%)
    all_gather x1, blocking collectives, summed(): return jnp.sum(lax.all_gather(part, axis), axis=0)  109 us
    ppermute x14, waiting for transfers between devices, passed_along(): return lax.ppermute(block, axis, route)  73 us
    ppermute x14, starting transfers between devices, passed_along(): return lax.ppermute(block, axis, route)  65.5 us
    another operation x3, other arithmetic, wy_factors(): jax.scipy.linalg.solve_triangular(system, weighted, lower=True, unit_diag...  19.7 us
  transfers between devices with their start and end apart: 15, of which 12 were waited for; matrix products, arithmetic and copies ran while one was open for 11% of the time, Pallas kernels for 0%

profile of v4, /device:TPU:6, one launch (start us, length us, event | category | flops | bytes accessed | tf_op | source)
XLA Modules:
  0.0 321.6 jit_solution(13167665392826876469)
XLA Ops:
  7.2 0.7 slice_bitcast_fusion.211
  8.0 0.7 slice_bitcast_fusion.209
  8.7 4.2 %collective-permute-start = (bf16[3,3,128]{2,1,0:T(4,128)(2,1)S(1)}, bf16[3,3,128]{2,1,0:T(4,128)(2,1)S(1)}, u32[]{:S(2)}, u32[]{:S(2)}) collective-permute-start(bf16[3,3,128]{2,1,0:T(4,128)(2,1)S(1)} %pad_maximum_fusion.5), channel_id=1, source_target_pairs={{0,16},{16,32},{32,48},{48,64},{64,80},{80,96},{96,112},{112,128},... | collective-permute-start | bytes 6920 | tf_op jit(solution)/shard_map/ppermute | solution.py:19
  13.0 0.6 copy-done.4
  13.7 0.5 broadcast.425
  14.2 0.7 fusion.159
  15.4 0.4 fusion.16
  15.8 19.7 %custom-call.10 = f32[1,4,1,64,64]{3,4,2,1,0:T(8,128)S(1)} custom-call(f32[1,4,1,64,64]{4,3,2,1,0:T(8,128)S(1)} %fusion.16), custom_call_target="InvertDiagBlocksLowerTriangular" | custom-call | tf_op jit(solution)/shard_map/jvp(vmap(vmap(jit(_solve_triangular))))/triangular_solve | solution.py:67
  35.6 0.4 fusion.65
  36.1 0.6 convolution_bitcast_fusion
  36.7 0.4 fusion.67
  37.1 0.6 fusion
  39.3 5.4 %collective-permute-start.1 = (f32[2,1,128,128]{2,3,1,0:T(8,128)S(1)}, f32[2,1,128,128]{2,3,1,0:T(8,128)S(1)}, u32[]{:S(2)}, u32[]{:S(2)}) collective-permute-start(f32[2,1,128,128]{2,3,1,0:T(8,128)S(1)} %pad_maximum_fusion), channel_id=1, source_target_pairs={{0,16},{16,32},{32,48},{48,64},{64,80},{80,96},{96,112},{112,128},... | collective-permute-start | bytes 393224 | tf_op jit(solution)/shard_map/ppermute | solution.py:19
  44.8 2.4 collective-permute-done.1
  47.8 3.8 %collective-permute-start.2 = (f32[2,1,128,128]{2,3,1,0:T(8,128)S(1)}, f32[2,1,128,128]{2,3,1,0:T(8,128)S(1)}, u32[]{:S(2)}, u32[]{:S(2)}) collective-permute-start(f32[2,1,128,128]{2,3,1,0:T(8,128)S(1)} %maximum_select_fusion), channel_id=1, source_target_pairs={{0,32},{16,48},{32,64},{48,80},{64,96},{80,112},{96,128},{112,144}... | collective-permute-start | bytes 393224 | tf_op jit(solution)/shard_map/ppermute | solution.py:19
  52.0 10.0 %collective-permute-done.2 = f32[2,1,128,128]{2,3,1,0:T(8,128)S(1)} collective-permute-done((f32[2,1,128,128]{2,3,1,0:T(8,128)S(1)}, f32[2,1,128,128]{2,3,1,0:T(8,128)S(1)}, u32[]{:S(2)}, u32[]{:S(2)}) %collective-permute-start.2) | collective-permute-done | bytes 131104 | tf_op jit(solution)/shard_map/ppermute | solution.py:19
  62.4 1.3 collective-permute-start.3
  64.2 2.0 collective-permute-done.3
  66.7 5.6 %collective-permute-start.4 = (f32[2,1,128,128]{2,3,1,0:T(8,128)S(1)}, f32[2,1,128,128]{2,3,1,0:T(8,128)S(1)}, u32[]{:S(2)}, u32[]{:S(2)}) collective-permute-start(f32[2,1,128,128]{2,3,1,0:T(8,128)S(1)} %maximum_select_fusion.4), channel_id=1, source_target_pairs={{0,128},{16,144},{32,160},{48,176},{64,192},{80,208},{96,224},{112... | collective-permute-start | bytes 393224 | tf_op jit(solution)/shard_map/ppermute | solution.py:19
  72.8 2.0 collective-permute-done.4
  75.3 11.2 %collective-permute-start.5 = (f32[2,1,128,128]{2,3,1,0:T(8,128)S(1)}, f32[2,1,128,128]{2,3,1,0:T(8,128)S(1)}, u32[]{:S(2)}, u32[]{:S(2)}) collective-permute-start(f32[2,1,128,128]{2,3,1,0:T(8,128)S(1)} %maximum_select_fusion.6), channel_id=1, source_target_pairs={{0,256},{16,272},{32,288},{48,304},{64,320},{80,336},{96,352},{112... | collective-permute-start | bytes 393224 | tf_op jit(solution)/shard_map/ppermute | solution.py:19
  87.0 2.0 collective-permute-done.5
  89.5 18.9 %collective-permute-start.6 = (f32[2,1,128,128]{2,3,1,0:T(8,128)S(1)}, f32[2,1,128,128]{2,3,1,0:T(8,128)S(1)}, u32[]{:S(2)}, u32[]{:S(2)}) collective-permute-start(f32[2,1,128,128]{2,3,1,0:T(8,128)S(1)} %maximum_select_fusion.8), channel_id=1, source_target_pairs={{0,512},{16,528},{32,544},{48,560},{64,576},{80,592},{96,608},{112... | collective-permute-start | bytes 393224 | tf_op jit(solution)/shard_map/ppermute | solution.py:19
  108.8 1.8 collective-permute-done.6
  111.4 0.3 convolution_add_fusion.14
  111.9 0.3 convolution_add_fusion.13
  112.5 0.3 convolution_add_fusion.12
  113.0 1.7 fusion.161
  116.9 0.3 fusion.4
  118.2 0.3 convolution_bitcast_fusion.27
  118.8 0.3 convolution_bitcast_fusion.23
  119.1 0.4 fusion.36
  119.8 0.3 fusion.37
  120.3 0.3 fusion.38
  120.8 0.3 convolution_bitcast_fusion.20
  121.1 0.3 fusion.40
  121.5 4.5 %collective-permute-start.7 = (f32[2,1,128,128]{2,3,1,0:T(8,128)S(1)}, f32[2,1,128,128]{2,3,1,0:T(8,128)S(1)}, u32[]{:S(2)}, u32[]{:S(2)}) collective-permute-start(f32[2,1,128,128]{2,3,1,0:T(8,128)S(1)} %pad_maximum_fusion.1), channel_id=1, source_target_pairs={{16,0},{32,16},{48,32},{64,48},{80,64},{96,80},{112,96},{128,112},... | collective-permute-start | bytes 393224 | tf_op jit(solution)/shard_map/ppermute | solution.py:19
  126.1 6.1 %collective-permute-done.7 = f32[2,1,128,128]{2,3,1,0:T(8,128)S(1)} collective-permute-done((f32[2,1,128,128]{2,3,1,0:T(8,128)S(1)}, f32[2,1,128,128]{2,3,1,0:T(8,128)S(1)}, u32[]{:S(2)}, u32[]{:S(2)}) %collective-permute-start.7) | collective-permute-done | bytes 131104 | tf_op jit(solution)/shard_map/ppermute | solution.py:19
  132.7 3.3 %collective-permute-start.8 = (f32[2,1,128,128]{2,3,1,0:T(8,128)S(1)}, f32[2,1,128,128]{2,3,1,0:T(8,128)S(1)}, u32[]{:S(2)}, u32[]{:S(2)}) collective-permute-start(f32[2,1,128,128]{2,3,1,0:T(8,128)S(1)} %maximum_select_fusion.9), channel_id=1, source_target_pairs={{32,0},{48,16},{64,32},{80,48},{96,64},{112,80},{128,96},{144,112}... | collective-permute-start | bytes 393224 | tf_op jit(solution)/shard_map/ppermute | solution.py:19
  136.5 5.5 %collective-permute-done.8 = f32[2,1,128,128]{2,3,1,0:T(8,128)S(1)} collective-permute-done((f32[2,1,128,128]{2,3,1,0:T(8,128)S(1)}, f32[2,1,128,128]{2,3,1,0:T(8,128)S(1)}, u32[]{:S(2)}, u32[]{:S(2)}) %collective-permute-start.8) | collective-permute-done | bytes 131104 | tf_op jit(solution)/shard_map/ppermute | solution.py:19
  142.4 1.3 collective-permute-start.9
  144.1 6.1 %collective-permute-done.9 = f32[2,1,128,128]{2,3,1,0:T(8,128)S(1)} collective-permute-done((f32[2,1,128,128]{2,3,1,0:T(8,128)S(1)}, f32[2,1,128,128]{2,3,1,0:T(8,128)S(1)}, u32[]{:S(2)}, u32[]{:S(2)}) %collective-permute-start.9) | collective-permute-done | bytes 131104 | tf_op jit(solution)/shard_map/ppermute | solution.py:19
  150.7 1.3 collective-permute-start.10
  152.5 10.1 %collective-permute-done.10 = f32[2,1,128,128]{2,3,1,0:T(8,128)S(1)} collective-permute-done((f32[2,1,128,128]{2,3,1,0:T(8,128)S(1)}, f32[2,1,128,128]{2,3,1,0:T(8,128)S(1)}, u32[]{:S(2)}, u32[]{:S(2)}) %collective-permute-start.10) | collective-permute-done | bytes 131104 | tf_op jit(solution)/shard_map/ppermute | solution.py:19
  163.0 1.3 collective-permute-start.11
  164.8 9.9 %collective-permute-done.11 = f32[2,1,128,128]{2,3,1,0:T(8,128)S(1)} collective-permute-done((f32[2,1,128,128]{2,3,1,0:T(8,128)S(1)}, f32[2,1,128,128]{2,3,1,0:T(8,128)S(1)}, u32[]{:S(2)}, u32[]{:S(2)}) %collective-permute-start.11) | collective-permute-done | bytes 131104 | tf_op jit(solution)/shard_map/ppermute | solution.py:19
  175.1 1.5 collective-permute-start.12
  177.1 15.1 %collective-permute-done.12 = f32[2,1,128,128]{2,3,1,0:T(8,128)S(1)} collective-permute-done((f32[2,1,128,128]{2,3,1,0:T(8,128)S(1)}, f32[2,1,128,128]{2,3,1,0:T(8,128)S(1)}, u32[]{:S(2)}, u32[]{:S(2)}) %collective-permute-start.12) | collective-permute-done | bytes 131104 | tf_op jit(solution)/shard_map/ppermute | solution.py:19
  193.1 0.3 fusion.43
  193.9 0.3 fusion.44
  194.6 0.3 fusion.46
  196.1 0.4 multiply_reduce_fusion.1
  196.5 0.3 fusion.81
  196.8 0.3 fusion.80
  197.9 0.4 multiply_reduce_fusion
  198.3 0.4 convolution_add_fusion.1
  198.7 0.4 fusion.8
  199.8 1.9 collective-permute-start.13
  201.8 109.5 %all_gather.7 = f32[64,3,4,128]{3,2,1,0:T(4,128)S(1)} all-gather(f32[1,3,4,128]{3,2,1,0:T(4,128)S(1)} %pad_add_fusion.3), channel_id=1, replica_groups=mesh['ctx'=64,'head'=16] {'ctx'}, dimensions={0}, use_global_device_ids=true | all-gather | bytes 399360 | tf_op jit(solution)/shard_map/all_gather | solution.py:49
  311.3 0.6 broadcast_multiply_fusion.15
  312.0 0.6 fusion.147
  312.7 0.7 maximum_bitcast_fusion.5
  313.4 0.7 maximum_bitcast_fusion.6
  314.1 0.7 maximum_bitcast_fusion.7
  (175 shorter events, 21.5 us)
Async XLA Ops:
  7.2 105.9 %copy-start = (bf16[128,2048]{1,0:T(8,128)(2,1)S(1)}, bf16[128,2048]{1,0:T(8,128)(2,1)}, u32[]{:S(2)}) copy-start(bf16[128,2048]{1,0:T(8,128)(2,1)} %param.18) | copy-start | bytes 1572868
  7.2 105.8 %all-gather.2.cloned.1.call-start = ((), (), s32[]{:S(2)}) async-start(), calls=%async_computation | async-start | bytes 1114112 | tf_op jit(solution)/shard_map/all_gather | solution.py:138
  8.7 6.4 %collective-permute-start = (bf16[3,3,128]{2,1,0:T(4,128)(2,1)S(1)}, bf16[3,3,128]{2,1,0:T(4,128)(2,1)S(1)}, u32[]{:S(2)}, u32[]{:S(2)}) collective-permute-start(bf16[3,3,128]{2,1,0:T(4,128)(2,1)S(1)} %pad_maximum_fusion.5), channel_id=1, source_target_pairs={{0,16},{16,32},{32,48},{48,64},{64,80},{80,96},{96,112},{112,128},... | collective-permute-start | bytes 6920 | tf_op jit(solution)/shard_map/ppermute | solution.py:19
  12.9 0.7 copy-start.4
  12.9 1.3 copy-start.5
  13.0 2.1 copy-start.1
  15.4 20.1 %copy-start.2 = (bf16[256,128]{1,0:T(8,128)(2,1)S(1)}, bf16[256,128]{1,0:T(8,128)(2,1)}, u32[]{:S(2)}) copy-start(bf16[256,128]{1,0:T(8,128)(2,1)} %param.15) | copy-start | bytes 196612
  39.2 5.6 %copy-start.3 = (bf16[256,128]{1,0:T(8,128)(2,1)S(1)}, bf16[256,128]{1,0:T(8,128)(2,1)}, u32[]{:S(2)}) copy-start(bf16[256,128]{1,0:T(8,128)(2,1)} %param.13) | copy-start | bytes 196612
  39.3 7.9 %collective-permute-start.1 = (f32[2,1,128,128]{2,3,1,0:T(8,128)S(1)}, f32[2,1,128,128]{2,3,1,0:T(8,128)S(1)}, u32[]{:S(2)}, u32[]{:S(2)}) collective-permute-start(f32[2,1,128,128]{2,3,1,0:T(8,128)S(1)} %pad_maximum_fusion), channel_id=1, source_target_pairs={{0,16},{16,32},{32,48},{48,64},{64,80},{80,96},{96,112},{112,128},... | collective-permute-start | bytes 393224 | tf_op jit(solution)/shard_map/ppermute | solution.py:19
  47.8 14.2 %collective-permute-start.2 = (f32[2,1,128,128]{2,3,1,0:T(8,128)S(1)}, f32[2,1,128,128]{2,3,1,0:T(8,128)S(1)}, u32[]{:S(2)}, u32[]{:S(2)}) collective-permute-start(f32[2,1,128,128]{2,3,1,0:T(8,128)S(1)} %maximum_select_fusion), channel_id=1, source_target_pairs={{0,32},{16,48},{32,64},{48,80},{64,96},{80,112},{96,128},{112,144}... | collective-permute-start | bytes 393224 | tf_op jit(solution)/shard_map/ppermute | solution.py:19
  62.4 3.8 %collective-permute-start.3 = (f32[2,1,128,128]{2,3,1,0:T(8,128)S(1)}, f32[2,1,128,128]{2,3,1,0:T(8,128)S(1)}, u32[]{:S(2)}, u32[]{:S(2)}) collective-permute-start(f32[2,1,128,128]{2,3,1,0:T(8,128)S(1)} %maximum_select_fusion.2), channel_id=1, source_target_pairs={{0,64},{16,80},{32,96},{48,112},{64,128},{80,144},{96,160},{112,17... | collective-permute-start | bytes 393224 | tf_op jit(solution)/shard_map/ppermute | solution.py:19
  66.7 8.1 %collective-permute-start.4 = (f32[2,1,128,128]{2,3,1,0:T(8,128)S(1)}, f32[2,1,128,128]{2,3,1,0:T(8,128)S(1)}, u32[]{:S(2)}, u32[]{:S(2)}) collective-permute-start(f32[2,1,128,128]{2,3,1,0:T(8,128)S(1)} %maximum_select_fusion.4), channel_id=1, source_target_pairs={{0,128},{16,144},{32,160},{48,176},{64,192},{80,208},{96,224},{112... | collective-permute-start | bytes 393224 | tf_op jit(solution)/shard_map/ppermute | solution.py:19
  75.3 13.7 %collective-permute-start.5 = (f32[2,1,128,128]{2,3,1,0:T(8,128)S(1)}, f32[2,1,128,128]{2,3,1,0:T(8,128)S(1)}, u32[]{:S(2)}, u32[]{:S(2)}) collective-permute-start(f32[2,1,128,128]{2,3,1,0:T(8,128)S(1)} %maximum_select_fusion.6), channel_id=1, source_target_pairs={{0,256},{16,272},{32,288},{48,304},{64,320},{80,336},{96,352},{112... | collective-permute-start | bytes 393224 | tf_op jit(solution)/shard_map/ppermute | solution.py:19
  89.5 21.2 %collective-permute-start.6 = (f32[2,1,128,128]{2,3,1,0:T(8,128)S(1)}, f32[2,1,128,128]{2,3,1,0:T(8,128)S(1)}, u32[]{:S(2)}, u32[]{:S(2)}) collective-permute-start(f32[2,1,128,128]{2,3,1,0:T(8,128)S(1)} %maximum_select_fusion.8), channel_id=1, source_target_pairs={{0,512},{16,528},{32,544},{48,560},{64,576},{80,592},{96,608},{112... | collective-permute-start | bytes 393224 | tf_op jit(solution)/shard_map/ppermute | solution.py:19
  121.5 10.8 %collective-permute-start.7 = (f32[2,1,128,128]{2,3,1,0:T(8,128)S(1)}, f32[2,1,128,128]{2,3,1,0:T(8,128)S(1)}, u32[]{:S(2)}, u32[]{:S(2)}) collective-permute-start(f32[2,1,128,128]{2,3,1,0:T(8,128)S(1)} %pad_maximum_fusion.1), channel_id=1, source_target_pairs={{16,0},{32,16},{48,32},{64,48},{80,64},{96,80},{112,96},{128,112},... | collective-permute-start | bytes 393224 | tf_op jit(solution)/shard_map/ppermute | solution.py:19
  132.7 9.3 %collective-permute-start.8 = (f32[2,1,128,128]{2,3,1,0:T(8,128)S(1)}, f32[2,1,128,128]{2,3,1,0:T(8,128)S(1)}, u32[]{:S(2)}, u32[]{:S(2)}) collective-permute-start(f32[2,1,128,128]{2,3,1,0:T(8,128)S(1)} %maximum_select_fusion.9), channel_id=1, source_target_pairs={{32,0},{48,16},{64,32},{80,48},{96,64},{112,80},{128,96},{144,112}... | collective-permute-start | bytes 393224 | tf_op jit(solution)/shard_map/ppermute | solution.py:19
  142.4 7.9 %collective-permute-start.9 = (f32[2,1,128,128]{2,3,1,0:T(8,128)S(1)}, f32[2,1,128,128]{2,3,1,0:T(8,128)S(1)}, u32[]{:S(2)}, u32[]{:S(2)}) collective-permute-start(f32[2,1,128,128]{2,3,1,0:T(8,128)S(1)} %maximum_select_fusion.11), channel_id=1, source_target_pairs={{64,0},{80,16},{96,32},{112,48},{128,64},{144,80},{160,96},{176,11... | collective-permute-start | bytes 393224 | tf_op jit(solution)/shard_map/ppermute | solution.py:19
  150.7 11.8 %collective-permute-start.10 = (f32[2,1,128,128]{2,3,1,0:T(8,128)S(1)}, f32[2,1,128,128]{2,3,1,0:T(8,128)S(1)}, u32[]{:S(2)}, u32[]{:S(2)}) collective-permute-start(f32[2,1,128,128]{2,3,1,0:T(8,128)S(1)} %maximum_select_fusion.13), channel_id=1, source_target_pairs={{128,0},{144,16},{160,32},{176,48},{192,64},{208,80},{224,96},{240... | collective-permute-start | bytes 393224 | tf_op jit(solution)/shard_map/ppermute | solution.py:19
  163.0 11.7 %collective-permute-start.11 = (f32[2,1,128,128]{2,3,1,0:T(8,128)S(1)}, f32[2,1,128,128]{2,3,1,0:T(8,128)S(1)}, u32[]{:S(2)}, u32[]{:S(2)}) collective-permute-start(f32[2,1,128,128]{2,3,1,0:T(8,128)S(1)} %maximum_select_fusion.15), channel_id=1, source_target_pairs={{256,0},{272,16},{288,32},{304,48},{320,64},{336,80},{352,96},{368... | collective-permute-start | bytes 393224 | tf_op jit(solution)/shard_map/ppermute | solution.py:19
  175.1 17.1 %collective-permute-start.12 = (f32[2,1,128,128]{2,3,1,0:T(8,128)S(1)}, f32[2,1,128,128]{2,3,1,0:T(8,128)S(1)}, u32[]{:S(2)}, u32[]{:S(2)}) collective-permute-start(f32[2,1,128,128]{2,3,1,0:T(8,128)S(1)} %maximum_select_fusion.17), channel_id=1, source_target_pairs={{512,0},{528,16},{544,32},{560,48},{576,64},{592,80},{608,96},{624... | collective-permute-start | bytes 393224 | tf_op jit(solution)/shard_map/ppermute | solution.py:19
  199.8 112.9 %collective-permute-start.13 = (f32[3,1,3,128]{3,2,1,0:T(4,128)S(1)}, f32[3,1,3,128]{3,2,1,0:T(4,128)S(1)}, u32[]{:S(2)}, u32[]{:S(2)}) collective-permute-start(f32[3,1,3,128]{3,2,1,0:T(4,128)S(1)} %pad_maximum_fusion.4), channel_id=1, source_target_pairs={{16,0},{32,16},{48,32},{64,48},{80,64},{96,80},{112,96},{128,112},... | collective-permute-start | bytes 13832 | tf_op jit(solution)/shard_map/ppermute | solution.py:19
Sparse Core Ops, SparseCore 0:
  13.0 52.2 all-gather.1

commit v5 on v3

--- a/solution.py
+++ b/solution.py
@@ -145,7 +145,7 @@
     head_count = col_count // FEATURE_DIM
     margin = CONV - 1
     tail = row_count - margin
-    rim_rows = passed_along((q_raw[tail:], k_raw[tail:], v_raw[tail:]), "ctx", 1)
+    rim_rows = passed_along(jnp.stack([q_raw[tail:], k_raw[tail:], v_raw[tail:]]), "ctx", 1)
 
     def extend(rim_part, main_part):
         joined = jnp.concatenate([rim_part, main_part], 0).astype(jnp.float32)
@@ -184,7 +184,7 @@
     _, backward = jax.vjp(batched, prepared, carried[1])
     grads = prepare_back(backward((out_cot, suffix[1]))[0])
     rim_back = passed_along(
-        (grads[0][:, :margin], grads[1][:, :margin], grads[2][:, :margin]), "ctx", -1
+        jnp.stack([grads[0][:, :margin], grads[1][:, :margin], grads[2][:, :margin]]), "ctx", -1
     )
 
     def finish(grad_ext, rim_part):

time: 274 us -> 264 us (0.964)
  starting transfers between devices: 124 us -> 108 us
  waiting for transfers between devices: 65.5 us -> 74 us
    ppermute x24 -> x20, starting transfers between devices: 93.3 us -> 75.8 us  [passed_along(): return lax.ppermute(block, axis, route)]
    ppermute x24 -> x20, waiting for transfers between devices: 57.2 us -> 64.1 us  [passed_along(): return lax.ppermute(block, axis, route)]
  transfers between devices with their start and end apart: 34 -> 30, of which waited for: 16 -> 18; matrix products, arithmetic and copies ran while one was open for 16% -> 16% of each run, Pallas kernels for 0% -> 0%
where the time goes in v5:
time: 264 us; the launch traced here: 261 us
  starting transfers between devices  108 us (41%)
  waiting for transfers between devices  74 us (28%)
  matrix products  32.2 us (12%)
  other arithmetic  26.7 us (10%)
  between operations  16 us (6%)
  local copies, waits for them, and re-layouts  4.85 us (2%)
    ppermute x20, starting transfers between devices, passed_along(): return lax.ppermute(block, axis, route)  75.8 us
    ppermute x20, waiting for transfers between devices, passed_along(): return lax.ppermute(block, axis, route)  64.1 us
    ppermute x9, starting transfers between devices, summed(): got.append(lax.ppermute(part, axis, route))  31.9 us
    another operation x3, other arithmetic, wy_factors(): jax.scipy.linalg.solve_triangular(system, weighted, lower=True, unit_diag...  19.7 us
    ppermute x9, waiting for transfers between devices, summed(): got.append(lax.ppermute(part, axis, route))  9.83 us
    dot_general x30, matrix products, combine_pairs(): offset_term = jnp.matmul(later[0], earlier[1], precision=HIGHEST) + later[1]  6.22 us
    dot_general x30, matrix products, combine_pairs(): product = jnp.matmul(later[0], earlier[0], precision=HIGHEST)  6.2 us
  transfers between devices with their start and end apart: 30, of which 18 were waited for; matrix products, arithmetic and copies ran while one was open for 16% of the time, Pallas kernels for 0%

profile of v5, /device:TPU:6, one launch (start us, length us, event | category | flops | bytes accessed | tf_op | source)
XLA Modules:
  0.0 261.4 jit_solution(15844365988202113152)
XLA Ops:
  7.2 0.7 slice_bitcast_fusion.271
  8.0 0.7 slice_bitcast_fusion.269
  8.7 4.2 %collective-permute-start = (bf16[3,3,128]{2,1,0:T(4,128)(2,1)S(1)}, bf16[3,3,128]{2,1,0:T(4,128)(2,1)S(1)}, u32[]{:S(2)}, u32[]{:S(2)}) collective-permute-start(bf16[3,3,128]{2,1,0:T(4,128)(2,1)S(1)} %pad_maximum_fusion.8), channel_id=1, source_target_pairs={{0,16},{16,32},{32,48},{48,64},{64,80},{80,96},{96,112},{112,128},... | collective-permute-start | bytes 6920 | tf_op jit(solution)/shard_map/ppermute | solution.py:19
  13.1 0.7 copy-done.4
  13.9 0.5 broadcast.684
  14.6 0.7 fusion.179
  16.2 19.7 %custom-call.10 = f32[1,4,1,64,64]{3,4,2,1,0:T(8,128)S(1)} custom-call(f32[1,4,1,64,64]{4,3,2,1,0:T(8,128)S(1)} %fusion.16), custom_call_target="InvertDiagBlocksLowerTriangular" | custom-call | tf_op jit(solution)/shard_map/jvp(vmap(vmap(jit(_solve_triangular))))/triangular_solve | solution.py:88
  36.0 0.4 fusion.73
  36.4 0.6 convolution_bitcast_fusion
  37.0 0.4 fusion.75
  37.5 0.6 fusion
  39.7 5.0 %collective-permute-start.1 = (f32[2,1,128,128]{2,3,1,0:T(8,128)S(1)}, f32[2,1,128,128]{2,3,1,0:T(8,128)S(1)}, u32[]{:S(2)}, u32[]{:S(2)}) collective-permute-start(f32[2,1,128,128]{2,3,1,0:T(8,128)S(1)} %pad_maximum_fusion), channel_id=1, source_target_pairs={{0,16},{16,32},{32,48},{48,64},{64,80},{80,96},{96,112},{112,128},... | collective-permute-start | bytes 393224 | tf_op jit(solution)/shard_map/ppermute | solution.py:19
  44.7 2.4 collective-permute-start.2
  47.1 4.1 %collective-permute-start.3 = (f32[2,1,128,128]{2,3,1,0:T(8,128)S(1)}, f32[2,1,128,128]{2,3,1,0:T(8,128)S(1)}, u32[]{:S(2)}, u32[]{:S(2)}) collective-permute-start(f32[2,1,128,128]{2,3,1,0:T(8,128)S(1)} %pad_maximum_fusion), channel_id=1, source_target_pairs={{0,48},{16,64},{32,80},{48,96},{64,112},{80,128},{96,144},{112,160... | collective-permute-start | bytes 393224 | tf_op jit(solution)/shard_map/ppermute | solution.py:19
  51.9 4.6 %collective-permute-done.2 = f32[2,1,128,128]{2,3,1,0:T(8,128)S(1)} collective-permute-done((f32[2,1,128,128]{2,3,1,0:T(8,128)S(1)}, f32[2,1,128,128]{2,3,1,0:T(8,128)S(1)}, u32[]{:S(2)}, u32[]{:S(2)}) %collective-permute-start.2) | collective-permute-done | bytes 131104 | tf_op jit(solution)/shard_map/ppermute | solution.py:19
  56.9 1.4 collective-permute-done.3
  58.8 1.8 collective-permute-start.4
  60.6 8.2 %collective-permute-start.5 = (f32[2,1,128,128]{2,3,1,0:T(8,128)S(1)}, f32[2,1,128,128]{2,3,1,0:T(8,128)S(1)}, u32[]{:S(2)}, u32[]{:S(2)}) collective-permute-start(f32[2,1,128,128]{2,3,1,0:T(8,128)S(1)} %maximum_select_fusion.4), channel_id=1, source_target_pairs={{0,128},{16,144},{32,160},{48,176},{64,192},{80,208},{96,224},{112... | collective-permute-start | bytes 393224 | tf_op jit(solution)/shard_map/ppermute | solution.py:19
  68.9 7.4 %collective-permute-start.6 = (f32[2,1,128,128]{2,3,1,0:T(8,128)S(1)}, f32[2,1,128,128]{2,3,1,0:T(8,128)S(1)}, u32[]{:S(2)}, u32[]{:S(2)}) collective-permute-start(f32[2,1,128,128]{2,3,1,0:T(8,128)S(1)} %maximum_select_fusion.4), channel_id=1, source_target_pairs={{0,192},{16,208},{32,224},{48,240},{64,256},{80,272},{96,288},{112... | collective-permute-start | bytes 393224 | tf_op jit(solution)/shard_map/ppermute | solution.py:19
  79.3 17.3 %collective-permute-start.9 = (f32[2,1,128,128]{2,3,1,0:T(8,128)S(1)}, f32[2,1,128,128]{2,3,1,0:T(8,128)S(1)}, u32[]{:S(2)}, u32[]{:S(2)}) collective-permute-start(f32[2,1,128,128]{2,3,1,0:T(8,128)S(1)} %maximum_select_fusion.10), channel_id=1, source_target_pairs={{0,768},{16,784},{32,800},{48,816},{64,832},{80,848},{96,864},{112... | collective-permute-start | bytes 393224 | tf_op jit(solution)/shard_map/ppermute | solution.py:19
  96.6 1.3 collective-permute-start.7
  97.9 7.5 %collective-permute-start.8 = (f32[2,1,128,128]{2,3,1,0:T(8,128)S(1)}, f32[2,1,128,128]{2,3,1,0:T(8,128)S(1)}, u32[]{:S(2)}, u32[]{:S(2)}) collective-permute-start(f32[2,1,128,128]{2,3,1,0:T(8,128)S(1)} %maximum_select_fusion.10), channel_id=1, source_target_pairs={{0,512},{16,528},{32,544},{48,560},{64,576},{80,592},{96,608},{112... | collective-permute-start | bytes 393224 | tf_op jit(solution)/shard_map/ppermute | solution.py:19
  108.2 7.1 %collective-permute-done.9 = f32[2,1,128,128]{2,3,1,0:T(8,128)S(1)} collective-permute-done((f32[2,1,128,128]{2,3,1,0:T(8,128)S(1)}, f32[2,1,128,128]{2,3,1,0:T(8,128)S(1)}, u32[]{:S(2)}, u32[]{:S(2)}) %collective-permute-start.9) | collective-permute-done | bytes 131104 | tf_op jit(solution)/shard_map/ppermute | solution.py:19
  117.6 1.7 fusion.181
  126.1 1.9 collective-permute-start.10
  128.0 1.9 collective-permute-start.11
  129.9 1.9 collective-permute-start.12
  132.0 4.9 %collective-permute-done.10 = f32[2,1,128,128]{2,3,1,0:T(8,128)S(1)} collective-permute-done((f32[2,1,128,128]{2,3,1,0:T(8,128)S(1)}, f32[2,1,128,128]{2,3,1,0:T(8,128)S(1)}, u32[]{:S(2)}, u32[]{:S(2)}) %collective-permute-start.10) | collective-permute-done | bytes 131104 | tf_op jit(solution)/shard_map/ppermute | solution.py:19
  137.4 1.1 collective-permute-done.11
  139.0 0.8 collective-permute-done.12
  140.3 1.3 collective-permute-start.13
  141.6 1.3 collective-permute-start.14
  142.9 1.3 collective-permute-start.15
  145.5 2.9 %collective-permute-done.13 = f32[2,1,128,128]{2,3,1,0:T(8,128)S(1)} collective-permute-done((f32[2,1,128,128]{2,3,1,0:T(8,128)S(1)}, f32[2,1,128,128]{2,3,1,0:T(8,128)S(1)}, u32[]{:S(2)}, u32[]{:S(2)}) %collective-permute-start.13) | collective-permute-done | bytes 131104 | tf_op jit(solution)/shard_map/ppermute | solution.py:19
  148.9 5.3 %collective-permute-done.14 = f32[2,1,128,128]{2,3,1,0:T(8,128)S(1)} collective-permute-done((f32[2,1,128,128]{2,3,1,0:T(8,128)S(1)}, f32[2,1,128,128]{2,3,1,0:T(8,128)S(1)}, u32[]{:S(2)}, u32[]{:S(2)}) %collective-permute-start.14) | collective-permute-done | bytes 131104 | tf_op jit(solution)/shard_map/ppermute | solution.py:19
  154.7 5.4 %collective-permute-done.15 = f32[2,1,128,128]{2,3,1,0:T(8,128)S(1)} collective-permute-done((f32[2,1,128,128]{2,3,1,0:T(8,128)S(1)}, f32[2,1,128,128]{2,3,1,0:T(8,128)S(1)}, u32[]{:S(2)}, u32[]{:S(2)}) %collective-permute-start.15) | collective-permute-done | bytes 131104 | tf_op jit(solution)/shard_map/ppermute | solution.py:19
  160.6 1.3 collective-permute-start.18
  161.9 1.3 collective-permute-start.16
  163.2 1.5 collective-permute-start.17
  166.1 8.4 %collective-permute-done.16 = f32[2,1,128,128]{2,3,1,0:T(8,128)S(1)} collective-permute-done((f32[2,1,128,128]{2,3,1,0:T(8,128)S(1)}, f32[2,1,128,128]{2,3,1,0:T(8,128)S(1)}, u32[]{:S(2)}, u32[]{:S(2)}) %collective-permute-start.16) | collective-permute-done | bytes 131104 | tf_op jit(solution)/shard_map/ppermute | solution.py:19
  175.0 3.9 %collective-permute-done.17 = f32[2,1,128,128]{2,3,1,0:T(8,128)S(1)} collective-permute-done((f32[2,1,128,128]{2,3,1,0:T(8,128)S(1)}, f32[2,1,128,128]{2,3,1,0:T(8,128)S(1)}, u32[]{:S(2)}, u32[]{:S(2)}) %collective-permute-start.17) | collective-permute-done | bytes 131104 | tf_op jit(solution)/shard_map/ppermute | solution.py:19
  186.1 0.4 fusion.8
  186.9 4.2 %collective-permute-start.22 = (f32[3,4,128]{2,1,0:T(4,128)S(1)}, f32[3,4,128]{2,1,0:T(4,128)S(1)}, u32[]{:S(2)}, u32[]{:S(2)}) collective-permute-start(f32[3,4,128]{2,1,0:T(4,128)S(1)} %get-tuple-element.61), channel_id=1, source_target_pairs={{48,0},{0,16},{16,32},{32,48},{112,64},{64,80},{80,96},{96,112},{1... | collective-permute-start | bytes 18440 | tf_op jit(solution)/shard_map/ppermute | solution.py:63
  191.1 4.5 %collective-permute-start.21 = (f32[3,4,128]{2,1,0:T(4,128)S(1)}, f32[3,4,128]{2,1,0:T(4,128)S(1)}, u32[]{:S(2)}, u32[]{:S(2)}) collective-permute-start(f32[3,4,128]{2,1,0:T(4,128)S(1)} %get-tuple-element.61), channel_id=1, source_target_pairs={{32,0},{48,16},{0,32},{16,48},{96,64},{112,80},{64,96},{80,112},{1... | collective-permute-start | bytes 18440 | tf_op jit(solution)/shard_map/ppermute | solution.py:63
  195.5 1.9 collective-permute-start.20
  197.5 2.8 %collective-permute-start.19 = (f32[3,1,3,128]{3,2,1,0:T(4,128)S(1)}, f32[3,1,3,128]{3,2,1,0:T(4,128)S(1)}, u32[]{:S(2)}, u32[]{:S(2)}) collective-permute-start(f32[3,1,3,128]{3,2,1,0:T(4,128)S(1)} %pad_maximum_fusion.7), channel_id=1, source_target_pairs={{16,0},{32,16},{48,32},{64,48},{80,64},{96,80},{112,96},{128,112},... | collective-permute-start | bytes 13832 | tf_op jit(solution)/shard_map/ppermute | solution.py:19
  200.5 0.6 fusion.160
  201.1 17.8 %collective-permute-done.19 = f32[3,1,3,128]{3,2,1,0:T(4,128)S(1)} collective-permute-done((f32[3,1,3,128]{3,2,1,0:T(4,128)S(1)}, f32[3,1,3,128]{3,2,1,0:T(4,128)S(1)}, u32[]{:S(2)}, u32[]{:S(2)}) %collective-permute-start.19) | collective-permute-done | bytes 4640 | tf_op jit(solution)/shard_map/ppermute | solution.py:19
  218.9 0.7 maximum_bitcast_fusion.5
  219.6 0.7 maximum_bitcast_fusion.6
  220.3 0.7 maximum_bitcast_fusion.7
  220.9 0.6 gather_fusion
  221.5 3.5 %collective-permute-start.25 = (f32[3,4,128]{2,1,0:T(4,128)S(1)}, f32[3,4,128]{2,1,0:T(4,128)S(1)}, u32[]{:S(2)}, u32[]{:S(2)}) collective-permute-start(f32[3,4,128]{2,1,0:T(4,128)S(1)} %fusion.235), channel_id=1, source_target_pairs={{192,0},{208,16},{224,32},{240,48},{0,64},{16,80},{32,96},{48,112}... | collective-permute-start | bytes 18440 | tf_op jit(solution)/shard_map/ppermute | solution.py:63
  225.0 3.5 %collective-permute-start.24 = (f32[3,4,128]{2,1,0:T(4,128)S(1)}, f32[3,4,128]{2,1,0:T(4,128)S(1)}, u32[]{:S(2)}, u32[]{:S(2)}) collective-permute-start(f32[3,4,128]{2,1,0:T(4,128)S(1)} %fusion.235), channel_id=1, source_target_pairs={{128,0},{144,16},{160,32},{176,48},{192,64},{208,80},{224,96},{240... | collective-permute-start | bytes 18440 | tf_op jit(solution)/shard_map/ppermute | solution.py:63
  228.6 2.7 %collective-permute-start.23 = (f32[3,4,128]{2,1,0:T(4,128)S(1)}, f32[3,4,128]{2,1,0:T(4,128)S(1)}, u32[]{:S(2)}, u32[]{:S(2)}) collective-permute-start(f32[3,4,128]{2,1,0:T(4,128)S(1)} %fusion.235), channel_id=1, source_target_pairs={{64,0},{80,16},{96,32},{112,48},{128,64},{144,80},{160,96},{176,11... | collective-permute-start | bytes 18440 | tf_op jit(solution)/shard_map/ppermute | solution.py:63
  231.4 2.7 %collective-permute-done.23 = f32[3,4,128]{2,1,0:T(4,128)S(1)} collective-permute-done((f32[3,4,128]{2,1,0:T(4,128)S(1)}, f32[3,4,128]{2,1,0:T(4,128)S(1)}, u32[]{:S(2)}, u32[]{:S(2)}) %collective-permute-start.23) | collective-permute-done | bytes 6176 | tf_op jit(solution)/shard_map/ppermute | solution.py:63
  234.1 0.6 gather_fusion.1
  234.7 1.9 collective-permute-start.28
  236.7 1.9 collective-permute-start.27
  238.6 7.8 %collective-permute-start.26 = (f32[3,4,128]{2,1,0:T(4,128)S(1)}, f32[3,4,128]{2,1,0:T(4,128)S(1)}, u32[]{:S(2)}, u32[]{:S(2)}) collective-permute-start(f32[3,4,128]{2,1,0:T(4,128)S(1)} %fusion.234), channel_id=1, source_target_pairs={{256,0},{272,16},{288,32},{304,48},{320,64},{336,80},{352,96},{368... | collective-permute-start | bytes 18440 | tf_op jit(solution)/shard_map/ppermute | solution.py:63
  246.4 4.4 %collective-permute-done.27 = f32[3,4,128]{2,1,0:T(4,128)S(1)} collective-permute-done((f32[3,4,128]{2,1,0:T(4,128)S(1)}, f32[3,4,128]{2,1,0:T(4,128)S(1)}, u32[]{:S(2)}, u32[]{:S(2)}) %collective-permute-start.27) | collective-permute-done | bytes 6176 | tf_op jit(solution)/shard_map/ppermute | solution.py:63
  250.9 2.5 collective-permute-done.26
  253.4 0.6 gather_fusion.2
  254.0 0.6 fusion.154
  (243 shorter events, 32.5 us)
Async XLA Ops:
  7.2 110.5 %copy-start = (bf16[128,2048]{1,0:T(8,128)(2,1)S(1)}, bf16[128,2048]{1,0:T(8,128)(2,1)}, u32[]{:S(2)}) copy-start(bf16[128,2048]{1,0:T(8,128)(2,1)} %param.18) | copy-start | bytes 1572868
  7.2 110.4 %all-gather.2.cloned.1.call-start = ((), (), s32[]{:S(2)}) async-start(), calls=%async_computation | async-start | bytes 1114112 | tf_op jit(solution)/shard_map/all_gather | solution.py:159
  8.7 6.7 %collective-permute-start = (bf16[3,3,128]{2,1,0:T(4,128)(2,1)S(1)}, bf16[3,3,128]{2,1,0:T(4,128)(2,1)S(1)}, u32[]{:S(2)}, u32[]{:S(2)}) collective-permute-start(bf16[3,3,128]{2,1,0:T(4,128)(2,1)S(1)} %pad_maximum_fusion.8), channel_id=1, source_target_pairs={{0,16},{16,32},{32,48},{48,64},{64,80},{80,96},{96,112},{112,128},... | collective-permute-start | bytes 6920 | tf_op jit(solution)/shard_map/ppermute | solution.py:19
  13.0 0.7 copy-start.4
  13.1 2.4 copy-start.1
  13.9 0.7 copy-start.5
  15.8 20.1 %copy-start.2 = (bf16[256,128]{1,0:T(8,128)(2,1)S(1)}, bf16[256,128]{1,0:T(8,128)(2,1)}, u32[]{:S(2)}) copy-start(bf16[256,128]{1,0:T(8,128)(2,1)} %param.15) | copy-start | bytes 196612
  39.6 11.7 %copy-start.3 = (bf16[256,128]{1,0:T(8,128)(2,1)S(1)}, bf16[256,128]{1,0:T(8,128)(2,1)}, u32[]{:S(2)}) copy-start(bf16[256,128]{1,0:T(8,128)(2,1)} %param.13) | copy-start | bytes 196612
  39.7 11.7 %collective-permute-start.1 = (f32[2,1,128,128]{2,3,1,0:T(8,128)S(1)}, f32[2,1,128,128]{2,3,1,0:T(8,128)S(1)}, u32[]{:S(2)}, u32[]{:S(2)}) collective-permute-start(f32[2,1,128,128]{2,3,1,0:T(8,128)S(1)} %pad_maximum_fusion), channel_id=1, source_target_pairs={{0,16},{16,32},{32,48},{48,64},{64,80},{80,96},{96,112},{112,128},... | collective-permute-start | bytes 393224 | tf_op jit(solution)/shard_map/ppermute | solution.py:19
  44.7 11.8 %collective-permute-start.2 = (f32[2,1,128,128]{2,3,1,0:T(8,128)S(1)}, f32[2,1,128,128]{2,3,1,0:T(8,128)S(1)}, u32[]{:S(2)}, u32[]{:S(2)}) collective-permute-start(f32[2,1,128,128]{2,3,1,0:T(8,128)S(1)} %pad_maximum_fusion), channel_id=1, source_target_pairs={{0,32},{16,48},{32,64},{48,80},{64,96},{80,112},{96,128},{112,144}... | collective-permute-start | bytes 393224 | tf_op jit(solution)/shard_map/ppermute | solution.py:19
  47.1 11.2 %collective-permute-start.3 = (f32[2,1,128,128]{2,3,1,0:T(8,128)S(1)}, f32[2,1,128,128]{2,3,1,0:T(8,128)S(1)}, u32[]{:S(2)}, u32[]{:S(2)}) collective-permute-start(f32[2,1,128,128]{2,3,1,0:T(8,128)S(1)} %pad_maximum_fusion), channel_id=1, source_target_pairs={{0,48},{16,64},{32,80},{48,96},{64,112},{80,128},{96,144},{112,160... | collective-permute-start | bytes 393224 | tf_op jit(solution)/shard_map/ppermute | solution.py:19
  58.8 18.9 %collective-permute-start.4 = (f32[2,1,128,128]{2,3,1,0:T(8,128)S(1)}, f32[2,1,128,128]{2,3,1,0:T(8,128)S(1)}, u32[]{:S(2)}, u32[]{:S(2)}) collective-permute-start(f32[2,1,128,128]{2,3,1,0:T(8,128)S(1)} %maximum_select_fusion.4), channel_id=1, source_target_pairs={{0,64},{16,80},{32,96},{48,112},{64,128},{80,144},{96,160},{112,17... | collective-permute-start | bytes 393224 | tf_op jit(solution)/shard_map/ppermute | solution.py:19
  60.6 17.5 %collective-permute-start.5 = (f32[2,1,128,128]{2,3,1,0:T(8,128)S(1)}, f32[2,1,128,128]{2,3,1,0:T(8,128)S(1)}, u32[]{:S(2)}, u32[]{:S(2)}) collective-permute-start(f32[2,1,128,128]{2,3,1,0:T(8,128)S(1)} %maximum_select_fusion.4), channel_id=1, source_target_pairs={{0,128},{16,144},{32,160},{48,176},{64,192},{80,208},{96,224},{112... | collective-permute-start | bytes 393224 | tf_op jit(solution)/shard_map/ppermute | solution.py:19
  68.9 10.0 %collective-permute-start.6 = (f32[2,1,128,128]{2,3,1,0:T(8,128)S(1)}, f32[2,1,128,128]{2,3,1,0:T(8,128)S(1)}, u32[]{:S(2)}, u32[]{:S(2)}) collective-permute-start(f32[2,1,128,128]{2,3,1,0:T(8,128)S(1)} %maximum_select_fusion.4), channel_id=1, source_target_pairs={{0,192},{16,208},{32,224},{48,240},{64,256},{80,272},{96,288},{112... | collective-permute-start | bytes 393224 | tf_op jit(solution)/shard_map/ppermute | solution.py:19
  79.3 36.0 %collective-permute-start.9 = (f32[2,1,128,128]{2,3,1,0:T(8,128)S(1)}, f32[2,1,128,128]{2,3,1,0:T(8,128)S(1)}, u32[]{:S(2)}, u32[]{:S(2)}) collective-permute-start(f32[2,1,128,128]{2,3,1,0:T(8,128)S(1)} %maximum_select_fusion.10), channel_id=1, source_target_pairs={{0,768},{16,784},{32,800},{48,816},{64,832},{80,848},{96,864},{112... | collective-permute-start | bytes 393224 | tf_op jit(solution)/shard_map/ppermute | solution.py:19
  96.6 10.2 %collective-permute-start.7 = (f32[2,1,128,128]{2,3,1,0:T(8,128)S(1)}, f32[2,1,128,128]{2,3,1,0:T(8,128)S(1)}, u32[]{:S(2)}, u32[]{:S(2)}) collective-permute-start(f32[2,1,128,128]{2,3,1,0:T(8,128)S(1)} %maximum_select_fusion.10), channel_id=1, source_target_pairs={{0,256},{16,272},{32,288},{48,304},{64,320},{80,336},{96,352},{112... | collective-permute-start | bytes 393224 | tf_op jit(solution)/shard_map/ppermute | solution.py:19
  97.9 9.8 %collective-permute-start.8 = (f32[2,1,128,128]{2,3,1,0:T(8,128)S(1)}, f32[2,1,128,128]{2,3,1,0:T(8,128)S(1)}, u32[]{:S(2)}, u32[]{:S(2)}) collective-permute-start(f32[2,1,128,128]{2,3,1,0:T(8,128)S(1)} %maximum_select_fusion.10), channel_id=1, source_target_pairs={{0,512},{16,528},{32,544},{48,560},{64,576},{80,592},{96,608},{112... | collective-permute-start | bytes 393224 | tf_op jit(solution)/shard_map/ppermute | solution.py:19
  126.1 10.9 %collective-permute-start.10 = (f32[2,1,128,128]{2,3,1,0:T(8,128)S(1)}, f32[2,1,128,128]{2,3,1,0:T(8,128)S(1)}, u32[]{:S(2)}, u32[]{:S(2)}) collective-permute-start(f32[2,1,128,128]{2,3,1,0:T(8,128)S(1)} %pad_maximum_fusion.1), channel_id=1, source_target_pairs={{16,0},{32,16},{48,32},{64,48},{80,64},{96,80},{112,96},{128,112},... | collective-permute-start | bytes 393224 | tf_op jit(solution)/shard_map/ppermute | solution.py:19
  128.0 10.5 %collective-permute-start.11 = (f32[2,1,128,128]{2,3,1,0:T(8,128)S(1)}, f32[2,1,128,128]{2,3,1,0:T(8,128)S(1)}, u32[]{:S(2)}, u32[]{:S(2)}) collective-permute-start(f32[2,1,128,128]{2,3,1,0:T(8,128)S(1)} %pad_maximum_fusion.1), channel_id=1, source_target_pairs={{32,0},{48,16},{64,32},{80,48},{96,64},{112,80},{128,96},{144,112}... | collective-permute-start | bytes 393224 | tf_op jit(solution)/shard_map/ppermute | solution.py:19
  129.9 9.9 %collective-permute-start.12 = (f32[2,1,128,128]{2,3,1,0:T(8,128)S(1)}, f32[2,1,128,128]{2,3,1,0:T(8,128)S(1)}, u32[]{:S(2)}, u32[]{:S(2)}) collective-permute-start(f32[2,1,128,128]{2,3,1,0:T(8,128)S(1)} %pad_maximum_fusion.1), channel_id=1, source_target_pairs={{48,0},{64,16},{80,32},{96,48},{112,64},{128,80},{144,96},{160,112... | collective-permute-start | bytes 393224 | tf_op jit(solution)/shard_map/ppermute | solution.py:19
  140.3 8.2 %collective-permute-start.13 = (f32[2,1,128,128]{2,3,1,0:T(8,128)S(1)}, f32[2,1,128,128]{2,3,1,0:T(8,128)S(1)}, u32[]{:S(2)}, u32[]{:S(2)}) collective-permute-start(f32[2,1,128,128]{2,3,1,0:T(8,128)S(1)} %maximum_select_fusion.17), channel_id=1, source_target_pairs={{64,0},{80,16},{96,32},{112,48},{128,64},{144,80},{160,96},{176,11... | collective-permute-start | bytes 393224 | tf_op jit(solution)/shard_map/ppermute | solution.py:19
  141.6 12.7 %collective-permute-start.14 = (f32[2,1,128,128]{2,3,1,0:T(8,128)S(1)}, f32[2,1,128,128]{2,3,1,0:T(8,128)S(1)}, u32[]{:S(2)}, u32[]{:S(2)}) collective-permute-start(f32[2,1,128,128]{2,3,1,0:T(8,128)S(1)} %maximum_select_fusion.17), channel_id=1, source_target_pairs={{128,0},{144,16},{160,32},{176,48},{192,64},{208,80},{224,96},{240... | collective-permute-start | bytes 393224 | tf_op jit(solution)/shard_map/ppermute | solution.py:19
  142.9 17.2 %collective-permute-start.15 = (f32[2,1,128,128]{2,3,1,0:T(8,128)S(1)}, f32[2,1,128,128]{2,3,1,0:T(8,128)S(1)}, u32[]{:S(2)}, u32[]{:S(2)}) collective-permute-start(f32[2,1,128,128]{2,3,1,0:T(8,128)S(1)} %maximum_select_fusion.17), channel_id=1, source_target_pairs={{192,0},{208,16},{224,32},{240,48},{256,64},{272,80},{288,96},{304... | collective-permute-start | bytes 393224 | tf_op jit(solution)/shard_map/ppermute | solution.py:19
  160.6 18.8 %collective-permute-start.18 = (f32[2,1,128,128]{2,3,1,0:T(8,128)S(1)}, f32[2,1,128,128]{2,3,1,0:T(8,128)S(1)}, u32[]{:S(2)}, u32[]{:S(2)}) collective-permute-start(f32[2,1,128,128]{2,3,1,0:T(8,128)S(1)} %maximum_select_fusion.23), channel_id=1, source_target_pairs={{768,0},{784,16},{800,32},{816,48},{832,64},{848,80},{864,96},{880... | collective-permute-start | bytes 393224 | tf_op jit(solution)/shard_map/ppermute | solution.py:19
  161.9 12.6 %collective-permute-start.16 = (f32[2,1,128,128]{2,3,1,0:T(8,128)S(1)}, f32[2,1,128,128]{2,3,1,0:T(8,128)S(1)}, u32[]{:S(2)}, u32[]{:S(2)}) collective-permute-start(f32[2,1,128,128]{2,3,1,0:T(8,128)S(1)} %maximum_select_fusion.23), channel_id=1, source_target_pairs={{256,0},{272,16},{288,32},{304,48},{320,64},{336,80},{352,96},{368... | collective-permute-start | bytes 393224 | tf_op jit(solution)/shard_map/ppermute | solution.py:19
  163.2 15.7 %collective-permute-start.17 = (f32[2,1,128,128]{2,3,1,0:T(8,128)S(1)}, f32[2,1,128,128]{2,3,1,0:T(8,128)S(1)}, u32[]{:S(2)}, u32[]{:S(2)}) collective-permute-start(f32[2,1,128,128]{2,3,1,0:T(8,128)S(1)} %maximum_select_fusion.23), channel_id=1, source_target_pairs={{512,0},{528,16},{544,32},{560,48},{576,64},{592,80},{608,96},{624... | collective-permute-start | bytes 393224 | tf_op jit(solution)/shard_map/ppermute | solution.py:19
  186.9 34.0 %collective-permute-start.22 = (f32[3,4,128]{2,1,0:T(4,128)S(1)}, f32[3,4,128]{2,1,0:T(4,128)S(1)}, u32[]{:S(2)}, u32[]{:S(2)}) collective-permute-start(f32[3,4,128]{2,1,0:T(4,128)S(1)} %get-tuple-element.61), channel_id=1, source_target_pairs={{48,0},{0,16},{16,32},{32,48},{112,64},{64,80},{80,96},{96,112},{1... | collective-permute-start | bytes 18440 | tf_op jit(solution)/shard_map/ppermute | solution.py:63
  191.1 29.9 %collective-permute-start.21 = (f32[3,4,128]{2,1,0:T(4,128)S(1)}, f32[3,4,128]{2,1,0:T(4,128)S(1)}, u32[]{:S(2)}, u32[]{:S(2)}) collective-permute-start(f32[3,4,128]{2,1,0:T(4,128)S(1)} %get-tuple-element.61), channel_id=1, source_target_pairs={{32,0},{48,16},{0,32},{16,48},{96,64},{112,80},{64,96},{80,112},{1... | collective-permute-start | bytes 18440 | tf_op jit(solution)/shard_map/ppermute | solution.py:63
  195.5 25.4 %collective-permute-start.20 = (f32[3,4,128]{2,1,0:T(4,128)S(1)}, f32[3,4,128]{2,1,0:T(4,128)S(1)}, u32[]{:S(2)}, u32[]{:S(2)}) collective-permute-start(f32[3,4,128]{2,1,0:T(4,128)S(1)} %get-tuple-element.61), channel_id=1, source_target_pairs={{16,0},{32,16},{48,32},{0,48},{80,64},{96,80},{112,96},{64,112},{1... | collective-permute-start | bytes 18440 | tf_op jit(solution)/shard_map/ppermute | solution.py:63
  197.5 21.4 %collective-permute-start.19 = (f32[3,1,3,128]{3,2,1,0:T(4,128)S(1)}, f32[3,1,3,128]{3,2,1,0:T(4,128)S(1)}, u32[]{:S(2)}, u32[]{:S(2)}) collective-permute-start(f32[3,1,3,128]{3,2,1,0:T(4,128)S(1)} %pad_maximum_fusion.7), channel_id=1, source_target_pairs={{16,0},{32,16},{48,32},{64,48},{80,64},{96,80},{112,96},{128,112},... | collective-permute-start | bytes 13832 | tf_op jit(solution)/shard_map/ppermute | solution.py:19
  221.5 9.7 %collective-permute-start.25 = (f32[3,4,128]{2,1,0:T(4,128)S(1)}, f32[3,4,128]{2,1,0:T(4,128)S(1)}, u32[]{:S(2)}, u32[]{:S(2)}) collective-permute-start(f32[3,4,128]{2,1,0:T(4,128)S(1)} %fusion.235), channel_id=1, source_target_pairs={{192,0},{208,16},{224,32},{240,48},{0,64},{16,80},{32,96},{48,112}... | collective-permute-start | bytes 18440 | tf_op jit(solution)/shard_map/ppermute | solution.py:63
  225.0 6.4 %collective-permute-start.24 = (f32[3,4,128]{2,1,0:T(4,128)S(1)}, f32[3,4,128]{2,1,0:T(4,128)S(1)}, u32[]{:S(2)}, u32[]{:S(2)}) collective-permute-start(f32[3,4,128]{2,1,0:T(4,128)S(1)} %fusion.235), channel_id=1, source_target_pairs={{128,0},{144,16},{160,32},{176,48},{192,64},{208,80},{224,96},{240... | collective-permute-start | bytes 18440 | tf_op jit(solution)/shard_map/ppermute | solution.py:63
  228.6 5.6 %collective-permute-start.23 = (f32[3,4,128]{2,1,0:T(4,128)S(1)}, f32[3,4,128]{2,1,0:T(4,128)S(1)}, u32[]{:S(2)}, u32[]{:S(2)}) collective-permute-start(f32[3,4,128]{2,1,0:T(4,128)S(1)} %fusion.235), channel_id=1, source_target_pairs={{64,0},{80,16},{96,32},{112,48},{128,64},{144,80},{160,96},{176,11... | collective-permute-start | bytes 18440 | tf_op jit(solution)/shard_map/ppermute | solution.py:63
  234.7 11.7 %collective-permute-start.28 = (f32[3,4,128]{2,1,0:T(4,128)S(1)}, f32[3,4,128]{2,1,0:T(4,128)S(1)}, u32[]{:S(2)}, u32[]{:S(2)}) collective-permute-start(f32[3,4,128]{2,1,0:T(4,128)S(1)} %fusion.234), channel_id=1, source_target_pairs={{768,0},{784,16},{800,32},{816,48},{832,64},{848,80},{864,96},{880... | collective-permute-start | bytes 18440 | tf_op jit(solution)/shard_map/ppermute | solution.py:63
  236.7 14.2 %collective-permute-start.27 = (f32[3,4,128]{2,1,0:T(4,128)S(1)}, f32[3,4,128]{2,1,0:T(4,128)S(1)}, u32[]{:S(2)}, u32[]{:S(2)}) collective-permute-start(f32[3,4,128]{2,1,0:T(4,128)S(1)} %fusion.234), channel_id=1, source_target_pairs={{512,0},{528,16},{544,32},{560,48},{576,64},{592,80},{608,96},{624... | collective-permute-start | bytes 18440 | tf_op jit(solution)/shard_map/ppermute | solution.py:63
  238.6 14.8 %collective-permute-start.26 = (f32[3,4,128]{2,1,0:T(4,128)S(1)}, f32[3,4,128]{2,1,0:T(4,128)S(1)}, u32[]{:S(2)}, u32[]{:S(2)}) collective-permute-start(f32[3,4,128]{2,1,0:T(4,128)S(1)} %fusion.234), channel_id=1, source_target_pairs={{256,0},{272,16},{288,32},{304,48},{320,64},{336,80},{352,96},{368... | collective-permute-start | bytes 18440 | tf_op jit(solution)/shard_map/ppermute | solution.py:63
Sparse Core Ops, SparseCore 0:
  13.0 52.3 all-gather.1

commit v6 on v5

--- a/solution.py
+++ b/solution.py
@@ -50,7 +50,7 @@
     place = lax.axis_index(axis)
     distance = 1
     while distance < count:
-        radix = 4 if (count // distance) % 4 == 0 else 2
+        radix = 2
         if (count // distance) % radix:
             return lax.psum(part, axis)
         digit = (place // distance) % radix

time: 264 us -> 267 us (1.011)
  starting transfers between devices: 108 us -> 100 us
  waiting for transfers between devices: 74 us -> 81.7 us
    ppermute x9 -> x6, waiting for transfers between devices: 9.83 us -> 26.3 us  [summed(): got.append(lax.ppermute(part, axis, route))]
    ppermute x20, waiting for transfers between devices: 64.1 us -> 55.4 us  [passed_along(): return lax.ppermute(block, axis, route)]
    ppermute x9 -> x6, starting transfers between devices: 31.9 us -> 24.5 us  [summed(): got.append(lax.ppermute(part, axis, route))]
  transfers between devices with their start and end apart: 30 -> 27, of which waited for: 18 -> 19; matrix products, arithmetic and copies ran while one was open for 16% -> 16% of each run, Pallas kernels for 0% -> 0%
where the time goes in v6:
time: 267 us; the launch traced here: 263 us
  starting transfers between devices  100 us (37%)
  waiting for transfers between devices  81.7 us (31%)
  matrix products  32.2 us (12%)
  other arithmetic  26.8 us (10%)
  between operations  16 us (6%)
  local copies, waits for them, and re-layouts  6.56 us (2%)
    ppermute x20, starting transfers between devices, passed_along(): return lax.ppermute(block, axis, route)  75.7 us
    ppermute x20, waiting for transfers between devices, passed_along(): return lax.ppermute(block, axis, route)  55.4 us
    ppermute x6, waiting for transfers between devices, summed(): got.append(lax.ppermute(part, axis, route))  26.3 us
    ppermute x6, starting transfers between devices, summed(): got.append(lax.ppermute(part, axis, route))  24.5 us
    another operation x3, other arithmetic, wy_factors(): jax.scipy.linalg.solve_triangular(system, weighted, lower=True, unit_diag...  19.7 us
    dot_general x30, matrix products, combine_pairs(): offset_term = jnp.matmul(later[0], earlier[1], precision=HIGHEST) + later[1]  6.21 us
    dot_general x30, matrix products, combine_pairs(): product = jnp.matmul(later[0], earlier[0], precision=HIGHEST)  6.2 us
  transfers between devices with their start and end apart: 27, of which 19 were waited for; matrix products, arithmetic and copies ran while one was open for 16% of the time, Pallas kernels for 0%

profile of v6, /device:TPU:6, one launch (start us, length us, event | category | flops | bytes accessed | tf_op | source)
XLA Modules:
  0.0 263.4 jit_solution(14986560541014356837)
XLA Ops:
  7.2 0.7 slice_bitcast_fusion.271
  8.0 0.7 slice_bitcast_fusion.269
  8.7 4.2 %collective-permute-start = (bf16[3,3,128]{2,1,0:T(4,128)(2,1)S(1)}, bf16[3,3,128]{2,1,0:T(4,128)(2,1)S(1)}, u32[]{:S(2)}, u32[]{:S(2)}) collective-permute-start(bf16[3,3,128]{2,1,0:T(4,128)(2,1)S(1)} %pad_maximum_fusion.11), channel_id=1, source_target_pairs={{0,16},{16,32},{32,48},{48,64},{64,80},{80,96},{96,112},{112,128},... | collective-permute-start | bytes 6920 | tf_op jit(solution)/shard_map/ppermute | solution.py:19
  13.1 0.7 copy-done.4
  14.1 0.5 broadcast.879
  14.8 0.7 fusion.182
  16.4 19.7 %custom-call.10 = f32[1,4,1,64,64]{3,4,2,1,0:T(8,128)S(1)} custom-call(f32[1,4,1,64,64]{4,3,2,1,0:T(8,128)S(1)} %fusion.16), custom_call_target="InvertDiagBlocksLowerTriangular" | custom-call | tf_op jit(solution)/shard_map/jvp(vmap(vmap(jit(_solve_triangular))))/triangular_solve | solution.py:88
  36.2 0.4 fusion.73
  36.6 0.6 convolution_bitcast_fusion
  37.7 0.6 fusion
  39.8 4.8 %collective-permute-start.1 = (f32[2,1,128,128]{2,3,1,0:T(8,128)S(1)}, f32[2,1,128,128]{2,3,1,0:T(8,128)S(1)}, u32[]{:S(2)}, u32[]{:S(2)}) collective-permute-start(f32[2,1,128,128]{2,3,1,0:T(8,128)S(1)} %pad_maximum_fusion), channel_id=1, source_target_pairs={{0,16},{16,32},{32,48},{48,64},{64,80},{80,96},{96,112},{112,128},... | collective-permute-start | bytes 393224 | tf_op jit(solution)/shard_map/ppermute | solution.py:19
  44.7 2.6 collective-permute-start.2
  47.3 3.9 %collective-permute-start.3 = (f32[2,1,128,128]{2,3,1,0:T(8,128)S(1)}, f32[2,1,128,128]{2,3,1,0:T(8,128)S(1)}, u32[]{:S(2)}, u32[]{:S(2)}) collective-permute-start(f32[2,1,128,128]{2,3,1,0:T(8,128)S(1)} %pad_maximum_fusion), channel_id=1, source_target_pairs={{0,48},{16,64},{32,80},{48,96},{64,112},{80,128},{96,144},{112,160... | collective-permute-start | bytes 393224 | tf_op jit(solution)/shard_map/ppermute | solution.py:19
  52.0 4.5 %collective-permute-done.2 = f32[2,1,128,128]{2,3,1,0:T(8,128)S(1)} collective-permute-done((f32[2,1,128,128]{2,3,1,0:T(8,128)S(1)}, f32[2,1,128,128]{2,3,1,0:T(8,128)S(1)}, u32[]{:S(2)}, u32[]{:S(2)}) %collective-permute-start.2) | collective-permute-done | bytes 131104 | tf_op jit(solution)/shard_map/ppermute | solution.py:19
  56.9 1.4 collective-permute-done.3
  58.8 1.8 collective-permute-start.4
  60.6 8.4 %collective-permute-start.5 = (f32[2,1,128,128]{2,3,1,0:T(8,128)S(1)}, f32[2,1,128,128]{2,3,1,0:T(8,128)S(1)}, u32[]{:S(2)}, u32[]{:S(2)}) collective-permute-start(f32[2,1,128,128]{2,3,1,0:T(8,128)S(1)} %maximum_select_fusion.4), channel_id=1, source_target_pairs={{0,128},{16,144},{32,160},{48,176},{64,192},{80,208},{96,224},{112... | collective-permute-start | bytes 393224 | tf_op jit(solution)/shard_map/ppermute | solution.py:19
  69.1 7.3 %collective-permute-start.6 = (f32[2,1,128,128]{2,3,1,0:T(8,128)S(1)}, f32[2,1,128,128]{2,3,1,0:T(8,128)S(1)}, u32[]{:S(2)}, u32[]{:S(2)}) collective-permute-start(f32[2,1,128,128]{2,3,1,0:T(8,128)S(1)} %maximum_select_fusion.4), channel_id=1, source_target_pairs={{0,192},{16,208},{32,224},{48,240},{64,256},{80,272},{96,288},{112... | collective-permute-start | bytes 393224 | tf_op jit(solution)/shard_map/ppermute | solution.py:19
  79.3 17.3 %collective-permute-start.9 = (f32[2,1,128,128]{2,3,1,0:T(8,128)S(1)}, f32[2,1,128,128]{2,3,1,0:T(8,128)S(1)}, u32[]{:S(2)}, u32[]{:S(2)}) collective-permute-start(f32[2,1,128,128]{2,3,1,0:T(8,128)S(1)} %maximum_select_fusion.10), channel_id=1, source_target_pairs={{0,768},{16,784},{32,800},{48,816},{64,832},{80,848},{96,864},{112... | collective-permute-start | bytes 393224 | tf_op jit(solution)/shard_map/ppermute | solution.py:19
  96.6 1.3 collective-permute-start.7
  97.9 7.5 %collective-permute-start.8 = (f32[2,1,128,128]{2,3,1,0:T(8,128)S(1)}, f32[2,1,128,128]{2,3,1,0:T(8,128)S(1)}, u32[]{:S(2)}, u32[]{:S(2)}) collective-permute-start(f32[2,1,128,128]{2,3,1,0:T(8,128)S(1)} %maximum_select_fusion.10), channel_id=1, source_target_pairs={{0,512},{16,528},{32,544},{48,560},{64,576},{80,592},{96,608},{112... | collective-permute-start | bytes 393224 | tf_op jit(solution)/shard_map/ppermute | solution.py:19
  108.2 7.1 %collective-permute-done.9 = f32[2,1,128,128]{2,3,1,0:T(8,128)S(1)} collective-permute-done((f32[2,1,128,128]{2,3,1,0:T(8,128)S(1)}, f32[2,1,128,128]{2,3,1,0:T(8,128)S(1)}, u32[]{:S(2)}, u32[]{:S(2)}) %collective-permute-start.9) | collective-permute-done | bytes 131104 | tf_op jit(solution)/shard_map/ppermute | solution.py:19
  117.6 1.7 fusion.184
  126.1 1.9 collective-permute-start.10
  128.0 2.0 collective-permute-start.11
  130.0 1.9 collective-permute-start.12
  132.1 4.9 %collective-permute-done.10 = f32[2,1,128,128]{2,3,1,0:T(8,128)S(1)} collective-permute-done((f32[2,1,128,128]{2,3,1,0:T(8,128)S(1)}, f32[2,1,128,128]{2,3,1,0:T(8,128)S(1)}, u32[]{:S(2)}, u32[]{:S(2)}) %collective-permute-start.10) | collective-permute-done | bytes 131104 | tf_op jit(solution)/shard_map/ppermute | solution.py:19
  137.5 1.1 collective-permute-done.11
  139.0 0.9 collective-permute-done.12
  140.4 1.3 collective-permute-start.13
  141.7 1.3 collective-permute-start.14
  143.0 1.3 collective-permute-start.15
  145.6 2.2 collective-permute-done.13
  148.3 5.6 %collective-permute-done.14 = f32[2,1,128,128]{2,3,1,0:T(8,128)S(1)} collective-permute-done((f32[2,1,128,128]{2,3,1,0:T(8,128)S(1)}, f32[2,1,128,128]{2,3,1,0:T(8,128)S(1)}, u32[]{:S(2)}, u32[]{:S(2)}) %collective-permute-start.14) | collective-permute-done | bytes 131104 | tf_op jit(solution)/shard_map/ppermute | solution.py:19
  154.4 6.1 %collective-permute-done.15 = f32[2,1,128,128]{2,3,1,0:T(8,128)S(1)} collective-permute-done((f32[2,1,128,128]{2,3,1,0:T(8,128)S(1)}, f32[2,1,128,128]{2,3,1,0:T(8,128)S(1)}, u32[]{:S(2)}, u32[]{:S(2)}) %collective-permute-start.15) | collective-permute-done | bytes 131104 | tf_op jit(solution)/shard_map/ppermute | solution.py:19
  161.0 1.3 collective-permute-start.18
  162.3 1.3 collective-permute-start.16
  163.6 1.5 collective-permute-start.17
  166.6 7.2 %collective-permute-done.16 = f32[2,1,128,128]{2,3,1,0:T(8,128)S(1)} collective-permute-done((f32[2,1,128,128]{2,3,1,0:T(8,128)S(1)}, f32[2,1,128,128]{2,3,1,0:T(8,128)S(1)}, u32[]{:S(2)}, u32[]{:S(2)}) %collective-permute-start.16) | collective-permute-done | bytes 131104 | tf_op jit(solution)/shard_map/ppermute | solution.py:19
  174.3 5.1 %collective-permute-done.17 = f32[2,1,128,128]{2,3,1,0:T(8,128)S(1)} collective-permute-done((f32[2,1,128,128]{2,3,1,0:T(8,128)S(1)}, f32[2,1,128,128]{2,3,1,0:T(8,128)S(1)}, u32[]{:S(2)}, u32[]{:S(2)}) %collective-permute-start.17) | collective-permute-done | bytes 131104 | tf_op jit(solution)/shard_map/ppermute | solution.py:19
  187.5 2.8 %collective-permute-start.19 = (f32[3,1,3,128]{3,2,1,0:T(4,128)S(1)}, f32[3,1,3,128]{3,2,1,0:T(4,128)S(1)}, u32[]{:S(2)}, u32[]{:S(2)}) collective-permute-start(f32[3,1,3,128]{3,2,1,0:T(4,128)S(1)} %pad_maximum_fusion.10), channel_id=1, source_target_pairs={{16,0},{32,16},{48,32},{64,48},{80,64},{96,80},{112,96},{128,112},... | collective-permute-start | bytes 13832 | tf_op jit(solution)/shard_map/ppermute | solution.py:19
  190.4 3.5 %collective-permute-start.20 = (f32[3,4,128]{2,1,0:T(4,128)S(1)}, f32[3,4,128]{2,1,0:T(4,128)S(1)}, u32[]{:S(2)}, u32[]{:S(2)}) collective-permute-start(f32[3,4,128]{2,1,0:T(4,128)S(1)} %get-tuple-element.61), channel_id=1, source_target_pairs={{16,0},{0,16},{48,32},{32,48},{80,64},{64,80},{112,96},{96,112},{1... | collective-permute-start | bytes 18440 | tf_op jit(solution)/shard_map/ppermute | solution.py:63
  194.0 0.6 fusion.157
  194.6 8.5 %collective-permute-done.19 = f32[3,1,3,128]{3,2,1,0:T(4,128)S(1)} collective-permute-done((f32[3,1,3,128]{3,2,1,0:T(4,128)S(1)}, f32[3,1,3,128]{3,2,1,0:T(4,128)S(1)}, u32[]{:S(2)}, u32[]{:S(2)}) %collective-permute-start.19) | collective-permute-done | bytes 4640 | tf_op jit(solution)/shard_map/ppermute | solution.py:19
  203.1 0.7 maximum_bitcast_fusion.5
  203.8 0.7 maximum_bitcast_fusion.6
  204.4 0.7 maximum_bitcast_fusion.7
  205.1 0.6 gather_fusion
  205.7 1.9 collective-permute-start.21
  207.6 5.1 %collective-permute-done.21 = f32[3,4,128]{2,1,0:T(4,128)S(1)} collective-permute-done((f32[3,4,128]{2,1,0:T(4,128)S(1)}, f32[3,4,128]{2,1,0:T(4,128)S(1)}, u32[]{:S(2)}, u32[]{:S(2)}) %collective-permute-start.21) | collective-permute-done | bytes 6176 | tf_op jit(solution)/shard_map/ppermute | solution.py:63
  212.7 0.6 gather_fusion.1
  213.3 8.6 %collective-permute-start.22 = (f32[3,4,128]{2,1,0:T(4,128)S(1)}, f32[3,4,128]{2,1,0:T(4,128)S(1)}, u32[]{:S(2)}, u32[]{:S(2)}) collective-permute-start(f32[3,4,128]{2,1,0:T(4,128)S(1)} %fusion.240), channel_id=1, source_target_pairs={{64,0},{80,16},{96,32},{112,48},{0,64},{16,80},{32,96},{48,112},{1... | collective-permute-start | bytes 18440 | tf_op jit(solution)/shard_map/ppermute | solution.py:63
  221.9 1.6 collective-permute-done.22
  223.5 0.6 gather_fusion.2
  224.1 3.5 %collective-permute-start.23 = (f32[3,4,128]{2,1,0:T(4,128)S(1)}, f32[3,4,128]{2,1,0:T(4,128)S(1)}, u32[]{:S(2)}, u32[]{:S(2)}) collective-permute-start(f32[3,4,128]{2,1,0:T(4,128)S(1)} %fusion.239), channel_id=1, source_target_pairs={{128,0},{144,16},{160,32},{176,48},{192,64},{208,80},{224,96},{240... | collective-permute-start | bytes 18440 | tf_op jit(solution)/shard_map/ppermute | solution.py:63
  227.6 2.9 %collective-permute-done.23 = f32[3,4,128]{2,1,0:T(4,128)S(1)} collective-permute-done((f32[3,4,128]{2,1,0:T(4,128)S(1)}, f32[3,4,128]{2,1,0:T(4,128)S(1)}, u32[]{:S(2)}, u32[]{:S(2)}) %collective-permute-start.23) | collective-permute-done | bytes 6176 | tf_op jit(solution)/shard_map/ppermute | solution.py:63
  230.5 0.6 gather_fusion.3
  231.1 4.0 %collective-permute-start.24 = (f32[3,4,128]{2,1,0:T(4,128)S(1)}, f32[3,4,128]{2,1,0:T(4,128)S(1)}, u32[]{:S(2)}, u32[]{:S(2)}) collective-permute-start(f32[3,4,128]{2,1,0:T(4,128)S(1)} %fusion.238), channel_id=1, source_target_pairs={{256,0},{272,16},{288,32},{304,48},{320,64},{336,80},{352,96},{368... | collective-permute-start | bytes 18440 | tf_op jit(solution)/shard_map/ppermute | solution.py:63
  235.1 5.4 %collective-permute-done.24 = f32[3,4,128]{2,1,0:T(4,128)S(1)} collective-permute-done((f32[3,4,128]{2,1,0:T(4,128)S(1)}, f32[3,4,128]{2,1,0:T(4,128)S(1)}, u32[]{:S(2)}, u32[]{:S(2)}) %collective-permute-start.24) | collective-permute-done | bytes 6176 | tf_op jit(solution)/shard_map/ppermute | solution.py:63
  240.5 0.6 gather_fusion.4
  241.1 3.0 %collective-permute-start.25 = (f32[3,4,128]{2,1,0:T(4,128)S(1)}, f32[3,4,128]{2,1,0:T(4,128)S(1)}, u32[]{:S(2)}, u32[]{:S(2)}) collective-permute-start(f32[3,4,128]{2,1,0:T(4,128)S(1)} %fusion.237), channel_id=1, source_target_pairs={{512,0},{528,16},{544,32},{560,48},{576,64},{592,80},{608,96},{624... | collective-permute-start | bytes 18440 | tf_op jit(solution)/shard_map/ppermute | solution.py:63
  244.1 11.2 %collective-permute-done.25 = f32[3,4,128]{2,1,0:T(4,128)S(1)} collective-permute-done((f32[3,4,128]{2,1,0:T(4,128)S(1)}, f32[3,4,128]{2,1,0:T(4,128)S(1)}, u32[]{:S(2)}, u32[]{:S(2)}) %collective-permute-start.25) | collective-permute-done | bytes 6176 | tf_op jit(solution)/shard_map/ppermute | solution.py:63
  255.3 0.6 gather_fusion.5
  255.9 0.6 fusion.153
  (255 shorter events, 33.3 us)
Async XLA Ops:
  7.2 110.5 %copy-start = (bf16[128,2048]{1,0:T(8,128)(2,1)S(1)}, bf16[128,2048]{1,0:T(8,128)(2,1)}, u32[]{:S(2)}) copy-start(bf16[128,2048]{1,0:T(8,128)(2,1)} %param.18) | copy-start | bytes 1572868
  7.2 110.4 %all-gather.2.cloned.1.call-start = ((), (), s32[]{:S(2)}) async-start(), calls=%async_computation | async-start | bytes 1114112 | tf_op jit(solution)/shard_map/all_gather | solution.py:159
  8.7 6.9 %collective-permute-start = (bf16[3,3,128]{2,1,0:T(4,128)(2,1)S(1)}, bf16[3,3,128]{2,1,0:T(4,128)(2,1)S(1)}, u32[]{:S(2)}, u32[]{:S(2)}) collective-permute-start(bf16[3,3,128]{2,1,0:T(4,128)(2,1)S(1)} %pad_maximum_fusion.11), channel_id=1, source_target_pairs={{0,16},{16,32},{32,48},{48,64},{64,80},{80,96},{96,112},{112,128},... | collective-permute-start | bytes 6920 | tf_op jit(solution)/shard_map/ppermute | solution.py:19
  13.1 0.7 copy-start.4
  13.9 1.7 copy-start.1
  14.1 0.7 copy-start.5
  16.0 20.1 %copy-start.2 = (bf16[256,128]{1,0:T(8,128)(2,1)S(1)}, bf16[256,128]{1,0:T(8,128)(2,1)}, u32[]{:S(2)}) copy-start(bf16[256,128]{1,0:T(8,128)(2,1)} %param.15) | copy-start | bytes 196612
  39.8 11.5 %copy-start.3 = (bf16[256,128]{1,0:T(8,128)(2,1)S(1)}, bf16[256,128]{1,0:T(8,128)(2,1)}, u32[]{:S(2)}) copy-start(bf16[256,128]{1,0:T(8,128)(2,1)} %param.13) | copy-start | bytes 196612
  39.8 11.5 %collective-permute-start.1 = (f32[2,1,128,128]{2,3,1,0:T(8,128)S(1)}, f32[2,1,128,128]{2,3,1,0:T(8,128)S(1)}, u32[]{:S(2)}, u32[]{:S(2)}) collective-permute-start(f32[2,1,128,128]{2,3,1,0:T(8,128)S(1)} %pad_maximum_fusion), channel_id=1, source_target_pairs={{0,16},{16,32},{32,48},{48,64},{64,80},{80,96},{96,112},{112,128},... | collective-permute-start | bytes 393224 | tf_op jit(solution)/shard_map/ppermute | solution.py:19
  44.7 11.8 %collective-permute-start.2 = (f32[2,1,128,128]{2,3,1,0:T(8,128)S(1)}, f32[2,1,128,128]{2,3,1,0:T(8,128)S(1)}, u32[]{:S(2)}, u32[]{:S(2)}) collective-permute-start(f32[2,1,128,128]{2,3,1,0:T(8,128)S(1)} %pad_maximum_fusion), channel_id=1, source_target_pairs={{0,32},{16,48},{32,64},{48,80},{64,96},{80,112},{96,128},{112,144}... | collective-permute-start | bytes 393224 | tf_op jit(solution)/shard_map/ppermute | solution.py:19
  47.3 11.1 %collective-permute-start.3 = (f32[2,1,128,128]{2,3,1,0:T(8,128)S(1)}, f32[2,1,128,128]{2,3,1,0:T(8,128)S(1)}, u32[]{:S(2)}, u32[]{:S(2)}) collective-permute-start(f32[2,1,128,128]{2,3,1,0:T(8,128)S(1)} %pad_maximum_fusion), channel_id=1, source_target_pairs={{0,48},{16,64},{32,80},{48,96},{64,112},{80,128},{96,144},{112,160... | collective-permute-start | bytes 393224 | tf_op jit(solution)/shard_map/ppermute | solution.py:19
  58.8 18.9 %collective-permute-start.4 = (f32[2,1,128,128]{2,3,1,0:T(8,128)S(1)}, f32[2,1,128,128]{2,3,1,0:T(8,128)S(1)}, u32[]{:S(2)}, u32[]{:S(2)}) collective-permute-start(f32[2,1,128,128]{2,3,1,0:T(8,128)S(1)} %maximum_select_fusion.4), channel_id=1, source_target_pairs={{0,64},{16,80},{32,96},{48,112},{64,128},{80,144},{96,160},{112,17... | collective-permute-start | bytes 393224 | tf_op jit(solution)/shard_map/ppermute | solution.py:19
  60.6 17.5 %collective-permute-start.5 = (f32[2,1,128,128]{2,3,1,0:T(8,128)S(1)}, f32[2,1,128,128]{2,3,1,0:T(8,128)S(1)}, u32[]{:S(2)}, u32[]{:S(2)}) collective-permute-start(f32[2,1,128,128]{2,3,1,0:T(8,128)S(1)} %maximum_select_fusion.4), channel_id=1, source_target_pairs={{0,128},{16,144},{32,160},{48,176},{64,192},{80,208},{96,224},{112... | collective-permute-start | bytes 393224 | tf_op jit(solution)/shard_map/ppermute | solution.py:19
  69.1 9.8 %collective-permute-start.6 = (f32[2,1,128,128]{2,3,1,0:T(8,128)S(1)}, f32[2,1,128,128]{2,3,1,0:T(8,128)S(1)}, u32[]{:S(2)}, u32[]{:S(2)}) collective-permute-start(f32[2,1,128,128]{2,3,1,0:T(8,128)S(1)} %maximum_select_fusion.4), channel_id=1, source_target_pairs={{0,192},{16,208},{32,224},{48,240},{64,256},{80,272},{96,288},{112... | collective-permute-start | bytes 393224 | tf_op jit(solution)/shard_map/ppermute | solution.py:19
  79.3 36.0 %collective-permute-start.9 = (f32[2,1,128,128]{2,3,1,0:T(8,128)S(1)}, f32[2,1,128,128]{2,3,1,0:T(8,128)S(1)}, u32[]{:S(2)}, u32[]{:S(2)}) collective-permute-start(f32[2,1,128,128]{2,3,1,0:T(8,128)S(1)} %maximum_select_fusion.10), channel_id=1, source_target_pairs={{0,768},{16,784},{32,800},{48,816},{64,832},{80,848},{96,864},{112... | collective-permute-start | bytes 393224 | tf_op jit(solution)/shard_map/ppermute | solution.py:19
  96.6 10.2 %collective-permute-start.7 = (f32[2,1,128,128]{2,3,1,0:T(8,128)S(1)}, f32[2,1,128,128]{2,3,1,0:T(8,128)S(1)}, u32[]{:S(2)}, u32[]{:S(2)}) collective-permute-start(f32[2,1,128,128]{2,3,1,0:T(8,128)S(1)} %maximum_select_fusion.10), channel_id=1, source_target_pairs={{0,256},{16,272},{32,288},{48,304},{64,320},{80,336},{96,352},{112... | collective-permute-start | bytes 393224 | tf_op jit(solution)/shard_map/ppermute | solution.py:19
  97.9 9.8 %collective-permute-start.8 = (f32[2,1,128,128]{2,3,1,0:T(8,128)S(1)}, f32[2,1,128,128]{2,3,1,0:T(8,128)S(1)}, u32[]{:S(2)}, u32[]{:S(2)}) collective-permute-start(f32[2,1,128,128]{2,3,1,0:T(8,128)S(1)} %maximum_select_fusion.10), channel_id=1, source_target_pairs={{0,512},{16,528},{32,544},{48,560},{64,576},{80,592},{96,608},{112... | collective-permute-start | bytes 393224 | tf_op jit(solution)/shard_map/ppermute | solution.py:19
  126.1 11.0 %collective-permute-start.10 = (f32[2,1,128,128]{2,3,1,0:T(8,128)S(1)}, f32[2,1,128,128]{2,3,1,0:T(8,128)S(1)}, u32[]{:S(2)}, u32[]{:S(2)}) collective-permute-start(f32[2,1,128,128]{2,3,1,0:T(8,128)S(1)} %pad_maximum_fusion.1), channel_id=1, source_target_pairs={{16,0},{32,16},{48,32},{64,48},{80,64},{96,80},{112,96},{128,112},... | collective-permute-start | bytes 393224 | tf_op jit(solution)/shard_map/ppermute | solution.py:19
  128.0 10.6 %collective-permute-start.11 = (f32[2,1,128,128]{2,3,1,0:T(8,128)S(1)}, f32[2,1,128,128]{2,3,1,0:T(8,128)S(1)}, u32[]{:S(2)}, u32[]{:S(2)}) collective-permute-start(f32[2,1,128,128]{2,3,1,0:T(8,128)S(1)} %pad_maximum_fusion.1), channel_id=1, source_target_pairs={{32,0},{48,16},{64,32},{80,48},{96,64},{112,80},{128,96},{144,112}... | collective-permute-start | bytes 393224 | tf_op jit(solution)/shard_map/ppermute | solution.py:19
  130.0 9.9 %collective-permute-start.12 = (f32[2,1,128,128]{2,3,1,0:T(8,128)S(1)}, f32[2,1,128,128]{2,3,1,0:T(8,128)S(1)}, u32[]{:S(2)}, u32[]{:S(2)}) collective-permute-start(f32[2,1,128,128]{2,3,1,0:T(8,128)S(1)} %pad_maximum_fusion.1), channel_id=1, source_target_pairs={{48,0},{64,16},{80,32},{96,48},{112,64},{128,80},{144,96},{160,112... | collective-permute-start | bytes 393224 | tf_op jit(solution)/shard_map/ppermute | solution.py:19
  140.4 7.5 %collective-permute-start.13 = (f32[2,1,128,128]{2,3,1,0:T(8,128)S(1)}, f32[2,1,128,128]{2,3,1,0:T(8,128)S(1)}, u32[]{:S(2)}, u32[]{:S(2)}) collective-permute-start(f32[2,1,128,128]{2,3,1,0:T(8,128)S(1)} %maximum_select_fusion.17), channel_id=1, source_target_pairs={{64,0},{80,16},{96,32},{112,48},{128,64},{144,80},{160,96},{176,11... | collective-permute-start | bytes 393224 | tf_op jit(solution)/shard_map/ppermute | solution.py:19
  141.7 12.3 %collective-permute-start.14 = (f32[2,1,128,128]{2,3,1,0:T(8,128)S(1)}, f32[2,1,128,128]{2,3,1,0:T(8,128)S(1)}, u32[]{:S(2)}, u32[]{:S(2)}) collective-permute-start(f32[2,1,128,128]{2,3,1,0:T(8,128)S(1)} %maximum_select_fusion.17), channel_id=1, source_target_pairs={{128,0},{144,16},{160,32},{176,48},{192,64},{208,80},{224,96},{240... | collective-permute-start | bytes 393224 | tf_op jit(solution)/shard_map/ppermute | solution.py:19
  143.0 17.6 %collective-permute-start.15 = (f32[2,1,128,128]{2,3,1,0:T(8,128)S(1)}, f32[2,1,128,128]{2,3,1,0:T(8,128)S(1)}, u32[]{:S(2)}, u32[]{:S(2)}) collective-permute-start(f32[2,1,128,128]{2,3,1,0:T(8,128)S(1)} %maximum_select_fusion.17), channel_id=1, source_target_pairs={{192,0},{208,16},{224,32},{240,48},{256,64},{272,80},{288,96},{304... | collective-permute-start | bytes 393224 | tf_op jit(solution)/shard_map/ppermute | solution.py:19
  161.0 18.9 %collective-permute-start.18 = (f32[2,1,128,128]{2,3,1,0:T(8,128)S(1)}, f32[2,1,128,128]{2,3,1,0:T(8,128)S(1)}, u32[]{:S(2)}, u32[]{:S(2)}) collective-permute-start(f32[2,1,128,128]{2,3,1,0:T(8,128)S(1)} %maximum_select_fusion.23), channel_id=1, source_target_pairs={{768,0},{784,16},{800,32},{816,48},{832,64},{848,80},{864,96},{880... | collective-permute-start | bytes 393224 | tf_op jit(solution)/shard_map/ppermute | solution.py:19
  162.3 11.5 %collective-permute-start.16 = (f32[2,1,128,128]{2,3,1,0:T(8,128)S(1)}, f32[2,1,128,128]{2,3,1,0:T(8,128)S(1)}, u32[]{:S(2)}, u32[]{:S(2)}) collective-permute-start(f32[2,1,128,128]{2,3,1,0:T(8,128)S(1)} %maximum_select_fusion.23), channel_id=1, source_target_pairs={{256,0},{272,16},{288,32},{304,48},{320,64},{336,80},{352,96},{368... | collective-permute-start | bytes 393224 | tf_op jit(solution)/shard_map/ppermute | solution.py:19
  163.6 15.8 %collective-permute-start.17 = (f32[2,1,128,128]{2,3,1,0:T(8,128)S(1)}, f32[2,1,128,128]{2,3,1,0:T(8,128)S(1)}, u32[]{:S(2)}, u32[]{:S(2)}) collective-permute-start(f32[2,1,128,128]{2,3,1,0:T(8,128)S(1)} %maximum_select_fusion.23), channel_id=1, source_target_pairs={{512,0},{528,16},{544,32},{560,48},{576,64},{592,80},{608,96},{624... | collective-permute-start | bytes 393224 | tf_op jit(solution)/shard_map/ppermute | solution.py:19
  187.5 15.6 %collective-permute-start.19 = (f32[3,1,3,128]{3,2,1,0:T(4,128)S(1)}, f32[3,1,3,128]{3,2,1,0:T(4,128)S(1)}, u32[]{:S(2)}, u32[]{:S(2)}) collective-permute-start(f32[3,1,3,128]{3,2,1,0:T(4,128)S(1)} %pad_maximum_fusion.10), channel_id=1, source_target_pairs={{16,0},{32,16},{48,32},{64,48},{80,64},{96,80},{112,96},{128,112},... | collective-permute-start | bytes 13832 | tf_op jit(solution)/shard_map/ppermute | solution.py:19
  190.4 14.7 %collective-permute-start.20 = (f32[3,4,128]{2,1,0:T(4,128)S(1)}, f32[3,4,128]{2,1,0:T(4,128)S(1)}, u32[]{:S(2)}, u32[]{:S(2)}) collective-permute-start(f32[3,4,128]{2,1,0:T(4,128)S(1)} %get-tuple-element.61), channel_id=1, source_target_pairs={{16,0},{0,16},{48,32},{32,48},{80,64},{64,80},{112,96},{96,112},{1... | collective-permute-start | bytes 18440 | tf_op jit(solution)/shard_map/ppermute | solution.py:63
  205.7 7.0 %collective-permute-start.21 = (f32[3,4,128]{2,1,0:T(4,128)S(1)}, f32[3,4,128]{2,1,0:T(4,128)S(1)}, u32[]{:S(2)}, u32[]{:S(2)}) collective-permute-start(f32[3,4,128]{2,1,0:T(4,128)S(1)} %fusion.241), channel_id=1, source_target_pairs={{32,0},{48,16},{0,32},{16,48},{96,64},{112,80},{64,96},{80,112},{1... | collective-permute-start | bytes 18440 | tf_op jit(solution)/shard_map/ppermute | solution.py:63
  213.3 10.2 %collective-permute-start.22 = (f32[3,4,128]{2,1,0:T(4,128)S(1)}, f32[3,4,128]{2,1,0:T(4,128)S(1)}, u32[]{:S(2)}, u32[]{:S(2)}) collective-permute-start(f32[3,4,128]{2,1,0:T(4,128)S(1)} %fusion.240), channel_id=1, source_target_pairs={{64,0},{80,16},{96,32},{112,48},{0,64},{16,80},{32,96},{48,112},{1... | collective-permute-start | bytes 18440 | tf_op jit(solution)/shard_map/ppermute | solution.py:63
  224.1 6.4 %collective-permute-start.23 = (f32[3,4,128]{2,1,0:T(4,128)S(1)}, f32[3,4,128]{2,1,0:T(4,128)S(1)}, u32[]{:S(2)}, u32[]{:S(2)}) collective-permute-start(f32[3,4,128]{2,1,0:T(4,128)S(1)} %fusion.239), channel_id=1, source_target_pairs={{128,0},{144,16},{160,32},{176,48},{192,64},{208,80},{224,96},{240... | collective-permute-start | bytes 18440 | tf_op jit(solution)/shard_map/ppermute | solution.py:63
  231.1 9.4 %collective-permute-start.24 = (f32[3,4,128]{2,1,0:T(4,128)S(1)}, f32[3,4,128]{2,1,0:T(4,128)S(1)}, u32[]{:S(2)}, u32[]{:S(2)}) collective-permute-start(f32[3,4,128]{2,1,0:T(4,128)S(1)} %fusion.238), channel_id=1, source_target_pairs={{256,0},{272,16},{288,32},{304,48},{320,64},{336,80},{352,96},{368... | collective-permute-start | bytes 18440 | tf_op jit(solution)/shard_map/ppermute | solution.py:63
  241.1 14.2 %collective-permute-start.25 = (f32[3,4,128]{2,1,0:T(4,128)S(1)}, f32[3,4,128]{2,1,0:T(4,128)S(1)}, u32[]{:S(2)}, u32[]{:S(2)}) collective-permute-start(f32[3,4,128]{2,1,0:T(4,128)S(1)} %fusion.237), channel_id=1, source_target_pairs={{512,0},{528,16},{544,32},{560,48},{576,64},{592,80},{608,96},{624... | collective-permute-start | bytes 18440 | tf_op jit(solution)/shard_map/ppermute | solution.py:63
Sparse Core Ops, SparseCore 0:
  13.0 52.0 all-gather.1
